TPU v7x, 512 devices: a whole 4x4x16 slice. The times are simulated.
512 devices in a mesh: param: 32 (over y_lo, z), row: 4 (over x), col: 4 (over y_hi, core).
Axes of the slice: x: 4, y: 4 (y_hi: 2, y_lo: 2; y = y_hi * 2 + y_lo), z: 16, core: 2. Of those that a mesh axis runs over, the one named last changes fastest.
Arguments:
- coefficients: bfloat16 [3, 2, 32, 512], P(None, None, 'row', 'col'), may hold values from -6 to 6
- noise_sigma: float32 [2, 32, 512], P(None, 'row', 'col'), may hold values from 0.5 to 4
- residual: float32 [2, 32, 512], P(None, 'row', 'col'), may hold values from -0.6 to 0.6
- crack_mask: int32 [32, 4], P('row', 'col'), may hold values 0 or 1
- node_panel: bfloat16 [4, 64, 3, 2048], P('row', 'col', None, 'param'), may hold values from -0.41992188 to 0.41992188
Outputs:
- hessian: float32 [2048, 2048], P('param', ('row', 'col'))
- gradient: float32 [2048], P(('param', 'row', 'col'))
All inputs are finite; a program needn't handle non-finite values. No bound on the sum of `crack_mask` on one device may be relied on, other than what follows from the above.
Results may differ from a plain program's by a relative error of at most 0.0055.
Values may be sent and summed in bfloat16 or wider, within the bound.
No kernel may reach another device: no remote copies, remote signals or barrier semaphores. Data moves between devices by JAX's collectives and lax.ppermute only.
A program may use at most 64 MiB of HBM per device.

v0:
```python
import jax
import jax.numpy as jnp
from jax import lax
from jax.sharding import PartitionSpec as P

EL = 8
CAMS = 2


def shifted(block, axis, distance):
    devices = range(lax.axis_size(axis))
    route = [(i - distance, i) for i in devices if i - distance in devices]
    return lax.ppermute(block, axis, route)


def corner_shapes(rows, cols):
    vertical = ((jnp.arange(rows) % EL).astype(jnp.float32) + 0.5) / EL
    horizontal = ((jnp.arange(cols) % EL).astype(jnp.float32) + 0.5) / EL
    lower = vertical[:, None]
    right = horizontal[None, :]
    return jnp.stack(
        [(1.0 - lower) * (1.0 - right), (1.0 - lower) * right, lower * (1.0 - right), lower * right]
    )


def pixel_rows(design, extended):
    corners = jnp.stack(
        [extended[:-1, :-1], extended[:-1, 1:], extended[1:, :-1], extended[1:, 1:]], axis=2
    )
    width = extended.shape[3]
    corners = corners.reshape(design.shape[1], 12, width)
    sensitivity = jnp.einsum("kep,ekq->epq", design, corners, preferred_element_type=jnp.float32)
    return sensitivity.astype(jnp.bfloat16).reshape(design.shape[1] * design.shape[2], width)


def block_product(own_rows, other_rows):
    return lax.dot_general(
        own_rows, other_rows, (((0,), (0,)), ((), ())), preferred_element_type=jnp.float32
    )


def on_device(coefficients, noise_sigma, residual, crack_mask, node_panel):
    rows = noise_sigma.shape[1]
    cols = noise_sigma.shape[2]
    elem_rows = rows // EL
    elem_cols = cols // EL
    shapes = corner_shapes(rows, cols)
    live_rows = jnp.repeat(crack_mask.astype(jnp.float32), 128, axis=1)
    pixel_scale = live_rows[None] / noise_sigma
    design = (
        shapes[:, None, None] * pixel_scale[None, None] * coefficients.astype(jnp.float32)[None]
    ).astype(jnp.bfloat16)
    design = design.reshape(4, 3, CAMS, elem_rows, EL, elem_cols, EL).transpose(0, 1, 3, 5, 2, 4, 6)
    design = design.reshape(12, elem_rows * elem_cols, CAMS * EL * EL)
    weighted = (pixel_scale * residual).astype(jnp.bfloat16)
    weighted = (
        weighted.reshape(CAMS, elem_rows, EL, elem_cols, EL).transpose(1, 3, 0, 2, 4).reshape(-1)
    )
    right_edge = shifted(node_panel[:, :1], "col", -1)
    widened = jnp.concatenate([node_panel, right_edge], axis=1)
    lower_edge = shifted(widened, "row", -1)
    extended = jnp.concatenate([widened, lower_edge], axis=0)
    own_rows = pixel_rows(design, extended)
    grad_part = jnp.dot(weighted, own_rows, preferred_element_type=jnp.float32)
    block = block_product(
        own_rows, pixel_rows(design, lax.all_gather(extended, "param", axis=3, tiled=True))
    )
    hessian, gradient = (
        lax.psum_scatter(block, ("row", "col"), scatter_dimension=1, tiled=True),
        lax.psum_scatter(grad_part, ("row", "col"), scatter_dimension=0, tiled=True),
    )
    return (hessian, gradient)


def solution(mesh):
    in_specs = (
        P(None, None, "row", "col"),
        P(None, "row", "col"),
        P(None, "row", "col"),
        P("row", "col"),
        P("row", "col", None, "param"),
    )
    out_specs = (P("param", ("row", "col")), P(("param", "row", "col")))
    return jax.shard_map(
        on_device, mesh=mesh, in_specs=in_specs, out_specs=out_specs, check_vma=False
    )
```

profile of v0, /device:TPU:1, one launch (start us, length us, event | category | flops | bytes accessed | tf_op | source)
XLA Modules:
  0.0 246.4 jit_solution(17997718687711013562)
XLA Ops:
  7.2 0.0 reduce-scatter.2.cloned.1.call-start
  7.2 0.7 slice.24
  7.9 8.7 %collective-permute-start = (bf16[1,1,3,64]{3,1,2,0:T(2,128)(2,1)S(1)}, bf16[1,1,3,64]{3,1,2,0:T(2,128)(2,1)S(1)}, u32[]{:S(2)}, u32[]{:S(2)}) collective-permute-start(bf16[1,1,3,64]{3,1,2,0:T(2,128)(2,1)S(1)} %slice.24), channel_id=1, source_target_pairs={{1,0},{2,1},{3,2},{5,4},{6,5},{7,6},{9,8},{10,9},{11,10},{13,12},{... | collective-permute-start | bytes 1160 | tf_op jit(solution)/shard_map/ppermute | solution.py:13
  16.7 0.7 convert_bitcast_fusion
  17.3 0.8 multiply_convert_fusion.1
  18.1 0.1 mul.140
  18.2 0.1 copy.28
  18.3 0.9 reshape.255
  19.3 0.1 copy.29
  19.4 0.1 broadcast_multiply_fusion.3
  19.6 0.1 multiply_convert_fusion
  19.7 0.7 constant_dynamic-update-slice_fusion.1
  20.4 0.8 copy.30
  21.2 0.0 collective-permute-done
  21.2 1.3 collective-permute-start.1
  22.5 0.6 slice_bitcast_fusion.2
  23.1 2.8 %collective-permute-done.1 = bf16[1,17,3,64]{3,1,2,0:T(8,128)(2,1)S(1)} collective-permute-done((bf16[1,17,3,64]{3,1,2,0:T(8,128)(2,1)S(1)}, bf16[1,17,3,64]{3,1,2,0:T(8,128)(2,1)S(1)}, u32[]{:S(2)}, u32[]{:S(2)}) %collective-permute-start.1) | collective-permute-done | bytes 6560 | tf_op jit(solution)/shard_map/ppermute | solution.py:13
  25.9 0.0 copy-start
  25.9 0.6 copy-done
  26.5 0.1 copy.32
  26.7 70.7 %all_gather.3 = bf16[2,17,3,2048]{1,0,2,3:T(2,128)(2,1)S(1)} all-gather(bf16[2,17,3,64]{1,0,2,3:T(2,128)(2,1)S(1)} %copy.32), channel_id=1, replica_groups=mesh['param'=32,'row'=4,'col'=4] {'param'}, dimensions={3}, use_global_device_ids=true | all-gather | bytes 430848 | tf_op jit(solution)/shard_map/all_gather | solution.py:66
  97.4 13.9 %fusion.21 = (bf16[1,16,3,2048]{1,0,2,3:T(2,128)(2,1)}, bf16[1,16,3,2048]{1,0,2,3:T(2,128)(2,1)}, bf16[1,16,3,2048]{1,0,2,3:T(2,128)(2,1)}, bf16[1,16,3,2048]{1,0,2,3:T(2,128)(2,1)S(1)}) fusion(bf16[2,17,3,2048]{1,0,2,3:T(2,128)(2,1)S(1)} %all_gather.3), kind=kLoop, calls=%fused_computation.42 | loop fusion | bytes 1572864 | tf_op jit(solution)/shard_map/slice | solution.py:28
  111.3 6.5 %copy.41 = bf16[1,16,3,2048]{3,1,2,0:T(8,128)(2,1)S(1)} copy(bf16[1,16,3,2048]{1,0,2,3:T(2,128)(2,1)} %get-tuple-element.4) | data formatting | bytes 393216
  117.7 6.5 %copy.43 = bf16[1,16,3,2048]{3,1,2,0:T(8,128)(2,1)S(1)} copy(bf16[1,16,3,2048]{1,0,2,3:T(2,128)(2,1)} %get-tuple-element.5) | data formatting | bytes 393216
  124.2 0.0 copy-start.1
  124.2 7.8 %copy.42 = bf16[1,16,3,2048]{3,1,2,0:T(8,128)(2,1)} copy(bf16[1,16,3,2048]{1,0,2,3:T(2,128)(2,1)} %get-tuple-element.6) | data formatting | bytes 393216
  132.0 5.6 %copy.44 = bf16[1,16,3,2048]{3,1,2,0:T(8,128)(2,1)} copy(bf16[1,16,3,2048]{1,0,2,3:T(2,128)(2,1)S(1)} %get-tuple-element.7) | data formatting | bytes 393216
  137.6 0.8 slice_bitcast_fusion.1
  138.4 0.0 copy-done.1
  138.4 0.7 pad_maximum_fusion.2
  139.1 1.1 convolution_convert_fusion
  140.2 1.1 pad_maximum_fusion
  141.4 5.4 %fusion.4 = f32[64,2048]{1,0:T(8,128)} fusion(bf16[16,128,64]{1,2,0:T(8,128)(2,1)S(1)} %convolution_convert_fusion, bf16[12,16,128]{2,0,1:T(8,128)(2,1)} %copy.30, bf16[16,12,2048]{2,0,1:T(8,128)(2,1)S(1)} %bitcast.44), kind=kOutput, calls=%fused_computation.3 | convolution fusion | flops 641728512 | bytes 1622016 | tf_op jit(solution)/shard_map/dot_general | solution.py:37
  146.8 0.0 reduce-scatter.2.cloned.1.call-update
  146.8 0.1 reshape.252
  147.0 0.1 reshape.257
  147.1 1.3 dynamic-slice
  149.0 0.2 convolution_bitcast_fusion
  149.2 46.2 %all-reduce = f32[64]{0:T(128)S(1)} all-reduce(f32[64]{0:T(128)S(1)} %convolution_bitcast_fusion), channel_id=3, replica_groups=mesh['param'=32,'row'=4,'col'=4] {'row','col'}, use_global_device_ids=true, to_apply=%region_1.2.clone | all-reduce | flops 64 | bytes 512
  195.4 0.6 dynamic-slice.1
  196.0 43.6 %reduce-scatter.2.cloned.1.call-done = f32[64,128]{1,0:T(8,128)} async-done(((f32[64,2048]{1,0:T(8,128)}), f32[64,128]{1,0:T(8,128)}) %reduce-scatter.2.cloned.1.call-update) | async-done | bytes 32784 | tf_op jit(solution)/shard_map/reduce_scatter | solution.py:69
  (7 shorter events, 0.1 us)
Async XLA Ops:
  7.2 232.4 %reduce-scatter.2.cloned.1.call-start = ((), (), s32[]{:S(2)}) async-start(), calls=%async_computation.1 | async-start | bytes 557056 | tf_op jit(solution)/shard_map/reduce_scatter | solution.py:69
  7.9 13.3 %collective-permute-start = (bf16[1,1,3,64]{3,1,2,0:T(2,128)(2,1)S(1)}, bf16[1,1,3,64]{3,1,2,0:T(2,128)(2,1)S(1)}, u32[]{:S(2)}, u32[]{:S(2)}) collective-permute-start(bf16[1,1,3,64]{3,1,2,0:T(2,128)(2,1)S(1)} %slice.24), channel_id=1, source_target_pairs={{1,0},{2,1},{3,2},{5,4},{6,5},{7,6},{9,8},{10,9},{11,10},{13,12},{... | collective-permute-start | bytes 1160 | tf_op jit(solution)/shard_map/ppermute | solution.py:13
  21.2 4.7 %collective-permute-start.1 = (bf16[1,17,3,64]{3,1,2,0:T(8,128)(2,1)S(1)}, bf16[1,17,3,64]{3,1,2,0:T(8,128)(2,1)S(1)}, u32[]{:S(2)}, u32[]{:S(2)}) collective-permute-start(bf16[1,17,3,64]{3,1,2,0:T(8,128)(2,1)S(1)} %constant_dynamic-update-slice_fusion), channel_id=1, source_target_pairs={{4,0},{8,4},{12,8},{5,1},{9,5},{13,9},{6,2},{10,6},{14,10},{7,3},{... | collective-permute-start | bytes 19592 | tf_op jit(solution)/shard_map/ppermute | solution.py:13
  25.9 0.6 copy-start
  124.2 14.2 %copy-start.1 = (bf16[1,16,3,64]{3,1,2,0:T(8,128)(2,1)S(1)}, bf16[1,16,3,64]{3,1,2,0:T(8,128)(2,1)}, u32[]{:S(2)}) copy-start(bf16[1,16,3,64]{3,1,2,0:T(8,128)(2,1)} %param.9) | copy-start | bytes 18436
Sparse Core Ops, SparseCore 0:
  146.9 92.6 reduce-scatter.1
where the time goes:
time: 248 us; the launch traced here: 246 us
  blocking collectives  117 us (47%)
  local copies, waits for them, and re-layouts  48 us (19%)
  waiting for transfers between devices  46.4 us (19%)
  between operations  14.8 us (6%)
  starting transfers between devices  10.1 us (4%)
  matrix products  6.69 us (3%)
  other arithmetic  3.54 us (1%)
    all_gather x1, blocking collectives, on_device(): lax.all_gather(extended, 'param', axis=3, tiled=True)  70.7 us
    unnamed x1, blocking collectives  46.2 us
    reduce_scatter x1, waiting for transfers between devices, on_device(): lax.psum_scatter(block, ('row', 'col'), scatter_dimension=1, tiled=True)  43.6 us
    unnamed x11, local copies, waits for them, and re-layouts  29.5 us
    slice x1, local copies, waits for them, and re-layouts, pixel_rows(): extended[:-1, :-1]  13.9 us
    ppermute x2, starting transfers between devices, shifted(): return lax.ppermute(block, axis, route)  10 us
    dot_general x1, matrix products, block_product(): lax.dot_general(own_rows, other_rows, (((0,), (0,)), ((), ())), preferred...  5.42 us
  transfers between devices with their start and end apart: 3, of which 2 were waited for; matrix products, arithmetic and copies ran while one was open for 3% of the time, Pallas kernels for 0%

commit v1 on v0

v1 whole, which is shorter than its diff:
```python
import jax
import jax.numpy as jnp
from jax import lax
from jax.sharding import PartitionSpec as P

EL = 8
CAMS = 2
LANES = 128
HIGHEST = lax.Precision.HIGHEST

PARAM_ORDER = (8, 4, 2, 1, 16)
TILE_ORDER = (8, 2, 4, 1)


def corner_shapes(rows, cols):
    vertical = ((jnp.arange(rows) % EL).astype(jnp.float32) + 0.5) / EL
    horizontal = ((jnp.arange(cols) % EL).astype(jnp.float32) + 0.5) / EL
    lower = vertical[:, None]
    right = horizontal[None, :]
    return jnp.stack(
        [(1.0 - lower) * (1.0 - right), (1.0 - lower) * right, lower * (1.0 - right), lower * right]
    )


def doubling_gather(piece, axes, order):
    size = 1
    for bit in order:
        size *= 2
    me = lax.axis_index(axes)
    data = piece[None]
    for bit in order:
        theirs = lax.ppermute(data, axes, [(i, i ^ bit) for i in range(size)])
        data = jnp.concatenate([data, theirs], axis=0)
    wanted = me ^ jnp.arange(size, dtype=jnp.int32)
    position = jnp.zeros((size,), jnp.int32)
    for step, bit in enumerate(order):
        position = position | (((wanted // bit) % 2) << step)
    return jnp.take(data, position, axis=0)


def as_lanes(flat, dtype):
    rows = -(-flat.shape[0] // (8 * LANES)) * 8
    flat = jnp.pad(flat.astype(dtype), (0, rows * LANES - flat.shape[0]))
    return flat.reshape(rows, LANES)


def element_corners(nodes):
    extended = jnp.pad(nodes, ((0, 1), (0, 1), (0, 0), (0, 0)))
    corners = jnp.stack(
        [extended[:-1, :-1], extended[:-1, 1:], extended[1:, :-1], extended[1:, 1:]], axis=2
    )
    return corners.reshape(nodes.shape[0] * nodes.shape[1], 12, nodes.shape[3])


def on_device(coefficients, noise_sigma, residual, crack_mask, node_panel):
    n_param = lax.axis_size("param")
    n_row = lax.axis_size("row")
    n_col = lax.axis_size("col")
    tiles = n_row * n_col
    per_block = n_param // tiles
    rows = noise_sigma.shape[1]
    cols = noise_sigma.shape[2]
    elem_rows = rows // EL
    elem_cols = cols // EL
    node_rows, node_cols, comps, width = node_panel.shape
    elements = elem_rows * elem_cols

    shapes = corner_shapes(rows, cols)
    live_rows = jnp.repeat(crack_mask.astype(jnp.float32), 128, axis=1)
    pixel_scale = live_rows[None] / noise_sigma
    design = (
        shapes[:, None, None] * pixel_scale[None, None] * coefficients.astype(jnp.float32)[None]
    ).astype(jnp.bfloat16)
    design = design.reshape(4, 3, CAMS, elem_rows, EL, elem_cols, EL).transpose(3, 5, 0, 1, 2, 4, 6)
    design = design.reshape(elements, 12, CAMS * EL * EL)
    weighted = (pixel_scale * residual).astype(jnp.bfloat16)
    weighted = weighted.reshape(CAMS, elem_rows, EL, elem_cols, EL).transpose(1, 3, 0, 2, 4)
    weighted = weighted.reshape(elements, CAMS * EL * EL)
    gram = jnp.einsum("eip,ejp->eij", design, design, preferred_element_type=jnp.float32)
    proj = jnp.einsum("eip,ep->ei", design, weighted, preferred_element_type=jnp.float32)

    payload = jnp.concatenate([node_panel.reshape(-1).astype(jnp.float32), gram.reshape(-1), proj.reshape(-1)])
    own = doubling_gather(as_lanes(payload, jnp.float32), ("row", "col"), TILE_ORDER)
    own = own.reshape(tiles, -1)
    n_nodes = node_rows * node_cols * comps * width
    n_gram = elements * 144
    own_nodes = own[:, :n_nodes].reshape(n_row, n_col, node_rows, node_cols, comps, width)
    own_nodes = own_nodes.transpose(0, 2, 1, 3, 4, 5).reshape(n_row * node_rows, n_col * node_cols, comps, width)
    grams = own[:, n_nodes : n_nodes + n_gram].reshape(n_row, n_col, elem_rows, elem_cols, 12, 12)
    grams = grams.transpose(0, 2, 1, 3, 4, 5).reshape(-1, 12, 12)
    projs = own[:, n_nodes + n_gram : n_nodes + n_gram + elements * 12]
    projs = projs.reshape(n_row, n_col, elem_rows, elem_cols, 12).transpose(0, 2, 1, 3, 4).reshape(-1, 12)

    route = []
    for b in range(n_param):
        for t in range(tiles):
            route.append((b * tiles + t, (per_block * t + b % per_block) * tiles + b // per_block))
    moved = lax.ppermute(as_lanes(node_panel.reshape(-1), jnp.bfloat16), ("param", "row", "col"), route)
    cross = doubling_gather(moved, "param", PARAM_ORDER).reshape(n_param, -1)[:, : node_rows * node_cols * comps * width]
    cross = cross.reshape(n_row, n_col, per_block, node_rows, node_cols, comps, width)
    cross = cross.transpose(0, 3, 1, 4, 5, 2, 6)
    cross = cross.reshape(n_row * node_rows, n_col * node_cols, comps, per_block * width)

    rows_of = element_corners(own_nodes.astype(jnp.bfloat16)).astype(jnp.float32)
    cols_of = element_corners(cross).astype(jnp.float32)
    weighted_cols = grams[:, :, 0, None] * cols_of[:, None, 0, :]
    for j in range(1, 12):
        weighted_cols = weighted_cols + grams[:, :, j, None] * cols_of[:, None, j, :]
    hessian = jnp.einsum("eip,eiq->pq", rows_of, weighted_cols, precision=HIGHEST)
    gradient = jnp.einsum("eip,ei->p", rows_of, projs, precision=HIGHEST)
    share = width // tiles
    gradient = lax.dynamic_slice(gradient, (lax.axis_index(("row", "col")) * share,), (share,))
    return (hessian, gradient)


def solution(mesh):
    in_specs = (
        P(None, None, "row", "col"),
        P(None, "row", "col"),
        P(None, "row", "col"),
        P("row", "col"),
        P("row", "col", None, "param"),
    )
    out_specs = (P("param", ("row", "col")), P(("param", "row", "col")))
    return jax.shard_map(
        on_device, mesh=mesh, in_specs=in_specs, out_specs=out_specs, check_vma=False
    )
```

time: 248 us -> 127 us (0.51)
  blocking collectives: 117 us -> 0 us
  starting transfers between devices: 10.1 us -> 64.5 us
  waiting for transfers between devices: 46.4 us -> 3.56 us
  between operations: 14.8 us -> 1.4 us
    all_gather x1 -> x0, blocking collectives: 70.7 us -> none  [on_device(): lax.all_gather(extended, 'param', axis=3, tiled=True)]
    ppermute x2 -> x10, starting transfers between devices: 10 us -> 64.5 us  [the longest x9 58.7 us: doubling_gather(): theirs = lax.ppermute(data, axes, [(i, i ^ bit) for i in range(size)])]
    unnamed x1 -> x0, blocking collectives: 46.2 us -> none
    reduce_scatter x1 -> x0, waiting for transfers between devices: 43.6 us -> none  [on_device(): lax.psum_scatter(block, ('row', 'col'), scatter_dimension=1, tiled=True)]
    unnamed x11 -> x50, local copies, waits for them, and re-layouts: 29.5 us -> 0.16 us
    slice x2 -> x17, local copies, waits for them, and re-layouts: 14.6 us -> 36.2 us  [the longest x11 21.9 us: on_device(): grams[:, :, j, None] * cols_of[:, None, j, :]]
    dot_general x3 -> x4, matrix products: 6.69 us -> 6.63 us  [the longest x1 5.9 us: on_device(): jnp.einsum('eip,eiq->pq', rows_of, weighted_cols, precision=HIGHEST)]
  transfers between devices with their start and end apart: 3 -> 10, of which waited for: 2 -> 3; matrix products, arithmetic and copies ran while one was open for 3% -> 3% of each run, Pallas kernels for 0% -> 0%
where the time goes in v1:
time: 127 us; the launch traced here: 126 us
  starting transfers between devices  64.5 us (51%)
  local copies, waits for them, and re-layouts  46 us (36%)
  matrix products  6.63 us (5%)
  other arithmetic  3.79 us (3%)
  waiting for transfers between devices  3.56 us (3%)
  between operations  1.4 us (1%)
    ppermute x9, starting transfers between devices, doubling_gather(): theirs = lax.ppermute(data, axes, [(i, i ^ bit) for i in range(size)])  58.7 us
    slice x11, local copies, waits for them, and re-layouts, on_device(): grams[:, :, j, None] * cols_of[:, None, j, :]  21.9 us
    slice x2, local copies, waits for them, and re-layouts, on_device(): weighted_cols = grams[:, :, 0, None] * cols_of[:, None, 0, :]  14.2 us
    dot_general x1, matrix products, on_device(): jnp.einsum('eip,eiq->pq', rows_of, weighted_cols, precision=HIGHEST)  5.9 us
    ppermute x1, starting transfers between devices, on_device(): lax.ppermute(as_lanes(node_panel.reshape(-1), jnp.bfloat16), ('param', 'r...  5.73 us
  transfers between devices with their start and end apart: 10, of which 3 were waited for; matrix products, arithmetic and copies ran while one was open for 3% of the time, Pallas kernels for 0%

profile of v1, /device:TPU:1, one launch (start us, length us, event | category | flops | bytes accessed | tf_op | source)
XLA Modules:
  0.0 125.8 jit_solution(8786268677498659305)
XLA Ops:
  0.7 0.7 convert_bitcast_fusion
  1.3 0.8 multiply_convert_fusion.1
  2.3 0.9 reshape.897
  3.6 0.2 copy.54
  4.8 5.5 %collective-permute-start = (f32[1,48,128]{2,1,0:T(8,128)S(1)}, f32[1,48,128]{2,1,0:T(8,128)S(1)}, u32[]{:S(2)}, u32[]{:S(2)}) collective-permute-start(f32[1,48,128]{2,1,0:T(8,128)S(1)} %get-tuple-element.3), channel_id=1, source_target_pairs={{0,8},{1,9},{2,10},{3,11},{4,12},{5,13},{6,14},{7,15},{8,0},{9,1},... | collective-permute-start | bytes 73736 | tf_op jit(solution)/shard_map/ppermute | solution.py:32
  10.4 5.7 %collective-permute-start.4 = (bf16[24,128]{1,0:T(8,128)(2,1)S(1)}, bf16[24,128]{1,0:T(8,128)(2,1)S(1)}, u32[]{:S(2)}, u32[]{:S(2)}) collective-permute-start(bf16[24,128]{1,0:T(8,128)(2,1)S(1)} %reshape.894), channel_id=1, source_target_pairs={{0,0},{1,32},{2,64},{3,96},{4,128},{5,160},{6,192},{7,224},{8,256}... | collective-permute-start | bytes 18440 | tf_op jit(solution)/shard_map/ppermute | solution.py:98
  16.3 1.1 collective-permute-done.4
  17.4 21.1 %collective-permute-start.5 = (bf16[1,24,128]{2,1,0:T(8,128)(2,1)S(1)}, bf16[1,24,128]{2,1,0:T(8,128)(2,1)S(1)}, u32[]{:S(2)}, u32[]{:S(2)}) collective-permute-start(bf16[1,24,128]{2,1,0:T(8,128)(2,1)S(1)} %bitcast.99), channel_id=1, source_target_pairs={{0,128},{16,144},{32,160},{48,176},{64,192},{80,208},{96,224},{112... | collective-permute-start | bytes 18440 | tf_op jit(solution)/shard_map/ppermute | solution.py:32
  38.6 1.0 collective-permute-done.5
  39.6 5.2 %collective-permute-start.6 = (bf16[2,24,128]{2,1,0:T(8,128)(2,1)S(1)}, bf16[2,24,128]{2,1,0:T(8,128)(2,1)S(1)}, u32[]{:S(2)}, u32[]{:S(2)}) collective-permute-start(bf16[2,24,128]{2,1,0:T(8,128)(2,1)S(1)} %pad_maximum_fusion.7), channel_id=1, source_target_pairs={{0,64},{16,80},{32,96},{48,112},{64,0},{80,16},{96,32},{112,48},{1... | collective-permute-start | bytes 36872 | tf_op jit(solution)/shard_map/ppermute | solution.py:32
  44.8 3.6 %collective-permute-start.1 = (f32[2,48,128]{2,1,0:T(8,128)S(1)}, f32[2,48,128]{2,1,0:T(8,128)S(1)}, u32[]{:S(2)}, u32[]{:S(2)}) collective-permute-start(f32[2,48,128]{2,1,0:T(8,128)S(1)} %pad_maximum_fusion.4), channel_id=1, source_target_pairs={{0,2},{1,3},{2,0},{3,1},{4,6},{5,7},{6,4},{7,5},{8,10},{9,11},{10,... | collective-permute-start | bytes 147464 | tf_op jit(solution)/shard_map/ppermute | solution.py:32
  48.5 4.5 %collective-permute-start.7 = (bf16[4,24,128]{2,1,0:T(8,128)(2,1)S(1)}, bf16[4,24,128]{2,1,0:T(8,128)(2,1)S(1)}, u32[]{:S(2)}, u32[]{:S(2)}) collective-permute-start(bf16[4,24,128]{2,1,0:T(8,128)(2,1)S(1)} %pad_maximum_fusion.6), channel_id=1, source_target_pairs={{0,32},{16,48},{32,0},{48,16},{64,96},{80,112},{96,64},{112,80},{1... | collective-permute-start | bytes 73736 | tf_op jit(solution)/shard_map/ppermute | solution.py:32
  53.0 1.5 %collective-permute-done.7 = bf16[4,24,128]{2,1,0:T(8,128)(2,1)S(1)} collective-permute-done((bf16[4,24,128]{2,1,0:T(8,128)(2,1)S(1)}, bf16[4,24,128]{2,1,0:T(8,128)(2,1)S(1)}, u32[]{:S(2)}, u32[]{:S(2)}) %collective-permute-start.7) | collective-permute-done | bytes 24608 | tf_op jit(solution)/shard_map/ppermute | solution.py:32
  54.5 2.6 %collective-permute-start.8 = (bf16[8,24,128]{2,1,0:T(8,128)(2,1)S(1)}, bf16[8,24,128]{2,1,0:T(8,128)(2,1)S(1)}, u32[]{:S(2)}, u32[]{:S(2)}) collective-permute-start(bf16[8,24,128]{2,1,0:T(8,128)(2,1)S(1)} %pad_maximum_fusion.5), channel_id=1, source_target_pairs={{0,16},{16,0},{32,48},{48,32},{64,80},{80,64},{96,112},{112,96},{1... | collective-permute-start | bytes 147464 | tf_op jit(solution)/shard_map/ppermute | solution.py:32
  57.2 5.9 %collective-permute-start.2 = (f32[4,48,128]{2,1,0:T(8,128)S(1)}, f32[4,48,128]{2,1,0:T(8,128)S(1)}, u32[]{:S(2)}, u32[]{:S(2)}) collective-permute-start(f32[4,48,128]{2,1,0:T(8,128)S(1)} %pad_maximum_fusion.3), channel_id=1, source_target_pairs={{0,4},{1,5},{2,6},{3,7},{4,0},{5,1},{6,2},{7,3},{8,12},{9,13},{10,... | collective-permute-start | bytes 294920 | tf_op jit(solution)/shard_map/ppermute | solution.py:32
  63.1 3.2 %collective-permute-start.9 = (bf16[16,24,128]{2,1,0:T(8,128)(2,1)S(1)}, bf16[16,24,128]{2,1,0:T(8,128)(2,1)S(1)}, u32[]{:S(2)}, u32[]{:S(2)}) collective-permute-start(bf16[16,24,128]{2,1,0:T(8,128)(2,1)S(1)} %get-tuple-element.36), channel_id=1, source_target_pairs={{0,256},{16,272},{32,288},{48,304},{64,320},{80,336},{96,352},{112... | collective-permute-start | bytes 294920 | tf_op jit(solution)/shard_map/ppermute | solution.py:32
  66.4 7.1 %collective-permute-start.3 = (f32[8,48,128]{2,1,0:T(8,128)S(1)}, f32[8,48,128]{2,1,0:T(8,128)S(1)}, u32[]{:S(2)}, u32[]{:S(2)}) collective-permute-start(f32[8,48,128]{2,1,0:T(8,128)S(1)} %pad_maximum_fusion.1), channel_id=1, source_target_pairs={{0,1},{1,0},{2,3},{3,2},{4,5},{5,4},{6,7},{7,6},{8,9},{9,8},{10,11... | collective-permute-start | bytes 589832 | tf_op jit(solution)/shard_map/ppermute | solution.py:32
  73.5 0.6 gather_fusion.1
  74.1 0.3 gather.15
  74.4 0.3 select_bitcast_fusion
  74.7 0.5 copy.60
  75.2 0.2 reshape.895
  75.4 0.2 stack.40
  76.0 1.1 slice_bitcast_fusion.14
  77.1 0.6 gather_fusion
  77.9 0.2 convert_element_type.98
  78.1 0.2 convert_element_type.97
  78.3 0.9 reshape_transpose_reshape.7
  79.3 11.6 %fusion.117 = (f32[256,12,1]{2,1,0:T(8,128)}, f32[256,12,1]{2,1,0:T(8,128)}, f32[256,12,1]{2,1,0:T(8,128)}, f32[256,12,1]{2,1,0:T(8,128)}, f32[256,12,1]{2,1,0:T...) fusion(f32[256,12,12]{2,1,0:T(8,128)S(1)} %reshape_transpose_re, ...), kind=kLoop, calls=%fused_computation.282 | loop fusion | bytes 294912 | tf_op jit(solution)/shard_map/slice | solution.py:106
  90.9 2.7 %copy.58 = f32[256,12,1]{0,1,2:T(8,128)S(1)} copy(f32[256,12,1]{2,1,0:T(8,128)} %get-tuple-element.6) | data formatting | bytes 24576 | tf_op jit(solution)/shard_map/slice | solution.py:106
  93.5 1.0 copy.63
  94.6 2.7 %copy.64 = f32[256,12,1]{0,1,2:T(8,128)S(1)} copy(f32[256,12,1]{2,1,0:T(8,128)} %get-tuple-element.16) | data formatting | bytes 24576 | tf_op jit(solution)/shard_map/slice | solution.py:108
  97.2 1.0 copy.65
  98.3 2.7 %copy.66 = f32[256,12,1]{0,1,2:T(8,128)S(1)} copy(f32[256,12,1]{2,1,0:T(8,128)} %get-tuple-element.14) | data formatting | bytes 24576 | tf_op jit(solution)/shard_map/slice | solution.py:108
  100.9 1.0 copy.67
  102.0 2.7 %copy.68 = f32[256,12,1]{0,1,2:T(8,128)S(1)} copy(f32[256,12,1]{2,1,0:T(8,128)} %get-tuple-element.12) | data formatting | bytes 24576 | tf_op jit(solution)/shard_map/slice | solution.py:108
  104.7 1.0 copy.69
  105.7 3.3 %copy.70 = f32[256,12,1]{0,1,2:T(8,128)} copy(f32[256,12,1]{2,1,0:T(8,128)} %get-tuple-element.10) | data formatting | bytes 24576 | tf_op jit(solution)/shard_map/slice | solution.py:108
  109.0 1.6 %copy.71 = f32[256,12,1]{0,1,2:T(8,128)} copy(f32[256,12,1]{2,1,0:T(8,128)S(1)} %copy-done.1) | data formatting | bytes 24576 | tf_op jit(solution)/shard_map/slice | solution.py:108
  110.6 3.3 %copy.72 = f32[256,12,1]{0,1,2:T(8,128)} copy(f32[256,12,1]{2,1,0:T(8,128)} %get-tuple-element.8) | data formatting | bytes 24576 | tf_op jit(solution)/shard_map/slice | solution.py:108
  113.8 1.6 %copy.73 = f32[256,12,1]{0,1,2:T(8,128)} copy(f32[256,12,1]{2,1,0:T(8,128)S(1)} %copy-done) | data formatting | bytes 24576 | tf_op jit(solution)/shard_map/slice | solution.py:108
  115.5 0.2 slice_bitcast_fusion.2
  115.7 1.3 %pad_maximum_fusion = bf16[4,64,4,3,64]{4,3,1,0,2:T(4,128)(2,1)S(1)} fusion(bf16[4,64,1,3,64]{4,3,1,0,2:T(4,128)(2,1)S(1)} %get-tuple-element.32, bf16[4,64,1,3,64]{4,3,1,0,2:T(4,128)(2,1)S(1)} %get-tuple-element.31, bf16[4,64,1,3,64]{4,3,1,0,2:T(4,128)(2,1)S(1)} %get-tuple-element.30, bf16[4,64,1,3,64]{4,3,1,0,2:T(4,128)(2,1)S(1)} %convert_element_type.97), kind=kLoop, calls=%fused_computation.28 | loop fusion | flops 589824 | bytes 786432 | tf_op jit(solution)/shard_map/stack | solution.py:49
  117.1 0.9 copy.57
  118.1 0.5 reshape.893
  118.8 0.4 convolution_bitcast_fusion
  119.2 0.6 dynamic_slice.3
  119.9 5.9 %fusion.24 = f32[64,128]{1,0:T(8,128)} fusion(bf16[256,12,64]{0,2,1:T(8,128)(2,1)S(1)} %reshape.893, f32[256,128]{1,0:T(8,128)S(1)} %get-tuple-element.19, f32[256,12]{0,1:T(8,128)S(1)} %bitcast.114, f32[256,128]{1,0:T(8,128)S(1)} %get-tuple-element.20, f32[256,12]{0,1:T(8,128)S(1)} %bitcast.113, f32[256,128]{1,0:T(8,128)S(1)} %copy-done.7, ...), kind=kOutput, calls=%fused_computation.26 | convolution fusion | flops 311033856 | bytes 2146304 | tf_op jit(solution)/shard_map/eip,eiq->pq/dot_general | solution.py:109
  (102 shorter events, 2.8 us)
Async XLA Ops:
  3.4 1.3 %copy-start.16 = (bf16[1,16,3,64]{3,1,2,0:T(8,128)(2,1)S(1)}, bf16[1,16,3,64]{3,1,2,0:T(8,128)(2,1)}, u32[]{:S(2)}) copy-start(bf16[1,16,3,64]{3,1,2,0:T(8,128)(2,1)} %param.9) | copy-start | bytes 18436
  4.8 40.0 %collective-permute-start = (f32[1,48,128]{2,1,0:T(8,128)S(1)}, f32[1,48,128]{2,1,0:T(8,128)S(1)}, u32[]{:S(2)}, u32[]{:S(2)}) collective-permute-start(f32[1,48,128]{2,1,0:T(8,128)S(1)} %get-tuple-element.3), channel_id=1, source_target_pairs={{0,8},{1,9},{2,10},{3,11},{4,12},{5,13},{6,14},{7,15},{8,0},{9,1},... | collective-permute-start | bytes 73736 | tf_op jit(solution)/shard_map/ppermute | solution.py:32
  10.4 7.0 %collective-permute-start.4 = (bf16[24,128]{1,0:T(8,128)(2,1)S(1)}, bf16[24,128]{1,0:T(8,128)(2,1)S(1)}, u32[]{:S(2)}, u32[]{:S(2)}) collective-permute-start(bf16[24,128]{1,0:T(8,128)(2,1)S(1)} %reshape.894), channel_id=1, source_target_pairs={{0,0},{1,32},{2,64},{3,96},{4,128},{5,160},{6,192},{7,224},{8,256}... | collective-permute-start | bytes 18440 | tf_op jit(solution)/shard_map/ppermute | solution.py:98
  17.4 22.2 %collective-permute-start.5 = (bf16[1,24,128]{2,1,0:T(8,128)(2,1)S(1)}, bf16[1,24,128]{2,1,0:T(8,128)(2,1)S(1)}, u32[]{:S(2)}, u32[]{:S(2)}) collective-permute-start(bf16[1,24,128]{2,1,0:T(8,128)(2,1)S(1)} %bitcast.99), channel_id=1, source_target_pairs={{0,128},{16,144},{32,160},{48,176},{64,192},{80,208},{96,224},{112... | collective-permute-start | bytes 18440 | tf_op jit(solution)/shard_map/ppermute | solution.py:32
  39.6 8.9 %collective-permute-start.6 = (bf16[2,24,128]{2,1,0:T(8,128)(2,1)S(1)}, bf16[2,24,128]{2,1,0:T(8,128)(2,1)S(1)}, u32[]{:S(2)}, u32[]{:S(2)}) collective-permute-start(bf16[2,24,128]{2,1,0:T(8,128)(2,1)S(1)} %pad_maximum_fusion.7), channel_id=1, source_target_pairs={{0,64},{16,80},{32,96},{48,112},{64,0},{80,16},{96,32},{112,48},{1... | collective-permute-start | bytes 36872 | tf_op jit(solution)/shard_map/ppermute | solution.py:32
  44.8 12.4 %collective-permute-start.1 = (f32[2,48,128]{2,1,0:T(8,128)S(1)}, f32[2,48,128]{2,1,0:T(8,128)S(1)}, u32[]{:S(2)}, u32[]{:S(2)}) collective-permute-start(f32[2,48,128]{2,1,0:T(8,128)S(1)} %pad_maximum_fusion.4), channel_id=1, source_target_pairs={{0,2},{1,3},{2,0},{3,1},{4,6},{5,7},{6,4},{7,5},{8,10},{9,11},{10,... | collective-permute-start | bytes 147464 | tf_op jit(solution)/shard_map/ppermute | solution.py:32
  48.5 6.0 %collective-permute-start.7 = (bf16[4,24,128]{2,1,0:T(8,128)(2,1)S(1)}, bf16[4,24,128]{2,1,0:T(8,128)(2,1)S(1)}, u32[]{:S(2)}, u32[]{:S(2)}) collective-permute-start(bf16[4,24,128]{2,1,0:T(8,128)(2,1)S(1)} %pad_maximum_fusion.6), channel_id=1, source_target_pairs={{0,32},{16,48},{32,0},{48,16},{64,96},{80,112},{96,64},{112,80},{1... | collective-permute-start | bytes 73736 | tf_op jit(solution)/shard_map/ppermute | solution.py:32
  54.5 8.6 %collective-permute-start.8 = (bf16[8,24,128]{2,1,0:T(8,128)(2,1)S(1)}, bf16[8,24,128]{2,1,0:T(8,128)(2,1)S(1)}, u32[]{:S(2)}, u32[]{:S(2)}) collective-permute-start(bf16[8,24,128]{2,1,0:T(8,128)(2,1)S(1)} %pad_maximum_fusion.5), channel_id=1, source_target_pairs={{0,16},{16,0},{32,48},{48,32},{64,80},{80,64},{96,112},{112,96},{1... | collective-permute-start | bytes 147464 | tf_op jit(solution)/shard_map/ppermute | solution.py:32
  57.2 9.1 %collective-permute-start.2 = (f32[4,48,128]{2,1,0:T(8,128)S(1)}, f32[4,48,128]{2,1,0:T(8,128)S(1)}, u32[]{:S(2)}, u32[]{:S(2)}) collective-permute-start(f32[4,48,128]{2,1,0:T(8,128)S(1)} %pad_maximum_fusion.3), channel_id=1, source_target_pairs={{0,4},{1,5},{2,6},{3,7},{4,0},{5,1},{6,2},{7,3},{8,12},{9,13},{10,... | collective-permute-start | bytes 294920 | tf_op jit(solution)/shard_map/ppermute | solution.py:32
  63.1 10.3 %collective-permute-start.9 = (bf16[16,24,128]{2,1,0:T(8,128)(2,1)S(1)}, bf16[16,24,128]{2,1,0:T(8,128)(2,1)S(1)}, u32[]{:S(2)}, u32[]{:S(2)}) collective-permute-start(bf16[16,24,128]{2,1,0:T(8,128)(2,1)S(1)} %get-tuple-element.36), channel_id=1, source_target_pairs={{0,256},{16,272},{32,288},{48,304},{64,320},{80,336},{96,352},{112... | collective-permute-start | bytes 294920 | tf_op jit(solution)/shard_map/ppermute | solution.py:32
  66.4 10.7 %collective-permute-start.3 = (f32[8,48,128]{2,1,0:T(8,128)S(1)}, f32[8,48,128]{2,1,0:T(8,128)S(1)}, u32[]{:S(2)}, u32[]{:S(2)}) collective-permute-start(f32[8,48,128]{2,1,0:T(8,128)S(1)} %pad_maximum_fusion.1), channel_id=1, source_target_pairs={{0,1},{1,0},{2,3},{3,2},{4,5},{5,4},{6,7},{7,6},{8,9},{9,8},{10,11... | collective-permute-start | bytes 589832 | tf_op jit(solution)/shard_map/ppermute | solution.py:32
  77.8 1.4 %copy-start.6 = (f32[16,6144]{1,0:T(8,128)}, f32[16,6144]{1,0:T(8,128)S(1)}, u32[]{:S(2)}) copy-start(f32[16,6144]{1,0:T(8,128)S(1)} %bitcast_select_fusion) | copy-start | bytes 1179652
  90.8 2.7 %copy-start.5 = (f32[256,12,1]{2,1,0:T(8,128)S(1)}, f32[256,12,1]{2,1,0:T(8,128)}, u32[]{:S(2)}) copy-start(f32[256,12,1]{2,1,0:T(8,128)} %get-tuple-element.17) | copy-start | bytes 36868
  94.6 2.7 %copy-start.4 = (f32[256,12,1]{2,1,0:T(8,128)S(1)}, f32[256,12,1]{2,1,0:T(8,128)}, u32[]{:S(2)}) copy-start(f32[256,12,1]{2,1,0:T(8,128)} %get-tuple-element.15) | copy-start | bytes 36868
  98.3 2.7 %copy-start.3 = (f32[256,12,1]{2,1,0:T(8,128)S(1)}, f32[256,12,1]{2,1,0:T(8,128)}, u32[]{:S(2)}) copy-start(f32[256,12,1]{2,1,0:T(8,128)} %get-tuple-element.13) | copy-start | bytes 36868
  102.0 2.7 %copy-start.2 = (f32[256,12,1]{2,1,0:T(8,128)S(1)}, f32[256,12,1]{2,1,0:T(8,128)}, u32[]{:S(2)}) copy-start(f32[256,12,1]{2,1,0:T(8,128)} %get-tuple-element.11) | copy-start | bytes 36868
  105.7 3.3 %copy-start.1 = (f32[256,12,1]{2,1,0:T(8,128)S(1)}, f32[256,12,1]{2,1,0:T(8,128)}, u32[]{:S(2)}) copy-start(f32[256,12,1]{2,1,0:T(8,128)} %get-tuple-element.9) | copy-start | bytes 36868
  110.6 3.3 %copy-start = (f32[256,12,1]{2,1,0:T(8,128)S(1)}, f32[256,12,1]{2,1,0:T(8,128)}, u32[]{:S(2)}) copy-start(f32[256,12,1]{2,1,0:T(8,128)} %get-tuple-element.7) | copy-start | bytes 36868
  117.0 1.6 %slice-start = ((f32[16,6144]{1,0:T(8,128)}), f32[16,192]{1,0:T(8,128)S(1)}, s32[]{:S(2)}) async-start(f32[16,6144]{1,0:T(8,128)} %copy-done.6), calls=%async_computation | async-start | bytes 32768 | tf_op jit(solution)/shard_map/slice | solution.py:91
  117.0 2.8 %copy-start.7 = (f32[256,128]{1,0:T(8,128)S(1)}, f32[256,128]{1,0:T(8,128)}, u32[]{:S(2)}) copy-start(f32[256,128]{1,0:T(8,128)} %get-tuple-element.21) | copy-start | bytes 393220
  117.0 2.8 %copy-start.8 = (f32[256,128]{1,0:T(8,128)S(1)}, f32[256,128]{1,0:T(8,128)}, u32[]{:S(2)}) copy-start(f32[256,128]{1,0:T(8,128)} %get-tuple-element.22) | copy-start | bytes 393220
  117.1 2.7 %copy-start.9 = (f32[256,128]{1,0:T(8,128)S(1)}, f32[256,128]{1,0:T(8,128)}, u32[]{:S(2)}) copy-start(f32[256,128]{1,0:T(8,128)} %get-tuple-element.23) | copy-start | bytes 393220
  117.1 2.7 %copy-start.10 = (f32[256,128]{1,0:T(8,128)S(1)}, f32[256,128]{1,0:T(8,128)}, u32[]{:S(2)}) copy-start(f32[256,128]{1,0:T(8,128)} %get-tuple-element.24) | copy-start | bytes 393220
  117.1 2.7 %copy-start.11 = (f32[256,128]{1,0:T(8,128)S(1)}, f32[256,128]{1,0:T(8,128)}, u32[]{:S(2)}) copy-start(f32[256,128]{1,0:T(8,128)} %get-tuple-element.25) | copy-start | bytes 393220
  117.1 2.7 %copy-start.12 = (f32[256,128]{1,0:T(8,128)S(1)}, f32[256,128]{1,0:T(8,128)}, u32[]{:S(2)}) copy-start(f32[256,128]{1,0:T(8,128)} %get-tuple-element.26) | copy-start | bytes 393220
  117.1 2.7 %copy-start.13 = (f32[256,128]{1,0:T(8,128)S(1)}, f32[256,128]{1,0:T(8,128)}, u32[]{:S(2)}) copy-start(f32[256,128]{1,0:T(8,128)} %get-tuple-element.27) | copy-start | bytes 393220
  117.1 2.7 %copy-start.14 = (f32[256,128]{1,0:T(8,128)S(1)}, f32[256,128]{1,0:T(8,128)}, u32[]{:S(2)}) copy-start(f32[256,128]{1,0:T(8,128)} %get-tuple-element.28) | copy-start | bytes 393220
  117.1 2.7 %copy-start.15 = (f32[256,128]{1,0:T(8,128)S(1)}, f32[256,128]{1,0:T(8,128)}, u32[]{:S(2)}) copy-start(f32[256,128]{1,0:T(8,128)} %get-tuple-element.29) | copy-start | bytes 393220
  118.1 1.8 %copy-start.17 = (f32[256,12,1]{0,1,2:T(8,128)S(1)}, f32[256,12,1]{0,1,2:T(8,128)}, u32[]{:S(2)}) copy-start(f32[256,12,1]{0,1,2:T(8,128)} %copy.70) | copy-start | bytes 36868
  118.1 1.8 %copy-start.18 = (f32[256,12,1]{0,1,2:T(8,128)S(1)}, f32[256,12,1]{0,1,2:T(8,128)}, u32[]{:S(2)}) copy-start(f32[256,12,1]{0,1,2:T(8,128)} %copy.71) | copy-start | bytes 36868
  118.1 1.8 %copy-start.19 = (f32[256,12,1]{0,1,2:T(8,128)S(1)}, f32[256,12,1]{0,1,2:T(8,128)}, u32[]{:S(2)}) copy-start(f32[256,12,1]{0,1,2:T(8,128)} %copy.72) | copy-start | bytes 36868
  118.1 1.8 %copy-start.20 = (f32[256,12,1]{0,1,2:T(8,128)S(1)}, f32[256,12,1]{0,1,2:T(8,128)}, u32[]{:S(2)}) copy-start(f32[256,12,1]{0,1,2:T(8,128)} %copy.73) | copy-start | bytes 36868

commit v2 on v1

--- a/solution.py
+++ b/solution.py
@@ -47,9 +47,10 @@
 def element_corners(nodes):
     extended = jnp.pad(nodes, ((0, 1), (0, 1), (0, 0), (0, 0)))
     corners = jnp.stack(
-        [extended[:-1, :-1], extended[:-1, 1:], extended[1:, :-1], extended[1:, 1:]], axis=2
+        [extended[:-1, :-1], extended[:-1, 1:], extended[1:, :-1], extended[1:, 1:]], axis=0
     )
-    return corners.reshape(nodes.shape[0] * nodes.shape[1], 12, nodes.shape[3])
+    corners = corners.transpose(0, 3, 1, 2, 4)
+    return corners.reshape(12, nodes.shape[0] * nodes.shape[1], nodes.shape[3])
 
 
 def on_device(coefficients, noise_sigma, residual, crack_mask, node_panel):
@@ -101,13 +102,19 @@
     cross = cross.transpose(0, 3, 1, 4, 5, 2, 6)
     cross = cross.reshape(n_row * node_rows, n_col * node_cols, comps, per_block * width)
 
-    rows_of = element_corners(own_nodes.astype(jnp.bfloat16)).astype(jnp.float32)
+    rows_of = element_corners(own_nodes.astype(jnp.bfloat16))
     cols_of = element_corners(cross).astype(jnp.float32)
-    weighted_cols = grams[:, :, 0, None] * cols_of[:, None, 0, :]
-    for j in range(1, 12):
-        weighted_cols = weighted_cols + grams[:, :, j, None] * cols_of[:, None, j, :]
-    hessian = jnp.einsum("eip,eiq->pq", rows_of, weighted_cols, precision=HIGHEST)
-    gradient = jnp.einsum("eip,ei->p", rows_of, projs, precision=HIGHEST)
+    weighted_cols = jnp.sum(grams.transpose(1, 2, 0)[:, :, :, None] * cols_of[None], axis=1)
+    high = weighted_cols.astype(jnp.bfloat16)
+    low = (weighted_cols - high.astype(jnp.float32)).astype(jnp.bfloat16)
+    proj_t = projs.T[:, :, None]
+    proj_high = proj_t.astype(jnp.bfloat16)
+    proj_low = (proj_t - proj_high.astype(jnp.float32)).astype(jnp.bfloat16)
+    operand = jnp.concatenate([high, low, proj_high, proj_low], axis=2)
+    product = jnp.einsum("iep,ieq->pq", rows_of, operand, preferred_element_type=jnp.float32)
+    cols = cross.shape[3]
+    hessian = product[:, :cols] + product[:, cols : 2 * cols]
+    gradient = product[:, 2 * cols] + product[:, 2 * cols + 1]
     share = width // tiles
     gradient = lax.dynamic_slice(gradient, (lax.axis_index(("row", "col")) * share,), (share,))
     return (hessian, gradient)

time: 127 us -> 92.6 us (0.73)
  local copies, waits for them, and re-layouts: 46 us -> 13.8 us
  other arithmetic: 3.79 us -> 12.4 us
  matrix products: 6.63 us -> 1.03 us
  starting transfers between devices: 64.5 us -> 60.7 us
    slice x13 -> x1, local copies, waits for them, and re-layouts: 36.2 us -> 0.07 us  [on_device(): gradient = product[:, 2 * cols] + product[:, 2 * cols + 1]]
    reduce_sum x0 -> x1, other arithmetic: none -> 7.29 us  [on_device(): jnp.sum(grams.transpose(1, 2, 0)[:, :, :, None] * cols_of[None], axis=1)]
    dot_general x2 -> x1, matrix products: 6.31 us -> 0.71 us  [on_device(): jnp.einsum('iep,ieq->pq', rows_of, operand, preferred_element_type=jnp.fl...]
    ppermute x9, starting transfers between devices: 58.7 us -> 54.4 us  [doubling_gather(): theirs = lax.ppermute(data, axes, [(i, i ^ bit) for i in range(size)])]
    transpose x0 -> x2, local copies, waits for them, and re-layouts: none -> 2.43 us  [the longest x1 1.51 us: on_device(): grams.transpose(1, 2, 0)[:, :, :, None] * cols_of[None]]
    another operation x1 -> x0, other arithmetic: 1.28 us -> none  [element_corners(): jnp.stack([extended[:-1, :-1], extended[:-1, 1:], extended[1:, :-1], exte...]
  transfers between devices with their start and end apart: 10 -> 10, of which waited for: 3 -> 2; matrix products, arithmetic and copies ran while one was open for 3% -> 9% of each run, Pallas kernels for 0% -> 0%
where the time goes in v2:
time: 92.6 us; the launch traced here: 91.8 us
  starting transfers between devices  60.7 us (66%)
  local copies, waits for them, and re-layouts  13.8 us (15%)
  other arithmetic  12.4 us (13%)
  waiting for transfers between devices  2.73 us (3%)
  between operations  1.19 us (1%)
  matrix products  1.03 us (1%)
    ppermute x9, starting transfers between devices, doubling_gather(): theirs = lax.ppermute(data, axes, [(i, i ^ bit) for i in range(size)])  54.4 us
    reduce_sum x1, other arithmetic, on_device(): jnp.sum(grams.transpose(1, 2, 0)[:, :, :, None] * cols_of[None], axis=1)  7.29 us
    ppermute x1, starting transfers between devices, on_device(): lax.ppermute(as_lanes(node_panel.reshape(-1), jnp.bfloat16), ('param', 'r...  6.27 us
    ppermute x9, waiting for transfers between devices, doubling_gather(): theirs = lax.ppermute(data, axes, [(i, i ^ bit) for i in range(size)])  2.73 us
  transfers between devices with their start and end apart: 10, of which 2 were waited for; matrix products, arithmetic and copies ran while one was open for 9% of the time, Pallas kernels for 0%

profile of v2, /device:TPU:1, one launch (start us, length us, event | category | flops | bytes accessed | tf_op | source)
XLA Modules:
  0.0 91.8 jit_solution(15279153796563208971)
XLA Ops:
  0.6 0.7 copy.79
  1.4 6.3 %collective-permute-start.4 = (bf16[24,128]{1,0:T(8,128)(2,1)S(1)}, bf16[24,128]{1,0:T(8,128)(2,1)S(1)}, u32[]{:S(2)}, u32[]{:S(2)}) collective-permute-start(bf16[24,128]{1,0:T(8,128)(2,1)S(1)} %reshape.906), channel_id=1, source_target_pairs={{0,0},{1,32},{2,64},{3,96},{4,128},{5,160},{6,192},{7,224},{8,256}... | collective-permute-start | bytes 18440 | tf_op jit(solution)/shard_map/ppermute | solution.py:99
  7.7 0.7 copy.71
  8.5 0.7 convert_bitcast_fusion.1
  9.1 0.8 multiply_convert_fusion.1
  10.1 0.9 %reshape.909 = f32[3,2,8,16,8]{4,3,2,1,0:T(8,128)S(1)} reshape(bf16[3,2,8,128]{3,2,1,0:T(8,128)(2,1)} %param.5) | data formatting | bytes 36864 | tf_op jit(solution)/shard_map/mul | solution.py:73
  11.0 0.1 copy.73
  11.4 0.2 copy.74
  11.7 0.1 reshape.902
  11.9 0.2 fusion.83
  12.1 0.1 fusion.84
  12.6 5.6 %collective-permute-start = (f32[1,48,128]{2,1,0:T(8,128)S(1)}, f32[1,48,128]{2,1,0:T(8,128)S(1)}, u32[]{:S(2)}, u32[]{:S(2)}) collective-permute-start(f32[1,48,128]{2,1,0:T(8,128)S(1)} %get-tuple-element.5), channel_id=1, source_target_pairs={{0,8},{1,9},{2,10},{3,11},{4,12},{5,13},{6,14},{7,15},{8,0},{9,1},... | collective-permute-start | bytes 73736 | tf_op jit(solution)/shard_map/ppermute | solution.py:32
  18.4 12.0 %collective-permute-start.5 = (bf16[1,24,128]{2,1,0:T(8,128)(2,1)S(1)}, bf16[1,24,128]{2,1,0:T(8,128)(2,1)S(1)}, u32[]{:S(2)}, u32[]{:S(2)}) collective-permute-start(bf16[1,24,128]{2,1,0:T(8,128)(2,1)S(1)} %bitcast.80), channel_id=1, source_target_pairs={{0,128},{16,144},{32,160},{48,176},{64,192},{80,208},{96,224},{112... | collective-permute-start | bytes 18440 | tf_op jit(solution)/shard_map/ppermute | solution.py:32
  30.5 1.0 %collective-permute-done.5 = bf16[1,24,128]{2,1,0:T(8,128)(2,1)S(1)} collective-permute-done((bf16[1,24,128]{2,1,0:T(8,128)(2,1)S(1)}, bf16[1,24,128]{2,1,0:T(8,128)(2,1)S(1)}, u32[]{:S(2)}, u32[]{:S(2)}) %collective-permute-start.5) | collective-permute-done | bytes 6176 | tf_op jit(solution)/shard_map/ppermute | solution.py:32
  31.5 6.6 %collective-permute-start.6 = (bf16[2,24,128]{2,1,0:T(8,128)(2,1)S(1)}, bf16[2,24,128]{2,1,0:T(8,128)(2,1)S(1)}, u32[]{:S(2)}, u32[]{:S(2)}) collective-permute-start(bf16[2,24,128]{2,1,0:T(8,128)(2,1)S(1)} %pad_maximum_fusion.6), channel_id=1, source_target_pairs={{0,64},{16,80},{32,96},{48,112},{64,0},{80,16},{96,32},{112,48},{1... | collective-permute-start | bytes 36872 | tf_op jit(solution)/shard_map/ppermute | solution.py:32
  38.1 1.7 %collective-permute-done.6 = bf16[2,24,128]{2,1,0:T(8,128)(2,1)S(1)} collective-permute-done((bf16[2,24,128]{2,1,0:T(8,128)(2,1)S(1)}, bf16[2,24,128]{2,1,0:T(8,128)(2,1)S(1)}, u32[]{:S(2)}, u32[]{:S(2)}) %collective-permute-start.6) | collective-permute-done | bytes 12320 | tf_op jit(solution)/shard_map/ppermute | solution.py:32
  39.8 4.3 %collective-permute-start.7 = (bf16[4,24,128]{2,1,0:T(8,128)(2,1)S(1)}, bf16[4,24,128]{2,1,0:T(8,128)(2,1)S(1)}, u32[]{:S(2)}, u32[]{:S(2)}) collective-permute-start(bf16[4,24,128]{2,1,0:T(8,128)(2,1)S(1)} %pad_maximum_fusion.5), channel_id=1, source_target_pairs={{0,32},{16,48},{32,0},{48,16},{64,96},{80,112},{96,64},{112,80},{1... | collective-permute-start | bytes 73736 | tf_op jit(solution)/shard_map/ppermute | solution.py:32
  44.1 7.9 %collective-permute-start.1 = (f32[2,48,128]{2,1,0:T(8,128)S(1)}, f32[2,48,128]{2,1,0:T(8,128)S(1)}, u32[]{:S(2)}, u32[]{:S(2)}) collective-permute-start(f32[2,48,128]{2,1,0:T(8,128)S(1)} %pad_maximum_fusion.3), channel_id=1, source_target_pairs={{0,2},{1,3},{2,0},{3,1},{4,6},{5,7},{6,4},{7,5},{8,10},{9,11},{10,... | collective-permute-start | bytes 147464 | tf_op jit(solution)/shard_map/ppermute | solution.py:32
  52.2 3.5 %collective-permute-start.8 = (bf16[8,24,128]{2,1,0:T(8,128)(2,1)S(1)}, bf16[8,24,128]{2,1,0:T(8,128)(2,1)S(1)}, u32[]{:S(2)}, u32[]{:S(2)}) collective-permute-start(bf16[8,24,128]{2,1,0:T(8,128)(2,1)S(1)} %pad_maximum_fusion.4), channel_id=1, source_target_pairs={{0,16},{16,0},{32,48},{48,32},{64,80},{80,64},{96,112},{112,96},{1... | collective-permute-start | bytes 147464 | tf_op jit(solution)/shard_map/ppermute | solution.py:32
  55.8 5.7 %collective-permute-start.2 = (f32[4,48,128]{2,1,0:T(8,128)S(1)}, f32[4,48,128]{2,1,0:T(8,128)S(1)}, u32[]{:S(2)}, u32[]{:S(2)}) collective-permute-start(f32[4,48,128]{2,1,0:T(8,128)S(1)} %pad_maximum_fusion.2), channel_id=1, source_target_pairs={{0,4},{1,5},{2,6},{3,7},{4,0},{5,1},{6,2},{7,3},{8,12},{9,13},{10,... | collective-permute-start | bytes 294920 | tf_op jit(solution)/shard_map/ppermute | solution.py:32
  61.5 2.8 %collective-permute-start.9 = (bf16[16,24,128]{2,1,0:T(8,128)(2,1)S(1)}, bf16[16,24,128]{2,1,0:T(8,128)(2,1)S(1)}, u32[]{:S(2)}, u32[]{:S(2)}) collective-permute-start(bf16[16,24,128]{2,1,0:T(8,128)(2,1)S(1)} %get-tuple-element.16), channel_id=1, source_target_pairs={{0,256},{16,272},{32,288},{48,304},{64,320},{80,336},{96,352},{112... | collective-permute-start | bytes 294920 | tf_op jit(solution)/shard_map/ppermute | solution.py:32
  64.4 5.8 %collective-permute-start.3 = (f32[8,48,128]{2,1,0:T(8,128)S(1)}, f32[8,48,128]{2,1,0:T(8,128)S(1)}, u32[]{:S(2)}, u32[]{:S(2)}) collective-permute-start(f32[8,48,128]{2,1,0:T(8,128)S(1)} %pad_maximum_fusion), channel_id=1, source_target_pairs={{0,1},{1,0},{2,3},{3,2},{4,5},{5,4},{6,7},{7,6},{8,9},{9,8},{10,11... | collective-permute-start | bytes 589832 | tf_op jit(solution)/shard_map/ppermute | solution.py:32
  70.3 0.6 gather_fusion.1
  70.9 0.3 gather.15
  71.2 0.3 select_bitcast_fusion
  71.5 0.5 copy.80
  72.0 0.2 reshape.907
  72.3 0.2 stack.40
  72.5 0.1 convert_bitcast_fusion
  72.7 1.3 %copy.82 = f32[4,3,4,64,128]{4,3,2,1,0:T(8,128)} copy(f32[4,3,4,64,128]{4,3,1,2,0:T(8,128)S(1)} %convert_bitcast_fusion) | data formatting | bytes 3145728 | tf_op jit(solution)/shard_map/convert_element_type | solution.py:106
  74.0 0.6 gather_fusion
  74.5 0.1 bitcast_select_fusion
  74.7 0.2 convert_element_type.129
  75.0 0.9 %convert_element_type.128 = bf16[1,4,64,3,64]{4,3,2,1,0:T(4,128)(2,1)} reshape(bf16[16,3072]{1,0:T(8,128)(2,1)S(1)} %slice.80) | data formatting | bytes 196608 | tf_op jit(solution)/shard_map/convert_element_type | solution.py:105
  75.9 0.1 reshape_transpose_reshape.8
  76.1 0.9 %reshape_transpose_reshape.7 = f32[256,12,12]{2,1,0:T(8,128)S(1)} reshape(f32[16,2304]{1,0:T(8,128)S(1)} %slice.59) | data formatting | bytes 294912 | tf_op jit(solution)/shard_map/reshape;transpose;reshape | solution.py:91
  77.0 1.5 %copy.78 = f32[12,12,256]{2,1,0:T(8,128)} copy(f32[12,12,256]{1,0,2:T(8,128)S(1)} %bitcast.74) | data formatting | bytes 294912 | tf_op jit(solution)/shard_map/transpose | solution.py:107
  78.5 7.3 %multiply_reduce_fusion = f32[12,256,128]{2,1,0:T(8,128)S(1)} fusion(f32[12,256,128]{2,1,0:T(8,128)} %bitcast.75, f32[12,12,256]{2,1,0:T(8,128)} %copy.78), kind=kLoop, calls=%fused_computation.2 | loop fusion | flops 9043968 | bytes 3293184 | tf_op jit(solution)/shard_map/reduce_sum | solution.py:107
  85.8 0.5 copy.83
  86.3 0.2 subtract_convert_fusion
  86.6 0.2 slice_bitcast_fusion.2
  86.8 0.4 copy-done
  87.3 1.1 %maximum_bitcast_fusion = bf16[4,3,4,64,64]{4,1,3,2,0:T(4,128)(2,1)S(1)} fusion(bf16[1,4,64,3,64]{4,3,2,1,0:T(4,128)(2,1)S(1)} %get-tuple-element.10, bf16[1,4,64,3,64]{4,3,2,1,0:T(4,128)(2,1)S(1)} %get-tuple-element.9, bf16[1,4,64,3,64]{4,3,2,1,0:T(4,128)(2,1)S(1)} %get-tuple-element.8, bf16[1,4,64,3,64]{4,3,2,1,0:T(4,128)(2,1)S(1)} %copy-done), kind=kLoop, calls=%fused_computation.14 | loop fusion | flops 589824 | bytes 786432 | tf_op jit(solution)/shard_map/transpose | solution.py:52
  88.3 0.9 %copy.77 = bf16[4,3,4,64,64]{3,2,4,1,0:T(4,128)(2,1)S(1)} copy(bf16[4,3,4,64,64]{4,1,3,2,0:T(4,128)(2,1)S(1)} %maximum_bitcast_fusion) | data formatting | bytes 786432 | tf_op jit(solution)/shard_map/transpose | solution.py:52
  89.3 0.5 reshape.905
  89.8 0.7 fusion.8
  90.6 0.6 slice_add_fusion
  91.2 0.6 fusion.41
  (56 shorter events, 1.7 us)
Async XLA Ops:
  1.4 17.0 %collective-permute-start.4 = (bf16[24,128]{1,0:T(8,128)(2,1)S(1)}, bf16[24,128]{1,0:T(8,128)(2,1)S(1)}, u32[]{:S(2)}, u32[]{:S(2)}) collective-permute-start(bf16[24,128]{1,0:T(8,128)(2,1)S(1)} %reshape.906), channel_id=1, source_target_pairs={{0,0},{1,32},{2,64},{3,96},{4,128},{5,160},{6,192},{7,224},{8,256}... | collective-permute-start | bytes 18440 | tf_op jit(solution)/shard_map/ppermute | solution.py:99
  12.6 31.6 %collective-permute-start = (f32[1,48,128]{2,1,0:T(8,128)S(1)}, f32[1,48,128]{2,1,0:T(8,128)S(1)}, u32[]{:S(2)}, u32[]{:S(2)}) collective-permute-start(f32[1,48,128]{2,1,0:T(8,128)S(1)} %get-tuple-element.5), channel_id=1, source_target_pairs={{0,8},{1,9},{2,10},{3,11},{4,12},{5,13},{6,14},{7,15},{8,0},{9,1},... | collective-permute-start | bytes 73736 | tf_op jit(solution)/shard_map/ppermute | solution.py:32
  18.4 13.1 %collective-permute-start.5 = (bf16[1,24,128]{2,1,0:T(8,128)(2,1)S(1)}, bf16[1,24,128]{2,1,0:T(8,128)(2,1)S(1)}, u32[]{:S(2)}, u32[]{:S(2)}) collective-permute-start(bf16[1,24,128]{2,1,0:T(8,128)(2,1)S(1)} %bitcast.80), channel_id=1, source_target_pairs={{0,128},{16,144},{32,160},{48,176},{64,192},{80,208},{96,224},{112... | collective-permute-start | bytes 18440 | tf_op jit(solution)/shard_map/ppermute | solution.py:32
  31.5 8.3 %collective-permute-start.6 = (bf16[2,24,128]{2,1,0:T(8,128)(2,1)S(1)}, bf16[2,24,128]{2,1,0:T(8,128)(2,1)S(1)}, u32[]{:S(2)}, u32[]{:S(2)}) collective-permute-start(bf16[2,24,128]{2,1,0:T(8,128)(2,1)S(1)} %pad_maximum_fusion.6), channel_id=1, source_target_pairs={{0,64},{16,80},{32,96},{48,112},{64,0},{80,16},{96,32},{112,48},{1... | collective-permute-start | bytes 36872 | tf_op jit(solution)/shard_map/ppermute | solution.py:32
  39.8 12.3 %collective-permute-start.7 = (bf16[4,24,128]{2,1,0:T(8,128)(2,1)S(1)}, bf16[4,24,128]{2,1,0:T(8,128)(2,1)S(1)}, u32[]{:S(2)}, u32[]{:S(2)}) collective-permute-start(bf16[4,24,128]{2,1,0:T(8,128)(2,1)S(1)} %pad_maximum_fusion.5), channel_id=1, source_target_pairs={{0,32},{16,48},{32,0},{48,16},{64,96},{80,112},{96,64},{112,80},{1... | collective-permute-start | bytes 73736 | tf_op jit(solution)/shard_map/ppermute | solution.py:32
  44.1 11.6 %collective-permute-start.1 = (f32[2,48,128]{2,1,0:T(8,128)S(1)}, f32[2,48,128]{2,1,0:T(8,128)S(1)}, u32[]{:S(2)}, u32[]{:S(2)}) collective-permute-start(f32[2,48,128]{2,1,0:T(8,128)S(1)} %pad_maximum_fusion.3), channel_id=1, source_target_pairs={{0,2},{1,3},{2,0},{3,1},{4,6},{5,7},{6,4},{7,5},{8,10},{9,11},{10,... | collective-permute-start | bytes 147464 | tf_op jit(solution)/shard_map/ppermute | solution.py:32
  52.2 9.3 %collective-permute-start.8 = (bf16[8,24,128]{2,1,0:T(8,128)(2,1)S(1)}, bf16[8,24,128]{2,1,0:T(8,128)(2,1)S(1)}, u32[]{:S(2)}, u32[]{:S(2)}) collective-permute-start(bf16[8,24,128]{2,1,0:T(8,128)(2,1)S(1)} %pad_maximum_fusion.4), channel_id=1, source_target_pairs={{0,16},{16,0},{32,48},{48,32},{64,80},{80,64},{96,112},{112,96},{1... | collective-permute-start | bytes 147464 | tf_op jit(solution)/shard_map/ppermute | solution.py:32
  55.8 8.6 %collective-permute-start.2 = (f32[4,48,128]{2,1,0:T(8,128)S(1)}, f32[4,48,128]{2,1,0:T(8,128)S(1)}, u32[]{:S(2)}, u32[]{:S(2)}) collective-permute-start(f32[4,48,128]{2,1,0:T(8,128)S(1)} %pad_maximum_fusion.2), channel_id=1, source_target_pairs={{0,4},{1,5},{2,6},{3,7},{4,0},{5,1},{6,2},{7,3},{8,12},{9,13},{10,... | collective-permute-start | bytes 294920 | tf_op jit(solution)/shard_map/ppermute | solution.py:32
  61.5 8.7 %collective-permute-start.9 = (bf16[16,24,128]{2,1,0:T(8,128)(2,1)S(1)}, bf16[16,24,128]{2,1,0:T(8,128)(2,1)S(1)}, u32[]{:S(2)}, u32[]{:S(2)}) collective-permute-start(bf16[16,24,128]{2,1,0:T(8,128)(2,1)S(1)} %get-tuple-element.16), channel_id=1, source_target_pairs={{0,256},{16,272},{32,288},{48,304},{64,320},{80,336},{96,352},{112... | collective-permute-start | bytes 294920 | tf_op jit(solution)/shard_map/ppermute | solution.py:32
  64.4 9.5 %collective-permute-start.3 = (f32[8,48,128]{2,1,0:T(8,128)S(1)}, f32[8,48,128]{2,1,0:T(8,128)S(1)}, u32[]{:S(2)}, u32[]{:S(2)}) collective-permute-start(f32[8,48,128]{2,1,0:T(8,128)S(1)} %pad_maximum_fusion), channel_id=1, source_target_pairs={{0,1},{1,0},{2,3},{3,2},{4,5},{5,4},{6,7},{7,6},{8,9},{9,8},{10,11... | collective-permute-start | bytes 589832 | tf_op jit(solution)/shard_map/ppermute | solution.py:32
  86.3 1.0 %copy-start = (bf16[1,4,64,3,64]{4,3,2,1,0:T(4,128)(2,1)S(1)}, bf16[1,4,64,3,64]{4,3,2,1,0:T(4,128)(2,1)}, u32[]{:S(2)}) copy-start(bf16[1,4,64,3,64]{4,3,2,1,0:T(4,128)(2,1)} %convert_element_type.128) | copy-start | bytes 294916

commit v3 on v2

--- a/solution.py
+++ b/solution.py
@@ -81,7 +81,10 @@
     proj = jnp.einsum("eip,ep->ei", design, weighted, preferred_element_type=jnp.float32)
 
     payload = jnp.concatenate([node_panel.reshape(-1).astype(jnp.float32), gram.reshape(-1), proj.reshape(-1)])
-    own = doubling_gather(as_lanes(payload, jnp.float32), ("row", "col"), TILE_ORDER)
+    piece = as_lanes(payload, jnp.float32)
+    slots = jnp.zeros((tiles,) + piece.shape, jnp.float32)
+    slots = lax.dynamic_update_slice(slots, piece[None], (lax.axis_index(("row", "col")), 0, 0))
+    own = lax.psum(slots, ("row", "col"))
     own = own.reshape(tiles, -1)
     n_nodes = node_rows * node_cols * comps * width
     n_gram = elements * 144
@@ -103,18 +106,14 @@
     cross = cross.reshape(n_row * node_rows, n_col * node_cols, comps, per_block * width)
 
     rows_of = element_corners(own_nodes.astype(jnp.bfloat16))
-    cols_of = element_corners(cross).astype(jnp.float32)
-    weighted_cols = jnp.sum(grams.transpose(1, 2, 0)[:, :, :, None] * cols_of[None], axis=1)
-    high = weighted_cols.astype(jnp.bfloat16)
-    low = (weighted_cols - high.astype(jnp.float32)).astype(jnp.bfloat16)
-    proj_t = projs.T[:, :, None]
-    proj_high = proj_t.astype(jnp.bfloat16)
-    proj_low = (proj_t - proj_high.astype(jnp.float32)).astype(jnp.bfloat16)
-    operand = jnp.concatenate([high, low, proj_high, proj_low], axis=2)
-    product = jnp.einsum("iep,ieq->pq", rows_of, operand, preferred_element_type=jnp.float32)
-    cols = cross.shape[3]
-    hessian = product[:, :cols] + product[:, cols : 2 * cols]
-    gradient = product[:, 2 * cols] + product[:, 2 * cols + 1]
+    cols_of = element_corners(cross)
+    weighted_rows = jnp.sum(grams.transpose(1, 2, 0)[:, :, :, None] * rows_of.astype(jnp.float32)[:, None], axis=0)
+    high = lax.reduce_precision(weighted_rows, exponent_bits=8, mantissa_bits=7)
+    low = weighted_rows - high
+    stacked = jnp.concatenate([high.astype(jnp.bfloat16), low.astype(jnp.bfloat16)], axis=2)
+    product = jnp.einsum("jep,jeq->pq", stacked, cols_of, preferred_element_type=jnp.float32)
+    hessian = product[:width] + product[width:]
+    gradient = jnp.einsum("iep,ie->p", rows_of.astype(jnp.float32), projs.T, precision=HIGHEST)
     share = width // tiles
     gradient = lax.dynamic_slice(gradient, (lax.axis_index(("row", "col")) * share,), (share,))
     return (hessian, gradient)

time: 92.6 us -> 189 us (2.04)
  waiting for transfers between devices: 2.73 us -> 112 us
  starting transfers between devices: 60.7 us -> 44.5 us
  between operations: 1.19 us -> 14.4 us
  other arithmetic: 12.4 us -> 4.86 us
  local copies, waits for them, and re-layouts: 13.8 us -> 11.7 us
    psum x0 -> x1, waiting for transfers between devices: none -> 99.9 us  [on_device(): own = lax.psum(slots, ('row', 'col'))]
    ppermute x9 -> x5, starting transfers between devices: 54.4 us -> 38.1 us  [doubling_gather(): theirs = lax.ppermute(data, axes, [(i, i ^ bit) for i in range(size)])]
    ppermute x9 -> x5, waiting for transfers between devices: 2.73 us -> 11 us  [doubling_gather(): theirs = lax.ppermute(data, axes, [(i, i ^ bit) for i in range(size)])]
    reduce_sum x1, other arithmetic: 7.29 us -> 0.71 us  [on_device(): jnp.sum(grams.transpose(1, 2, 0)[:, :, :, None] * rows_of.astype(jnp.floa...]
  transfers between devices with their start and end apart: 10 -> 7, of which waited for: 2 -> 7; matrix products, arithmetic and copies ran while one was open for 9% -> 2% of each run, Pallas kernels for 0% -> 0%
where the time goes in v3:
time: 189 us
  waiting for transfers between devices  112 us (59%)
  starting transfers between devices  44.5 us (24%)
  between operations  14.4 us (8%)
  local copies, waits for them, and re-layouts  11.7 us (6%)
  other arithmetic  4.86 us (3%)
    psum x1, waiting for transfers between devices, on_device(): own = lax.psum(slots, ('row', 'col'))  99.9 us
    ppermute x5, starting transfers between devices, doubling_gather(): theirs = lax.ppermute(data, axes, [(i, i ^ bit) for i in range(size)])  38.1 us
    ppermute x5, waiting for transfers between devices, doubling_gather(): theirs = lax.ppermute(data, axes, [(i, i ^ bit) for i in range(size)])  11 us
    ppermute x1, starting transfers between devices, on_device(): lax.ppermute(as_lanes(node_panel.reshape(-1), jnp.bfloat16), ('param', 'r...  6.27 us
  transfers between devices with their start and end apart: 7, of which 7 were waited for; matrix products, arithmetic and copies ran while one was open for 2% of the time, Pallas kernels for 0%

profile of v3, /device:TPU:1, one launch (start us, length us, event | category | flops | bytes accessed | tf_op | source)
XLA Modules:
  0.0 188.7 jit_solution(4385200336250286118)
XLA Ops:
  7.2 0.7 convert_bitcast_fusion
  7.9 0.8 multiply_convert_fusion.1
  8.7 0.1 mul.160
  8.9 0.9 reshape.641
  9.8 0.1 copy.35
  10.2 0.2 copy.36
  10.4 0.1 reshape.632
  10.7 0.2 fusion.50
  10.9 0.1 fusion.51
  11.4 0.9 copy.50
  12.4 6.3 %collective-permute-start = (bf16[24,128]{1,0:T(8,128)(2,1)S(1)}, bf16[24,128]{1,0:T(8,128)(2,1)S(1)}, u32[]{:S(2)}, u32[]{:S(2)}) collective-permute-start(bf16[24,128]{1,0:T(8,128)(2,1)S(1)} %reshape.637), channel_id=1, source_target_pairs={{0,0},{1,32},{2,64},{3,96},{4,128},{5,160},{6,192},{7,224},{8,256}... | collective-permute-start | bytes 18440 | tf_op jit(solution)/shard_map/ppermute | solution.py:102
  18.7 1.2 collective-permute-done
  20.0 21.4 %collective-permute-start.1 = (bf16[1,24,128]{2,1,0:T(8,128)(2,1)S(1)}, bf16[1,24,128]{2,1,0:T(8,128)(2,1)S(1)}, u32[]{:S(2)}, u32[]{:S(2)}) collective-permute-start(bf16[1,24,128]{2,1,0:T(8,128)(2,1)S(1)} %bitcast.74), channel_id=1, source_target_pairs={{0,128},{16,144},{32,160},{48,176},{64,192},{80,208},{96,224},{112... | collective-permute-start | bytes 18440 | tf_op jit(solution)/shard_map/ppermute | solution.py:32
  41.4 1.0 collective-permute-done.1
  42.5 5.2 %collective-permute-start.2 = (bf16[2,24,128]{2,1,0:T(8,128)(2,1)S(1)}, bf16[2,24,128]{2,1,0:T(8,128)(2,1)S(1)}, u32[]{:S(2)}, u32[]{:S(2)}) collective-permute-start(bf16[2,24,128]{2,1,0:T(8,128)(2,1)S(1)} %pad_maximum_fusion.3), channel_id=1, source_target_pairs={{0,64},{16,80},{32,96},{48,112},{64,0},{80,16},{96,32},{112,48},{1... | collective-permute-start | bytes 36872 | tf_op jit(solution)/shard_map/ppermute | solution.py:32
  47.6 3.6 %collective-permute-done.2 = bf16[2,24,128]{2,1,0:T(8,128)(2,1)S(1)} collective-permute-done((bf16[2,24,128]{2,1,0:T(8,128)(2,1)S(1)}, bf16[2,24,128]{2,1,0:T(8,128)(2,1)S(1)}, u32[]{:S(2)}, u32[]{:S(2)}) %collective-permute-start.2) | collective-permute-done | bytes 12320 | tf_op jit(solution)/shard_map/ppermute | solution.py:32
  51.2 3.9 %collective-permute-start.3 = (bf16[4,24,128]{2,1,0:T(8,128)(2,1)S(1)}, bf16[4,24,128]{2,1,0:T(8,128)(2,1)S(1)}, u32[]{:S(2)}, u32[]{:S(2)}) collective-permute-start(bf16[4,24,128]{2,1,0:T(8,128)(2,1)S(1)} %pad_maximum_fusion.2), channel_id=1, source_target_pairs={{0,32},{16,48},{32,0},{48,16},{64,96},{80,112},{96,64},{112,80},{1... | collective-permute-start | bytes 73736 | tf_op jit(solution)/shard_map/ppermute | solution.py:32
  55.1 2.0 %collective-permute-done.3 = bf16[4,24,128]{2,1,0:T(8,128)(2,1)S(1)} collective-permute-done((bf16[4,24,128]{2,1,0:T(8,128)(2,1)S(1)}, bf16[4,24,128]{2,1,0:T(8,128)(2,1)S(1)}, u32[]{:S(2)}, u32[]{:S(2)}) %collective-permute-start.3) | collective-permute-done | bytes 24608 | tf_op jit(solution)/shard_map/ppermute | solution.py:32
  57.1 2.6 %collective-permute-start.4 = (bf16[8,24,128]{2,1,0:T(8,128)(2,1)S(1)}, bf16[8,24,128]{2,1,0:T(8,128)(2,1)S(1)}, u32[]{:S(2)}, u32[]{:S(2)}) collective-permute-start(bf16[8,24,128]{2,1,0:T(8,128)(2,1)S(1)} %pad_maximum_fusion.1), channel_id=1, source_target_pairs={{0,16},{16,0},{32,48},{48,32},{64,80},{80,64},{96,112},{112,96},{1... | collective-permute-start | bytes 147464 | tf_op jit(solution)/shard_map/ppermute | solution.py:32
  59.7 2.5 %collective-permute-done.4 = bf16[8,24,128]{2,1,0:T(8,128)(2,1)S(1)} collective-permute-done((bf16[8,24,128]{2,1,0:T(8,128)(2,1)S(1)}, bf16[8,24,128]{2,1,0:T(8,128)(2,1)S(1)}, u32[]{:S(2)}, u32[]{:S(2)}) %collective-permute-start.4) | collective-permute-done | bytes 49184 | tf_op jit(solution)/shard_map/ppermute | solution.py:32
  62.2 5.1 %collective-permute-start.5 = (bf16[16,24,128]{2,1,0:T(8,128)(2,1)S(1)}, bf16[16,24,128]{2,1,0:T(8,128)(2,1)S(1)}, u32[]{:S(2)}, u32[]{:S(2)}) collective-permute-start(bf16[16,24,128]{2,1,0:T(8,128)(2,1)S(1)} %get-tuple-element.12), channel_id=1, source_target_pairs={{0,256},{16,272},{32,288},{48,304},{64,320},{80,336},{96,352},{112... | collective-permute-start | bytes 294920 | tf_op jit(solution)/shard_map/ppermute | solution.py:32
  67.4 2.0 %collective-permute-done.5 = bf16[16,24,128]{2,1,0:T(8,128)(2,1)S(1)} collective-permute-done((bf16[16,24,128]{2,1,0:T(8,128)(2,1)S(1)}, bf16[16,24,128]{2,1,0:T(8,128)(2,1)S(1)}, u32[]{:S(2)}, u32[]{:S(2)}) %collective-permute-start.5) | collective-permute-done | bytes 98336 | tf_op jit(solution)/shard_map/ppermute | solution.py:32
  69.4 0.6 gather_fusion
  70.0 0.3 gather.7
  70.3 0.3 select_bitcast_fusion
  70.6 0.5 copy.42
  71.1 0.2 reshape.638
  71.3 0.2 stack.40
  71.6 0.1 maximum_bitcast_fusion.1
  71.7 0.9 copy.44
  72.7 99.9 %all-reduce.5.cloned.1.call-done = f32[16,6144]{1,0:T(8,128)} async-done(((f32[16,6144]{1,0:T(8,128)}), f32[16,6144]{1,0:T(8,128)}) %all-reduce.5.cloned.1.call-update) | async-done | bytes 393232 | tf_op jit(solution)/shard_map/psum | solution.py:87
  172.5 0.9 slice.68
  173.5 0.2 convert_element_type.105
  173.7 0.2 convert_element_type.104
  173.9 0.2 slice_bitcast_fusion.2
  174.2 1.1 maximum_bitcast_fusion
  175.2 0.9 copy.40
  176.2 0.5 reshape.636
  176.7 0.1 reshape_transpose_reshape.8
  176.9 0.4 convolution_bitcast_fusion.1
  177.3 1.0 reshape_transpose_reshape.7
  178.3 0.8 copy.39
  179.2 0.7 multiply_reduce_fusion
  179.9 0.2 reduce-precision_convert_fusion
  180.0 0.3 copy-done
  180.3 0.4 convolution_bitcast_fusion
  180.7 0.6 slice_add_fusion
  181.3 0.6 dynamic_slice.3
  (41 shorter events, 1.5 us)
Async XLA Ops:
  7.2 165.4 %all-reduce.5.cloned.1.call-start = ((), (), s32[]{:S(2)}) async-start(), calls=%async_computation | async-start | bytes 786432 | tf_op jit(solution)/shard_map/psum | solution.py:87
  8.7 2.6 %copy-start.1 = (bf16[1,16,3,64]{3,1,2,0:T(8,128)(2,1)S(1)}, bf16[1,16,3,64]{3,1,2,0:T(8,128)(2,1)}, u32[]{:S(2)}) copy-start(bf16[1,16,3,64]{3,1,2,0:T(8,128)(2,1)} %param.9) | copy-start | bytes 18436
  12.4 7.6 %collective-permute-start = (bf16[24,128]{1,0:T(8,128)(2,1)S(1)}, bf16[24,128]{1,0:T(8,128)(2,1)S(1)}, u32[]{:S(2)}, u32[]{:S(2)}) collective-permute-start(bf16[24,128]{1,0:T(8,128)(2,1)S(1)} %reshape.637), channel_id=1, source_target_pairs={{0,0},{1,32},{2,64},{3,96},{4,128},{5,160},{6,192},{7,224},{8,256}... | collective-permute-start | bytes 18440 | tf_op jit(solution)/shard_map/ppermute | solution.py:102
  20.0 22.5 %collective-permute-start.1 = (bf16[1,24,128]{2,1,0:T(8,128)(2,1)S(1)}, bf16[1,24,128]{2,1,0:T(8,128)(2,1)S(1)}, u32[]{:S(2)}, u32[]{:S(2)}) collective-permute-start(bf16[1,24,128]{2,1,0:T(8,128)(2,1)S(1)} %bitcast.74), channel_id=1, source_target_pairs={{0,128},{16,144},{32,160},{48,176},{64,192},{80,208},{96,224},{112... | collective-permute-start | bytes 18440 | tf_op jit(solution)/shard_map/ppermute | solution.py:32
  42.5 8.7 %collective-permute-start.2 = (bf16[2,24,128]{2,1,0:T(8,128)(2,1)S(1)}, bf16[2,24,128]{2,1,0:T(8,128)(2,1)S(1)}, u32[]{:S(2)}, u32[]{:S(2)}) collective-permute-start(bf16[2,24,128]{2,1,0:T(8,128)(2,1)S(1)} %pad_maximum_fusion.3), channel_id=1, source_target_pairs={{0,64},{16,80},{32,96},{48,112},{64,0},{80,16},{96,32},{112,48},{1... | collective-permute-start | bytes 36872 | tf_op jit(solution)/shard_map/ppermute | solution.py:32
  51.2 5.9 %collective-permute-start.3 = (bf16[4,24,128]{2,1,0:T(8,128)(2,1)S(1)}, bf16[4,24,128]{2,1,0:T(8,128)(2,1)S(1)}, u32[]{:S(2)}, u32[]{:S(2)}) collective-permute-start(bf16[4,24,128]{2,1,0:T(8,128)(2,1)S(1)} %pad_maximum_fusion.2), channel_id=1, source_target_pairs={{0,32},{16,48},{32,0},{48,16},{64,96},{80,112},{96,64},{112,80},{1... | collective-permute-start | bytes 73736 | tf_op jit(solution)/shard_map/ppermute | solution.py:32
  57.1 5.1 %collective-permute-start.4 = (bf16[8,24,128]{2,1,0:T(8,128)(2,1)S(1)}, bf16[8,24,128]{2,1,0:T(8,128)(2,1)S(1)}, u32[]{:S(2)}, u32[]{:S(2)}) collective-permute-start(bf16[8,24,128]{2,1,0:T(8,128)(2,1)S(1)} %pad_maximum_fusion.1), channel_id=1, source_target_pairs={{0,16},{16,0},{32,48},{48,32},{64,80},{80,64},{96,112},{112,96},{1... | collective-permute-start | bytes 147464 | tf_op jit(solution)/shard_map/ppermute | solution.py:32
  62.2 7.2 %collective-permute-start.5 = (bf16[16,24,128]{2,1,0:T(8,128)(2,1)S(1)}, bf16[16,24,128]{2,1,0:T(8,128)(2,1)S(1)}, u32[]{:S(2)}, u32[]{:S(2)}) collective-permute-start(bf16[16,24,128]{2,1,0:T(8,128)(2,1)S(1)} %get-tuple-element.12), channel_id=1, source_target_pairs={{0,256},{16,272},{32,288},{48,304},{64,320},{80,336},{96,352},{112... | collective-permute-start | bytes 294920 | tf_op jit(solution)/shard_map/ppermute | solution.py:32
  174.2 2.5 %slice-start = ((f32[16,6144]{1,0:T(8,128)}), f32[16,192]{1,0:T(8,128)S(1)}, s32[]{:S(2)}) async-start(f32[16,6144]{1,0:T(8,128)} %all-reduce.5.cloned.1.call-done), calls=%async_computation.1 | async-start | bytes 32768 | tf_op jit(solution)/shard_map/slice | solution.py:95
  176.2 1.2 slice-start.1
  179.2 1.1 copy-start
Sparse Core Ops, SparseCore 0:
  12.4 160.0 all-reduce.4

commit v4 on v3

--- a/solution.py
+++ b/solution.py
@@ -81,10 +81,7 @@
     proj = jnp.einsum("eip,ep->ei", design, weighted, preferred_element_type=jnp.float32)
 
     payload = jnp.concatenate([node_panel.reshape(-1).astype(jnp.float32), gram.reshape(-1), proj.reshape(-1)])
-    piece = as_lanes(payload, jnp.float32)
-    slots = jnp.zeros((tiles,) + piece.shape, jnp.float32)
-    slots = lax.dynamic_update_slice(slots, piece[None], (lax.axis_index(("row", "col")), 0, 0))
-    own = lax.psum(slots, ("row", "col"))
+    own = doubling_gather(as_lanes(payload, jnp.float32), ("row", "col"), TILE_ORDER)
     own = own.reshape(tiles, -1)
     n_nodes = node_rows * node_cols * comps * width
     n_gram = elements * 144

time: 189 us -> 87.2 us (0.46)
  waiting for transfers between devices: 112 us -> 3.56 us
  starting transfers between devices: 44.5 us -> 64.5 us
  between operations: 14.4 us -> 1.21 us
    psum x1 -> x0, waiting for transfers between devices: 99.9 us -> none  [on_device(): own = lax.psum(slots, ('row', 'col'))]
    ppermute x5 -> x9, starting transfers between devices: 38.1 us -> 58.7 us  [doubling_gather(): theirs = lax.ppermute(data, axes, [(i, i ^ bit) for i in range(size)])]
    ppermute x5 -> x9, waiting for transfers between devices: 11 us -> 2.48 us  [doubling_gather(): theirs = lax.ppermute(data, axes, [(i, i ^ bit) for i in range(size)])]
  transfers between devices with their start and end apart: 7 -> 10, of which waited for: 7 -> 3; matrix products, arithmetic and copies ran while one was open for 2% -> 4% of each run, Pallas kernels for 0% -> 0%
where the time goes in v4:
time: 87.2 us; the launch traced here: 85.9 us
  starting transfers between devices  64.5 us (74%)
  local copies, waits for them, and re-layouts  10.5 us (12%)
  other arithmetic  5.1 us (6%)
  waiting for transfers between devices  3.56 us (4%)
  between operations  1.21 us (1%)
  matrix products  1.08 us (1%)
    ppermute x9, starting transfers between devices, doubling_gather(): theirs = lax.ppermute(data, axes, [(i, i ^ bit) for i in range(size)])  58.7 us
    ppermute x1, starting transfers between devices, on_device(): lax.ppermute(as_lanes(node_panel.reshape(-1), jnp.bfloat16), ('param', 'r...  5.73 us
    ppermute x9, waiting for transfers between devices, doubling_gather(): theirs = lax.ppermute(data, axes, [(i, i ^ bit) for i in range(size)])  2.48 us
    transpose x2, local copies, waits for them, and re-layouts, element_corners(): corners = corners.transpose(0, 3, 1, 2, 4)  1.87 us
  transfers between devices with their start and end apart: 10, of which 3 were waited for; matrix products, arithmetic and copies ran while one was open for 4% of the time, Pallas kernels for 0%

profile of v4, /device:TPU:1, one launch (start us, length us, event | category | flops | bytes accessed | tf_op | source)
XLA Modules:
  0.0 85.9 jit_solution(15183574428357886287)
XLA Ops:
  0.7 0.7 convert_bitcast_fusion
  1.3 0.8 multiply_convert_fusion.1
  2.1 0.1 mul.161
  2.3 0.9 %reshape.904 = f32[3,2,8,16,8]{4,3,2,1,0:T(8,128)S(1)} reshape(bf16[3,2,8,128]{3,2,1,0:T(8,128)(2,1)} %param.5) | data formatting | bytes 36864 | tf_op jit(solution)/shard_map/mul | solution.py:73
  3.2 0.1 copy.35
  3.6 0.2 copy.36
  3.9 0.1 reshape.896
  4.1 0.2 fusion.71
  4.3 0.1 fusion.72
  4.8 5.5 %collective-permute-start = (f32[1,48,128]{2,1,0:T(8,128)S(1)}, f32[1,48,128]{2,1,0:T(8,128)S(1)}, u32[]{:S(2)}, u32[]{:S(2)}) collective-permute-start(f32[1,48,128]{2,1,0:T(8,128)S(1)} %get-tuple-element.3), channel_id=1, source_target_pairs={{0,8},{1,9},{2,10},{3,11},{4,12},{5,13},{6,14},{7,15},{8,0},{9,1},... | collective-permute-start | bytes 73736 | tf_op jit(solution)/shard_map/ppermute | solution.py:32
  10.4 5.7 %collective-permute-start.4 = (bf16[24,128]{1,0:T(8,128)(2,1)S(1)}, bf16[24,128]{1,0:T(8,128)(2,1)S(1)}, u32[]{:S(2)}, u32[]{:S(2)}) collective-permute-start(bf16[24,128]{1,0:T(8,128)(2,1)S(1)} %reshape.900), channel_id=1, source_target_pairs={{0,0},{1,32},{2,64},{3,96},{4,128},{5,160},{6,192},{7,224},{8,256}... | collective-permute-start | bytes 18440 | tf_op jit(solution)/shard_map/ppermute | solution.py:99
  16.3 1.1 %collective-permute-done.4 = bf16[24,128]{1,0:T(8,128)(2,1)S(1)} collective-permute-done((bf16[24,128]{1,0:T(8,128)(2,1)S(1)}, bf16[24,128]{1,0:T(8,128)(2,1)S(1)}, u32[]{:S(2)}, u32[]{:S(2)}) %collective-permute-start.4) | collective-permute-done | bytes 6176 | tf_op jit(solution)/shard_map/ppermute | solution.py:99
  17.4 21.1 %collective-permute-start.5 = (bf16[1,24,128]{2,1,0:T(8,128)(2,1)S(1)}, bf16[1,24,128]{2,1,0:T(8,128)(2,1)S(1)}, u32[]{:S(2)}, u32[]{:S(2)}) collective-permute-start(bf16[1,24,128]{2,1,0:T(8,128)(2,1)S(1)} %bitcast.73), channel_id=1, source_target_pairs={{0,128},{16,144},{32,160},{48,176},{64,192},{80,208},{96,224},{112... | collective-permute-start | bytes 18440 | tf_op jit(solution)/shard_map/ppermute | solution.py:32
  38.6 1.0 %collective-permute-done.5 = bf16[1,24,128]{2,1,0:T(8,128)(2,1)S(1)} collective-permute-done((bf16[1,24,128]{2,1,0:T(8,128)(2,1)S(1)}, bf16[1,24,128]{2,1,0:T(8,128)(2,1)S(1)}, u32[]{:S(2)}, u32[]{:S(2)}) %collective-permute-start.5) | collective-permute-done | bytes 6176 | tf_op jit(solution)/shard_map/ppermute | solution.py:32
  39.6 5.2 %collective-permute-start.6 = (bf16[2,24,128]{2,1,0:T(8,128)(2,1)S(1)}, bf16[2,24,128]{2,1,0:T(8,128)(2,1)S(1)}, u32[]{:S(2)}, u32[]{:S(2)}) collective-permute-start(bf16[2,24,128]{2,1,0:T(8,128)(2,1)S(1)} %pad_maximum_fusion.6), channel_id=1, source_target_pairs={{0,64},{16,80},{32,96},{48,112},{64,0},{80,16},{96,32},{112,48},{1... | collective-permute-start | bytes 36872 | tf_op jit(solution)/shard_map/ppermute | solution.py:32
  44.8 3.6 %collective-permute-start.1 = (f32[2,48,128]{2,1,0:T(8,128)S(1)}, f32[2,48,128]{2,1,0:T(8,128)S(1)}, u32[]{:S(2)}, u32[]{:S(2)}) collective-permute-start(f32[2,48,128]{2,1,0:T(8,128)S(1)} %pad_maximum_fusion.3), channel_id=1, source_target_pairs={{0,2},{1,3},{2,0},{3,1},{4,6},{5,7},{6,4},{7,5},{8,10},{9,11},{10,... | collective-permute-start | bytes 147464 | tf_op jit(solution)/shard_map/ppermute | solution.py:32
  48.5 4.5 %collective-permute-start.7 = (bf16[4,24,128]{2,1,0:T(8,128)(2,1)S(1)}, bf16[4,24,128]{2,1,0:T(8,128)(2,1)S(1)}, u32[]{:S(2)}, u32[]{:S(2)}) collective-permute-start(bf16[4,24,128]{2,1,0:T(8,128)(2,1)S(1)} %pad_maximum_fusion.5), channel_id=1, source_target_pairs={{0,32},{16,48},{32,0},{48,16},{64,96},{80,112},{96,64},{112,80},{1... | collective-permute-start | bytes 73736 | tf_op jit(solution)/shard_map/ppermute | solution.py:32
  53.0 1.5 %collective-permute-done.7 = bf16[4,24,128]{2,1,0:T(8,128)(2,1)S(1)} collective-permute-done((bf16[4,24,128]{2,1,0:T(8,128)(2,1)S(1)}, bf16[4,24,128]{2,1,0:T(8,128)(2,1)S(1)}, u32[]{:S(2)}, u32[]{:S(2)}) %collective-permute-start.7) | collective-permute-done | bytes 24608 | tf_op jit(solution)/shard_map/ppermute | solution.py:32
  54.5 2.6 %collective-permute-start.8 = (bf16[8,24,128]{2,1,0:T(8,128)(2,1)S(1)}, bf16[8,24,128]{2,1,0:T(8,128)(2,1)S(1)}, u32[]{:S(2)}, u32[]{:S(2)}) collective-permute-start(bf16[8,24,128]{2,1,0:T(8,128)(2,1)S(1)} %pad_maximum_fusion.4), channel_id=1, source_target_pairs={{0,16},{16,0},{32,48},{48,32},{64,80},{80,64},{96,112},{112,96},{1... | collective-permute-start | bytes 147464 | tf_op jit(solution)/shard_map/ppermute | solution.py:32
  57.2 5.9 %collective-permute-start.2 = (f32[4,48,128]{2,1,0:T(8,128)S(1)}, f32[4,48,128]{2,1,0:T(8,128)S(1)}, u32[]{:S(2)}, u32[]{:S(2)}) collective-permute-start(f32[4,48,128]{2,1,0:T(8,128)S(1)} %pad_maximum_fusion.2), channel_id=1, source_target_pairs={{0,4},{1,5},{2,6},{3,7},{4,0},{5,1},{6,2},{7,3},{8,12},{9,13},{10,... | collective-permute-start | bytes 294920 | tf_op jit(solution)/shard_map/ppermute | solution.py:32
  63.1 3.2 %collective-permute-start.9 = (bf16[16,24,128]{2,1,0:T(8,128)(2,1)S(1)}, bf16[16,24,128]{2,1,0:T(8,128)(2,1)S(1)}, u32[]{:S(2)}, u32[]{:S(2)}) collective-permute-start(bf16[16,24,128]{2,1,0:T(8,128)(2,1)S(1)} %get-tuple-element.14), channel_id=1, source_target_pairs={{0,256},{16,272},{32,288},{48,304},{64,320},{80,336},{96,352},{112... | collective-permute-start | bytes 294920 | tf_op jit(solution)/shard_map/ppermute | solution.py:32
  66.4 7.1 %collective-permute-start.3 = (f32[8,48,128]{2,1,0:T(8,128)S(1)}, f32[8,48,128]{2,1,0:T(8,128)S(1)}, u32[]{:S(2)}, u32[]{:S(2)}) collective-permute-start(f32[8,48,128]{2,1,0:T(8,128)S(1)} %pad_maximum_fusion), channel_id=1, source_target_pairs={{0,1},{1,0},{2,3},{3,2},{4,5},{5,4},{6,7},{7,6},{8,9},{9,8},{10,11... | collective-permute-start | bytes 589832 | tf_op jit(solution)/shard_map/ppermute | solution.py:32
  73.5 0.6 gather_fusion.1
  74.1 0.3 gather.15
  74.4 0.3 select_bitcast_fusion
  74.7 0.5 copy.42
  75.2 0.2 reshape.901
  75.4 0.2 stack.40
  75.7 0.1 maximum_bitcast_fusion.1
  75.8 0.9 %copy.44 = bf16[4,3,4,64,128]{4,3,2,1,0:T(8,128)(2,1)} copy(bf16[4,3,4,64,128]{4,3,1,2,0:T(8,128)(2,1)S(1)} %maximum_bitcast_fusion.1) | data formatting | bytes 1572864 | tf_op jit(solution)/shard_map/transpose | solution.py:52
  76.8 0.6 gather_fusion
  77.4 0.1 bitcast_select_fusion
  77.6 0.2 convert_element_type.105
  77.8 0.2 convert_element_type.104
  78.0 0.2 slice_bitcast_fusion.2
  78.3 1.1 %maximum_bitcast_fusion = bf16[4,3,4,64,64]{4,1,3,2,0:T(4,128)(2,1)S(1)} fusion(bf16[1,4,64,3,64]{4,3,2,1,0:T(4,128)(2,1)S(1)} %get-tuple-element.10, bf16[1,4,64,3,64]{4,3,2,1,0:T(4,128)(2,1)S(1)} %get-tuple-element.9, bf16[1,4,64,3,64]{4,3,2,1,0:T(4,128)(2,1)S(1)} %get-tuple-element.8, bf16[1,4,64,3,64]{4,3,2,1,0:T(4,128)(2,1)S(1)} %convert_element_type.104), kind=kLoop, calls=%fused_computation.7 | loop fusion | flops 589824 | bytes 786432 | tf_op jit(solution)/shard_map/transpose | solution.py:52
  79.3 0.9 %copy.40 = bf16[4,3,4,64,64]{3,2,4,1,0:T(4,128)(2,1)S(1)} copy(bf16[4,3,4,64,64]{4,1,3,2,0:T(4,128)(2,1)S(1)} %maximum_bitcast_fusion) | data formatting | bytes 786432 | tf_op jit(solution)/shard_map/transpose | solution.py:52
  80.3 0.5 reshape.899
  80.7 0.1 reshape_transpose_reshape.8
  81.0 0.4 convolution_bitcast_fusion.1
  81.4 1.0 %reshape_transpose_reshape.7 = f32[256,12,12]{2,1,0:T(8,128)S(1)} reshape(f32[16,2304]{1,0:T(8,128)S(1)} %slice-done) | data formatting | bytes 294912 | tf_op jit(solution)/shard_map/reshape;transpose;reshape | solution.py:91
  82.4 0.8 copy.39
  83.2 0.7 multiply_reduce_fusion
  84.0 0.2 reduce-precision_convert_fusion
  84.1 0.3 copy-done.1
  84.4 0.4 convolution_bitcast_fusion
  84.7 0.6 slice_add_fusion
  85.4 0.6 dynamic_slice.3
  (57 shorter events, 1.5 us)
Async XLA Ops:
  2.1 2.6 %copy-start.2 = (bf16[1,16,3,64]{3,1,2,0:T(8,128)(2,1)S(1)}, bf16[1,16,3,64]{3,1,2,0:T(8,128)(2,1)}, u32[]{:S(2)}) copy-start(bf16[1,16,3,64]{3,1,2,0:T(8,128)(2,1)} %param.9) | copy-start | bytes 18436
  4.8 40.0 %collective-permute-start = (f32[1,48,128]{2,1,0:T(8,128)S(1)}, f32[1,48,128]{2,1,0:T(8,128)S(1)}, u32[]{:S(2)}, u32[]{:S(2)}) collective-permute-start(f32[1,48,128]{2,1,0:T(8,128)S(1)} %get-tuple-element.3), channel_id=1, source_target_pairs={{0,8},{1,9},{2,10},{3,11},{4,12},{5,13},{6,14},{7,15},{8,0},{9,1},... | collective-permute-start | bytes 73736 | tf_op jit(solution)/shard_map/ppermute | solution.py:32
  10.4 7.0 %collective-permute-start.4 = (bf16[24,128]{1,0:T(8,128)(2,1)S(1)}, bf16[24,128]{1,0:T(8,128)(2,1)S(1)}, u32[]{:S(2)}, u32[]{:S(2)}) collective-permute-start(bf16[24,128]{1,0:T(8,128)(2,1)S(1)} %reshape.900), channel_id=1, source_target_pairs={{0,0},{1,32},{2,64},{3,96},{4,128},{5,160},{6,192},{7,224},{8,256}... | collective-permute-start | bytes 18440 | tf_op jit(solution)/shard_map/ppermute | solution.py:99
  17.4 22.2 %collective-permute-start.5 = (bf16[1,24,128]{2,1,0:T(8,128)(2,1)S(1)}, bf16[1,24,128]{2,1,0:T(8,128)(2,1)S(1)}, u32[]{:S(2)}, u32[]{:S(2)}) collective-permute-start(bf16[1,24,128]{2,1,0:T(8,128)(2,1)S(1)} %bitcast.73), channel_id=1, source_target_pairs={{0,128},{16,144},{32,160},{48,176},{64,192},{80,208},{96,224},{112... | collective-permute-start | bytes 18440 | tf_op jit(solution)/shard_map/ppermute | solution.py:32
  39.6 8.9 %collective-permute-start.6 = (bf16[2,24,128]{2,1,0:T(8,128)(2,1)S(1)}, bf16[2,24,128]{2,1,0:T(8,128)(2,1)S(1)}, u32[]{:S(2)}, u32[]{:S(2)}) collective-permute-start(bf16[2,24,128]{2,1,0:T(8,128)(2,1)S(1)} %pad_maximum_fusion.6), channel_id=1, source_target_pairs={{0,64},{16,80},{32,96},{48,112},{64,0},{80,16},{96,32},{112,48},{1... | collective-permute-start | bytes 36872 | tf_op jit(solution)/shard_map/ppermute | solution.py:32
  44.8 12.4 %collective-permute-start.1 = (f32[2,48,128]{2,1,0:T(8,128)S(1)}, f32[2,48,128]{2,1,0:T(8,128)S(1)}, u32[]{:S(2)}, u32[]{:S(2)}) collective-permute-start(f32[2,48,128]{2,1,0:T(8,128)S(1)} %pad_maximum_fusion.3), channel_id=1, source_target_pairs={{0,2},{1,3},{2,0},{3,1},{4,6},{5,7},{6,4},{7,5},{8,10},{9,11},{10,... | collective-permute-start | bytes 147464 | tf_op jit(solution)/shard_map/ppermute | solution.py:32
  48.5 6.0 %collective-permute-start.7 = (bf16[4,24,128]{2,1,0:T(8,128)(2,1)S(1)}, bf16[4,24,128]{2,1,0:T(8,128)(2,1)S(1)}, u32[]{:S(2)}, u32[]{:S(2)}) collective-permute-start(bf16[4,24,128]{2,1,0:T(8,128)(2,1)S(1)} %pad_maximum_fusion.5), channel_id=1, source_target_pairs={{0,32},{16,48},{32,0},{48,16},{64,96},{80,112},{96,64},{112,80},{1... | collective-permute-start | bytes 73736 | tf_op jit(solution)/shard_map/ppermute | solution.py:32
  54.5 8.6 %collective-permute-start.8 = (bf16[8,24,128]{2,1,0:T(8,128)(2,1)S(1)}, bf16[8,24,128]{2,1,0:T(8,128)(2,1)S(1)}, u32[]{:S(2)}, u32[]{:S(2)}) collective-permute-start(bf16[8,24,128]{2,1,0:T(8,128)(2,1)S(1)} %pad_maximum_fusion.4), channel_id=1, source_target_pairs={{0,16},{16,0},{32,48},{48,32},{64,80},{80,64},{96,112},{112,96},{1... | collective-permute-start | bytes 147464 | tf_op jit(solution)/shard_map/ppermute | solution.py:32
  57.2 9.1 %collective-permute-start.2 = (f32[4,48,128]{2,1,0:T(8,128)S(1)}, f32[4,48,128]{2,1,0:T(8,128)S(1)}, u32[]{:S(2)}, u32[]{:S(2)}) collective-permute-start(f32[4,48,128]{2,1,0:T(8,128)S(1)} %pad_maximum_fusion.2), channel_id=1, source_target_pairs={{0,4},{1,5},{2,6},{3,7},{4,0},{5,1},{6,2},{7,3},{8,12},{9,13},{10,... | collective-permute-start | bytes 294920 | tf_op jit(solution)/shard_map/ppermute | solution.py:32
  63.1 10.3 %collective-permute-start.9 = (bf16[16,24,128]{2,1,0:T(8,128)(2,1)S(1)}, bf16[16,24,128]{2,1,0:T(8,128)(2,1)S(1)}, u32[]{:S(2)}, u32[]{:S(2)}) collective-permute-start(bf16[16,24,128]{2,1,0:T(8,128)(2,1)S(1)} %get-tuple-element.14), channel_id=1, source_target_pairs={{0,256},{16,272},{32,288},{48,304},{64,320},{80,336},{96,352},{112... | collective-permute-start | bytes 294920 | tf_op jit(solution)/shard_map/ppermute | solution.py:32
  66.4 10.4 %collective-permute-start.3 = (f32[8,48,128]{2,1,0:T(8,128)S(1)}, f32[8,48,128]{2,1,0:T(8,128)S(1)}, u32[]{:S(2)}, u32[]{:S(2)}) collective-permute-start(f32[8,48,128]{2,1,0:T(8,128)S(1)} %pad_maximum_fusion), channel_id=1, source_target_pairs={{0,1},{1,0},{2,3},{3,2},{4,5},{5,4},{6,7},{7,6},{8,9},{9,8},{10,11... | collective-permute-start | bytes 589832 | tf_op jit(solution)/shard_map/ppermute | solution.py:32
  77.5 1.8 %copy-start = (f32[16,6144]{1,0:T(8,128)}, f32[16,6144]{1,0:T(8,128)S(1)}, u32[]{:S(2)}) copy-start(f32[16,6144]{1,0:T(8,128)S(1)} %bitcast_select_fusion) | copy-start | bytes 1179652
  80.3 1.2 %slice-start = ((f32[16,6144]{1,0:T(8,128)}), f32[16,2304]{1,0:T(8,128)S(1)}, s32[]{:S(2)}) async-start(f32[16,6144]{1,0:T(8,128)} %copy-done), calls=%async_computation | async-start | bytes 294912 | tf_op jit(solution)/shard_map/slice | solution.py:90
  83.2 1.1 %copy-start.1 = (bf16[4,3,4,64,128]{4,3,2,1,0:T(8,128)(2,1)S(1)}, bf16[4,3,4,64,128]{4,3,2,1,0:T(8,128)(2,1)}, u32[]{:S(2)}) copy-start(bf16[4,3,4,64,128]{4,3,2,1,0:T(8,128)(2,1)} %copy.44) | copy-start | bytes 2359300

commit v5 on v4

--- a/solution.py
+++ b/solution.py
@@ -9,7 +9,6 @@
 HIGHEST = lax.Precision.HIGHEST
 
 PARAM_ORDER = (8, 4, 2, 1, 16)
-TILE_ORDER = (8, 2, 4, 1)
 
 
 def corner_shapes(rows, cols):
@@ -80,29 +79,35 @@
     gram = jnp.einsum("eip,ejp->eij", design, design, preferred_element_type=jnp.float32)
     proj = jnp.einsum("eip,ep->ei", design, weighted, preferred_element_type=jnp.float32)
 
-    payload = jnp.concatenate([node_panel.reshape(-1).astype(jnp.float32), gram.reshape(-1), proj.reshape(-1)])
-    own = doubling_gather(as_lanes(payload, jnp.float32), ("row", "col"), TILE_ORDER)
-    own = own.reshape(tiles, -1)
     n_nodes = node_rows * node_cols * comps * width
     n_gram = elements * 144
-    own_nodes = own[:, :n_nodes].reshape(n_row, n_col, node_rows, node_cols, comps, width)
-    own_nodes = own_nodes.transpose(0, 2, 1, 3, 4, 5).reshape(n_row * node_rows, n_col * node_cols, comps, width)
-    grams = own[:, n_nodes : n_nodes + n_gram].reshape(n_row, n_col, elem_rows, elem_cols, 12, 12)
-    grams = grams.transpose(0, 2, 1, 3, 4, 5).reshape(-1, 12, 12)
-    projs = own[:, n_nodes + n_gram : n_nodes + n_gram + elements * 12]
-    projs = projs.reshape(n_row, n_col, elem_rows, elem_cols, 12).transpose(0, 2, 1, 3, 4).reshape(-1, 12)
-
+    payload = jnp.concatenate([node_panel.reshape(-1).astype(jnp.float32), gram.reshape(-1), proj.reshape(-1)])
     route = []
     for b in range(n_param):
         for t in range(tiles):
             route.append((b * tiles + t, (per_block * t + b % per_block) * tiles + b // per_block))
-    moved = lax.ppermute(as_lanes(node_panel.reshape(-1), jnp.bfloat16), ("param", "row", "col"), route)
-    cross = doubling_gather(moved, "param", PARAM_ORDER).reshape(n_param, -1)[:, : node_rows * node_cols * comps * width]
+    moved = lax.ppermute(as_lanes(payload, jnp.float32), ("param", "row", "col"), route)
+    gathered = doubling_gather(moved, "param", PARAM_ORDER).reshape(tiles, per_block, -1)
+    cross = gathered[:, :, :n_nodes].astype(jnp.bfloat16)
     cross = cross.reshape(n_row, n_col, per_block, node_rows, node_cols, comps, width)
     cross = cross.transpose(0, 3, 1, 4, 5, 2, 6)
     cross = cross.reshape(n_row * node_rows, n_col * node_cols, comps, per_block * width)
+    grams = gathered[:, 0, n_nodes : n_nodes + n_gram].reshape(n_row, n_col, elem_rows, elem_cols, 12, 12)
+    grams = grams.transpose(0, 2, 1, 3, 4, 5).reshape(-1, 12, 12)
+    projs = gathered[:, 0, n_nodes + n_gram : n_nodes + n_gram + elements * 12]
+    projs = projs.reshape(n_row, n_col, elem_rows, elem_cols, 12).transpose(0, 2, 1, 3, 4).reshape(-1, 12)
 
-    rows_of = element_corners(own_nodes.astype(jnp.bfloat16))
+    half = lax.axis_index("param") % per_block
+    mine = lax.dynamic_index_in_dim(gathered[:, :, :n_nodes], half, axis=1, keepdims=False)
+    back = []
+    for x in range(n_param):
+        for t in range(tiles):
+            back.append((x * tiles + t, (per_block * t + x % per_block) * tiles + x // per_block))
+    own = lax.ppermute(as_lanes(mine.reshape(-1), jnp.bfloat16), ("param", "row", "col"), back)
+    own_nodes = own.reshape(-1)[: tiles * n_nodes].reshape(n_row, n_col, node_rows, node_cols, comps, width)
+    own_nodes = own_nodes.transpose(0, 2, 1, 3, 4, 5).reshape(n_row * node_rows, n_col * node_cols, comps, width)
+
+    rows_of = element_corners(own_nodes)
     cols_of = element_corners(cross)
     weighted_rows = jnp.sum(grams.transpose(1, 2, 0)[:, :, :, None] * rows_of.astype(jnp.float32)[:, None], axis=0)
     high = lax.reduce_precision(weighted_rows, exponent_bits=8, mantissa_bits=7)

time: 87.2 us -> 107 us (1.23)
  the two profiles are of different devices: /device:TPU:1 before, /device:TPU:282 now
where the time goes in v5:
time: 107 us; the launch traced here: 106 us
  waiting for transfers between devices  71.8 us (67%)
  starting transfers between devices  17 us (16%)
  local copies, waits for them, and re-layouts  10.5 us (10%)
  other arithmetic  4.98 us (5%)
  between operations  1.08 us (1%)
  matrix products  1.07 us (1%)
    ppermute x5, waiting for transfers between devices, doubling_gather(): theirs = lax.ppermute(data, axes, [(i, i ^ bit) for i in range(size)])  45 us
    ppermute x1, waiting for transfers between devices, on_device(): lax.ppermute(as_lanes(mine.reshape(-1), jnp.bfloat16), ('param', 'row', '...  17.6 us
    ppermute x5, starting transfers between devices, doubling_gather(): theirs = lax.ppermute(data, axes, [(i, i ^ bit) for i in range(size)])  9.58 us
    ppermute x1, waiting for transfers between devices, on_device(): lax.ppermute(as_lanes(payload, jnp.float32), ('param', 'row', 'col'), route)  9.19 us
    ppermute x1, starting transfers between devices, on_device(): lax.ppermute(as_lanes(payload, jnp.float32), ('param', 'row', 'col'), route)  5.5 us
  transfers between devices with their start and end apart: 7, of which 7 were waited for; matrix products, arithmetic and copies ran while one was open for 2% of the time, Pallas kernels for 0%

profile of v5, /device:TPU:282, one launch (start us, length us, event | category | flops | bytes accessed | tf_op | source)
XLA Modules:
  0.0 106.4 jit_solution(16975958924165913821)
XLA Ops:
  0.7 0.7 convert_bitcast_fusion
  1.3 0.8 multiply_convert_fusion.1
  2.3 0.9 reshape.625
  3.2 0.1 copy.47
  3.6 0.2 copy.48
  3.9 0.1 reshape.616
  4.1 0.2 fusion.46
  4.3 0.1 fusion.47
  4.8 5.5 %collective-permute-start = (f32[48,128]{1,0:T(8,128)S(1)}, f32[48,128]{1,0:T(8,128)S(1)}, u32[]{:S(2)}, u32[]{:S(2)}) collective-permute-start(f32[48,128]{1,0:T(8,128)S(1)} %fusion.7), channel_id=1, source_target_pairs={{0,0},{1,32},{2,64},{3,96},{4,128},{5,160},{6,192},{7,224},{8,256}... | collective-permute-start | bytes 73736 | tf_op jit(solution)/shard_map/ppermute | solution.py:89
  10.3 9.2 %collective-permute-done = f32[48,128]{1,0:T(8,128)S(1)} collective-permute-done((f32[48,128]{1,0:T(8,128)S(1)}, f32[48,128]{1,0:T(8,128)S(1)}, u32[]{:S(2)}, u32[]{:S(2)}) %collective-permute-start) | collective-permute-done | bytes 24608 | tf_op jit(solution)/shard_map/ppermute | solution.py:89
  19.5 1.9 %collective-permute-start.1 = (f32[1,48,128]{2,1,0:T(8,128)S(1)}, f32[1,48,128]{2,1,0:T(8,128)S(1)}, u32[]{:S(2)}, u32[]{:S(2)}) collective-permute-start(f32[1,48,128]{2,1,0:T(8,128)S(1)} %bitcast.66), channel_id=1, source_target_pairs={{0,128},{16,144},{32,160},{48,176},{64,192},{80,208},{96,224},{112... | collective-permute-start | bytes 73736 | tf_op jit(solution)/shard_map/ppermute | solution.py:31
  21.4 12.6 %collective-permute-done.1 = f32[1,48,128]{2,1,0:T(8,128)S(1)} collective-permute-done((f32[1,48,128]{2,1,0:T(8,128)S(1)}, f32[1,48,128]{2,1,0:T(8,128)S(1)}, u32[]{:S(2)}, u32[]{:S(2)}) %collective-permute-start.1) | collective-permute-done | bytes 24608 | tf_op jit(solution)/shard_map/ppermute | solution.py:31
  34.0 1.9 %collective-permute-start.2 = (f32[2,48,128]{2,1,0:T(8,128)S(1)}, f32[2,48,128]{2,1,0:T(8,128)S(1)}, u32[]{:S(2)}, u32[]{:S(2)}) collective-permute-start(f32[2,48,128]{2,1,0:T(8,128)S(1)} %pad_maximum_fusion.3), channel_id=1, source_target_pairs={{0,64},{16,80},{32,96},{48,112},{64,0},{80,16},{96,32},{112,48},{1... | collective-permute-start | bytes 147464 | tf_op jit(solution)/shard_map/ppermute | solution.py:31
  35.9 9.1 %collective-permute-done.2 = f32[2,48,128]{2,1,0:T(8,128)S(1)} collective-permute-done((f32[2,48,128]{2,1,0:T(8,128)S(1)}, f32[2,48,128]{2,1,0:T(8,128)S(1)}, u32[]{:S(2)}, u32[]{:S(2)}) %collective-permute-start.2) | collective-permute-done | bytes 49184 | tf_op jit(solution)/shard_map/ppermute | solution.py:31
  45.1 1.9 %collective-permute-start.3 = (f32[4,48,128]{2,1,0:T(8,128)S(1)}, f32[4,48,128]{2,1,0:T(8,128)S(1)}, u32[]{:S(2)}, u32[]{:S(2)}) collective-permute-start(f32[4,48,128]{2,1,0:T(8,128)S(1)} %pad_maximum_fusion.2), channel_id=1, source_target_pairs={{0,32},{16,48},{32,0},{48,16},{64,96},{80,112},{96,64},{112,80},{1... | collective-permute-start | bytes 294920 | tf_op jit(solution)/shard_map/ppermute | solution.py:31
  47.0 6.6 %collective-permute-done.3 = f32[4,48,128]{2,1,0:T(8,128)S(1)} collective-permute-done((f32[4,48,128]{2,1,0:T(8,128)S(1)}, f32[4,48,128]{2,1,0:T(8,128)S(1)}, u32[]{:S(2)}, u32[]{:S(2)}) %collective-permute-start.3) | collective-permute-done | bytes 98336 | tf_op jit(solution)/shard_map/ppermute | solution.py:31
  53.6 1.9 %collective-permute-start.4 = (f32[8,48,128]{2,1,0:T(8,128)S(1)}, f32[8,48,128]{2,1,0:T(8,128)S(1)}, u32[]{:S(2)}, u32[]{:S(2)}) collective-permute-start(f32[8,48,128]{2,1,0:T(8,128)S(1)} %pad_maximum_fusion), channel_id=1, source_target_pairs={{0,16},{16,0},{32,48},{48,32},{64,80},{80,64},{96,112},{112,96},{1... | collective-permute-start | bytes 589832 | tf_op jit(solution)/shard_map/ppermute | solution.py:31
  55.6 6.8 %collective-permute-done.4 = f32[8,48,128]{2,1,0:T(8,128)S(1)} collective-permute-done((f32[8,48,128]{2,1,0:T(8,128)S(1)}, f32[8,48,128]{2,1,0:T(8,128)S(1)}, u32[]{:S(2)}, u32[]{:S(2)}) %collective-permute-start.4) | collective-permute-done | bytes 196640 | tf_op jit(solution)/shard_map/ppermute | solution.py:31
  62.4 1.9 %collective-permute-start.5 = (f32[16,48,128]{2,1,0:T(8,128)S(1)}, f32[16,48,128]{2,1,0:T(8,128)S(1)}, u32[]{:S(2)}, u32[]{:S(2)}) collective-permute-start(f32[16,48,128]{2,1,0:T(8,128)S(1)} %get-tuple-element.14), channel_id=1, source_target_pairs={{0,256},{16,272},{32,288},{48,304},{64,320},{80,336},{96,352},{112... | collective-permute-start | bytes 1179656 | tf_op jit(solution)/shard_map/ppermute | solution.py:31
  64.5 10.0 %collective-permute-done.5 = f32[16,48,128]{2,1,0:T(8,128)S(1)} collective-permute-done((f32[16,48,128]{2,1,0:T(8,128)S(1)}, f32[16,48,128]{2,1,0:T(8,128)S(1)}, u32[]{:S(2)}, u32[]{:S(2)}) %collective-permute-start.5) | collective-permute-done | bytes 393248 | tf_op jit(solution)/shard_map/ppermute | solution.py:31
  74.5 0.6 gather_fusion
  75.1 0.4 gather.7
  75.6 0.5 broadcast_select_fusion
  76.0 0.1 slice.74
  76.2 0.4 slice_reduce_fusion
  76.6 0.4 reshape.621
  77.1 0.5 copy.54
  77.5 0.2 reshape.622
  77.8 0.2 stack.43
  78.0 0.6 convert_reduce_fusion
  78.6 1.9 %collective-permute-start.6 = (bf16[384,128]{1,0:T(8,128)(2,1)S(1)}, bf16[384,128]{1,0:T(8,128)(2,1)S(1)}, u32[]{:S(2)}, u32[]{:S(2)}) collective-permute-start(bf16[384,128]{1,0:T(8,128)(2,1)S(1)} %convert_element_type.98), channel_id=1, source_target_pairs={{0,0},{1,32},{2,64},{3,96},{4,128},{5,160},{6,192},{7,224},{8,256}... | collective-permute-start | bytes 294920 | tf_op jit(solution)/shard_map/ppermute | solution.py:106
  80.5 0.1 reshape_transpose_reshape_squeeze.7
  80.7 0.9 reshape_transpose_reshape_squeeze.6
  81.7 0.8 copy.51
  82.6 0.1 maximum_bitcast_fusion.1
  82.8 17.6 %collective-permute-done.6 = bf16[384,128]{1,0:T(8,128)(2,1)S(1)} collective-permute-done((bf16[384,128]{1,0:T(8,128)(2,1)S(1)}, bf16[384,128]{1,0:T(8,128)(2,1)S(1)}, u32[]{:S(2)}, u32[]{:S(2)}) %collective-permute-start.6) | collective-permute-done | bytes 98336 | tf_op jit(solution)/shard_map/ppermute | solution.py:106
  100.4 0.2 reshape_transpose_reshape_reshape.3
  100.6 0.2 slice_bitcast_fusion.2
  100.8 0.2 stack.38
  101.0 1.1 maximum_bitcast_fusion
  102.1 0.9 copy.52
  103.0 0.5 reshape.620
  103.6 0.4 convolution_bitcast_fusion.1
  104.0 0.7 multiply_reduce_fusion
  104.7 0.2 reduce-precision_convert_fusion
  104.9 0.4 convolution_bitcast_fusion
  105.2 0.6 slice_add_fusion
  105.8 0.6 dynamic_slice.8
  (37 shorter events, 1.6 us)
Async XLA Ops:
  2.1 2.6 %copy-start = (bf16[1,16,3,64]{3,1,2,0:T(8,128)(2,1)S(1)}, bf16[1,16,3,64]{3,1,2,0:T(8,128)(2,1)}, u32[]{:S(2)}) copy-start(bf16[1,16,3,64]{3,1,2,0:T(8,128)(2,1)} %param.9) | copy-start | bytes 18436
  4.8 14.7 %collective-permute-start = (f32[48,128]{1,0:T(8,128)S(1)}, f32[48,128]{1,0:T(8,128)S(1)}, u32[]{:S(2)}, u32[]{:S(2)}) collective-permute-start(f32[48,128]{1,0:T(8,128)S(1)} %fusion.7), channel_id=1, source_target_pairs={{0,0},{1,32},{2,64},{3,96},{4,128},{5,160},{6,192},{7,224},{8,256}... | collective-permute-start | bytes 73736 | tf_op jit(solution)/shard_map/ppermute | solution.py:89
  19.5 14.5 %collective-permute-start.1 = (f32[1,48,128]{2,1,0:T(8,128)S(1)}, f32[1,48,128]{2,1,0:T(8,128)S(1)}, u32[]{:S(2)}, u32[]{:S(2)}) collective-permute-start(f32[1,48,128]{2,1,0:T(8,128)S(1)} %bitcast.66), channel_id=1, source_target_pairs={{0,128},{16,144},{32,160},{48,176},{64,192},{80,208},{96,224},{112... | collective-permute-start | bytes 73736 | tf_op jit(solution)/shard_map/ppermute | solution.py:31
  34.0 11.1 %collective-permute-start.2 = (f32[2,48,128]{2,1,0:T(8,128)S(1)}, f32[2,48,128]{2,1,0:T(8,128)S(1)}, u32[]{:S(2)}, u32[]{:S(2)}) collective-permute-start(f32[2,48,128]{2,1,0:T(8,128)S(1)} %pad_maximum_fusion.3), channel_id=1, source_target_pairs={{0,64},{16,80},{32,96},{48,112},{64,0},{80,16},{96,32},{112,48},{1... | collective-permute-start | bytes 147464 | tf_op jit(solution)/shard_map/ppermute | solution.py:31
  45.1 8.6 %collective-permute-start.3 = (f32[4,48,128]{2,1,0:T(8,128)S(1)}, f32[4,48,128]{2,1,0:T(8,128)S(1)}, u32[]{:S(2)}, u32[]{:S(2)}) collective-permute-start(f32[4,48,128]{2,1,0:T(8,128)S(1)} %pad_maximum_fusion.2), channel_id=1, source_target_pairs={{0,32},{16,48},{32,0},{48,16},{64,96},{80,112},{96,64},{112,80},{1... | collective-permute-start | bytes 294920 | tf_op jit(solution)/shard_map/ppermute | solution.py:31
  53.6 8.7 %collective-permute-start.4 = (f32[8,48,128]{2,1,0:T(8,128)S(1)}, f32[8,48,128]{2,1,0:T(8,128)S(1)}, u32[]{:S(2)}, u32[]{:S(2)}) collective-permute-start(f32[8,48,128]{2,1,0:T(8,128)S(1)} %pad_maximum_fusion), channel_id=1, source_target_pairs={{0,16},{16,0},{32,48},{48,32},{64,80},{80,64},{96,112},{112,96},{1... | collective-permute-start | bytes 589832 | tf_op jit(solution)/shard_map/ppermute | solution.py:31
  62.4 12.1 %collective-permute-start.5 = (f32[16,48,128]{2,1,0:T(8,128)S(1)}, f32[16,48,128]{2,1,0:T(8,128)S(1)}, u32[]{:S(2)}, u32[]{:S(2)}) collective-permute-start(f32[16,48,128]{2,1,0:T(8,128)S(1)} %get-tuple-element.14), channel_id=1, source_target_pairs={{0,256},{16,272},{32,288},{48,304},{64,320},{80,336},{96,352},{112... | collective-permute-start | bytes 1179656 | tf_op jit(solution)/shard_map/ppermute | solution.py:31
  78.6 21.8 %collective-permute-start.6 = (bf16[384,128]{1,0:T(8,128)(2,1)S(1)}, bf16[384,128]{1,0:T(8,128)(2,1)S(1)}, u32[]{:S(2)}, u32[]{:S(2)}) collective-permute-start(bf16[384,128]{1,0:T(8,128)(2,1)S(1)} %convert_element_type.98), channel_id=1, source_target_pairs={{0,0},{1,32},{2,64},{3,96},{4,128},{5,160},{6,192},{7,224},{8,256}... | collective-permute-start | bytes 294920 | tf_op jit(solution)/shard_map/ppermute | solution.py:106

commit v6 on v4

--- a/solution.py
+++ b/solution.py
@@ -7,10 +7,6 @@
 CAMS = 2
 LANES = 128
 HIGHEST = lax.Precision.HIGHEST
-
-PARAM_ORDER = (8, 4, 2, 1, 16)
-TILE_ORDER = (8, 2, 4, 1)
-
 
 def corner_shapes(rows, cols):
     vertical = ((jnp.arange(rows) % EL).astype(jnp.float32) + 0.5) / EL
@@ -22,20 +18,10 @@
     )
 
 
-def doubling_gather(piece, axes, order):
-    size = 1
-    for bit in order:
-        size *= 2
-    me = lax.axis_index(axes)
-    data = piece[None]
-    for bit in order:
-        theirs = lax.ppermute(data, axes, [(i, i ^ bit) for i in range(size)])
-        data = jnp.concatenate([data, theirs], axis=0)
-    wanted = me ^ jnp.arange(size, dtype=jnp.int32)
-    position = jnp.zeros((size,), jnp.int32)
-    for step, bit in enumerate(order):
-        position = position | (((wanted // bit) % 2) << step)
-    return jnp.take(data, position, axis=0)
+def exchange_gather(piece, axes):
+    size = lax.axis_size(axes)
+    copies = jnp.broadcast_to(piece[None], (size,) + piece.shape)
+    return lax.all_to_all(copies, axes, 0, 0, tiled=False)
 
 
 def as_lanes(flat, dtype):
@@ -81,7 +67,7 @@
     proj = jnp.einsum("eip,ep->ei", design, weighted, preferred_element_type=jnp.float32)
 
     payload = jnp.concatenate([node_panel.reshape(-1).astype(jnp.float32), gram.reshape(-1), proj.reshape(-1)])
-    own = doubling_gather(as_lanes(payload, jnp.float32), ("row", "col"), TILE_ORDER)
+    own = exchange_gather(as_lanes(payload, jnp.float32), ("row", "col"))
     own = own.reshape(tiles, -1)
     n_nodes = node_rows * node_cols * comps * width
     n_gram = elements * 144
@@ -97,7 +83,7 @@
         for t in range(tiles):
             route.append((b * tiles + t, (per_block * t + b % per_block) * tiles + b // per_block))
     moved = lax.ppermute(as_lanes(node_panel.reshape(-1), jnp.bfloat16), ("param", "row", "col"), route)
-    cross = doubling_gather(moved, "param", PARAM_ORDER).reshape(n_param, -1)[:, : node_rows * node_cols * comps * width]
+    cross = exchange_gather(moved, "param").reshape(n_param, -1)[:, : node_rows * node_cols * comps * width]
     cross = cross.reshape(n_row, n_col, per_block, node_rows, node_cols, comps, width)
     cross = cross.transpose(0, 3, 1, 4, 5, 2, 6)
     cross = cross.reshape(n_row * node_rows, n_col * node_cols, comps, per_block * width)

time: 87.2 us -> 69 us (0.79)
  the two profiles are of different devices: /device:TPU:1 before, /device:TPU:19 now
where the time goes in v6:
time: 69 us; the launch traced here: 68.5 us
  starting transfers between devices  37.4 us (54%)
  waiting for transfers between devices  13.8 us (20%)
  local copies, waits for them, and re-layouts  10.9 us (16%)
  other arithmetic  4.42 us (6%)
  matrix products  1.07 us (2%)
  between operations  0.94 us (1%)
    all_to_all x2, starting transfers between devices, exchange_gather(): return lax.all_to_all(copies, axes, 0, 0, tiled=False)  27.8 us
    all_to_all x2, waiting for transfers between devices, exchange_gather(): return lax.all_to_all(copies, axes, 0, 0, tiled=False)  12.5 us
    ppermute x1, starting transfers between devices, on_device(): lax.ppermute(as_lanes(node_panel.reshape(-1), jnp.bfloat16), ('param', 'r...  9.59 us
    broadcast_in_dim x2, local copies, waits for them, and re-layouts, exchange_gather(): copies = jnp.broadcast_to(piece[None], (size,) + piece.shape)  1.48 us
    another operation x1, local copies, waits for them, and re-layouts, on_device(): cross.reshape(n_row, n_col, per_block, node_rows, node_cols, comps, width)  1.46 us
  transfers between devices with their start and end apart: 3, of which 2 were waited for; matrix products, arithmetic and copies ran while one was open for 11% of the time, Pallas kernels for 0%

profile of v6, /device:TPU:19, one launch (start us, length us, event | category | flops | bytes accessed | tf_op | source)
XLA Modules:
  0.0 68.5 jit_solution(2778361394412302196)
XLA Ops:
  0.7 0.7 convert_bitcast_fusion
  1.3 0.8 %multiply_convert_fusion.1 = (bf16[2,8,128]{2,1,0:T(8,128)(2,1)S(1)}, f32[2,8,128]{2,1,0:T(8,128)S(1)}) fusion(f32[2,8,128]{2,1,0:T(8,128)} %param.7, f32[2,8,128]{2,1,0:T(8,128)} %param.6, f32[8]{0:T(128)S(1)} %convert_bitcast_fusion), kind=kLoop, calls=%fused_computation.34 | loop fusion | flops 6144 | bytes 28704 | tf_op jit(solution)/shard_map/convert_element_type | solution.py:63
  2.1 0.1 mul.159
  2.2 0.1 copy.34
  2.3 0.9 %reshape.297 = f32[3,2,8,16,8]{4,3,2,1,0:T(8,128)S(1)} reshape(bf16[3,2,8,128]{3,2,1,0:T(8,128)(2,1)} %param.5) | data formatting | bytes 36864 | tf_op jit(solution)/shard_map/mul | solution.py:59
  3.2 0.1 copy.35
  3.4 0.1 broadcast_multiply_fusion.3
  3.6 0.1 multiply_convert_fusion
  3.6 0.2 copy.36
  3.9 0.1 reshape.288
  4.0 0.1 copy.38
  4.1 0.2 fusion.18
  4.3 0.1 fusion.19
  4.5 0.1 reshape.290
  4.6 0.1 reshape.287
  4.7 0.1 reshape.296
  4.8 0.8 %broadcast_in_dim.7 = f32[16,48,128]{2,1,0:T(8,128)} broadcast(f32[48,128]{1,0:T(8,128)S(1)} %fusion.7), dimensions={1,2} | broadcast | bytes 417792 | tf_op jit(solution)/shard_map/broadcast_in_dim | solution.py:23
  5.6 9.3 %all-to-all-start = ((f32[16,48,128]{2,1,0:T(8,128)}), f32[16,48,128]{2,1,0:T(8,128)S(1)}, u32[]{:S(2)}, u32[]{:S(2)}) async-start(f32[16,48,128]{2,1,0:T(8,128)} %broadcast_in_dim.7), calls=%async_computation | async-start | bytes 786432 | tf_op jit(solution)/shard_map/all_to_all | solution.py:24
  14.9 0.1 reshape.293
  15.0 9.6 %collective-permute-start = (bf16[24,128]{1,0:T(8,128)(2,1)S(1)}, bf16[24,128]{1,0:T(8,128)(2,1)S(1)}, u32[]{:S(2)}, u32[]{:S(2)}) collective-permute-start(bf16[24,128]{1,0:T(8,128)(2,1)S(1)} %reshape.293), channel_id=1, source_target_pairs={{0,0},{1,32},{2,64},{3,96},{4,128},{5,160},{6,192},{7,224},{8,256}... | collective-permute-start | bytes 18440 | tf_op jit(solution)/shard_map/ppermute | solution.py:85
  24.6 1.3 %collective-permute-done = bf16[24,128]{1,0:T(8,128)(2,1)S(1)} collective-permute-done((bf16[24,128]{1,0:T(8,128)(2,1)S(1)}, bf16[24,128]{1,0:T(8,128)(2,1)S(1)}, u32[]{:S(2)}, u32[]{:S(2)}) %collective-permute-start) | collective-permute-done | bytes 6176 | tf_op jit(solution)/shard_map/ppermute | solution.py:85
  25.9 0.7 %broadcast_in_dim.8 = bf16[32,24,128]{2,1,0:T(8,128)(2,1)} broadcast(bf16[24,128]{1,0:T(8,128)(2,1)S(1)} %collective-permute-done), dimensions={1,2} | broadcast | bytes 202752 | tf_op jit(solution)/shard_map/broadcast_in_dim | solution.py:23
  26.6 18.5 %all-to-all-start.1 = ((bf16[32,24,128]{2,1,0:T(8,128)(2,1)}), bf16[32,24,128]{2,1,0:T(8,128)(2,1)}, u32[]{:S(2)}, u32[]{:S(2)}) async-start(bf16[32,24,128]{2,1,0:T(8,128)(2,1)} %broadcast_in_dim.8), calls=%async_computation.1 | async-start | bytes 393216 | tf_op jit(solution)/shard_map/all_to_all | solution.py:24
  45.1 0.1 copy.50
  45.3 0.2 convert_element_type.105
  45.5 0.2 convert_element_type.104
  45.7 0.2 slice_bitcast_fusion.2
  46.0 1.1 %maximum_bitcast_fusion = bf16[4,3,4,64,64]{4,1,3,2,0:T(4,128)(2,1)S(1)} fusion(bf16[1,4,64,3,64]{4,3,2,1,0:T(4,128)(2,1)S(1)} %get-tuple-element.8, bf16[1,4,64,3,64]{4,3,2,1,0:T(4,128)(2,1)S(1)} %get-tuple-element.7, bf16[1,4,64,3,64]{4,3,2,1,0:T(4,128)(2,1)S(1)} %get-tuple-element.6, bf16[1,4,64,3,64]{4,3,2,1,0:T(4,128)(2,1)S(1)} %convert_element_type.104), kind=kLoop, calls=%fused_computation.5 | loop fusion | flops 589824 | bytes 786432 | tf_op jit(solution)/shard_map/transpose | solution.py:38
  47.0 0.9 %copy.40 = bf16[4,3,4,64,64]{3,2,4,1,0:T(4,128)(2,1)S(1)} copy(bf16[4,3,4,64,64]{4,1,3,2,0:T(4,128)(2,1)S(1)} %maximum_bitcast_fusion) | data formatting | bytes 786432 | tf_op jit(solution)/shard_map/transpose | solution.py:38
  48.0 0.5 reshape.292
  48.4 0.1 reshape_transpose_reshape.8
  48.6 0.1 copy.47
  48.6 0.1 convert_element_type.106
  48.7 0.9 %reshape_transpose_reshape.7 = f32[256,12,12]{2,1,0:T(8,128)S(1)} reshape(f32[16,2304]{1,0:T(8,128)S(1)} %slice.46) | data formatting | bytes 294912 | tf_op jit(solution)/shard_map/reshape;transpose;reshape | solution.py:77
  49.7 0.8 %copy.39 = f32[12,12,256]{2,1,0:T(8,128)S(1)} copy(f32[12,12,256]{1,0,2:T(8,128)S(1)} %bitcast.58) | data formatting | bytes 294912 | tf_op jit(solution)/shard_map/transpose | solution.py:93
  50.5 0.4 convolution_bitcast_fusion.1
  50.9 0.6 dynamic_slice.3
  51.5 0.7 %multiply_reduce_fusion = f32[12,256,64]{1,2,0:T(8,128)S(1)} fusion(f32[12,256,64]{1,2,0:T(8,128)S(1)} %convert_element_type.106, f32[12,12,256]{2,1,0:T(8,128)S(1)} %copy.39), kind=kLoop, calls=%fused_computation | loop fusion | flops 4521984 | bytes 1720320 | tf_op jit(solution)/shard_map/reduce_sum | solution.py:93
  52.2 0.2 reduce-precision_convert_fusion
  52.4 12.5 %all-to-all-done.1 = bf16[32,24,128]{2,1,0:T(8,128)(2,1)} async-done(((bf16[32,24,128]{2,1,0:T(8,128)(2,1)}), bf16[32,24,128]{2,1,0:T(8,128)(2,1)}, u32[]{:S(2)}, u32[]{:S(2)}) %all-to-all-start.1) | async-done | bytes 196640 | tf_op jit(solution)/shard_map/all_to_all | solution.py:24
  64.9 1.5 %reshape_reshape.3 = bf16[4,4,2,1,16,3,64]{6,5,4,2,1,0,3:T(4,128)(2,1)S(1)} reshape(bf16[32,24,128]{2,1,0:T(8,128)(2,1)} %all-to-all-done.1) | data formatting | bytes 393216 | tf_op jit(solution)/shard_map/reshape;reshape | solution.py:87
  66.4 0.5 copy.42
  66.9 0.2 reshape.294
  67.1 0.2 stack.40
  67.3 0.1 fusion.4
  67.4 0.1 maximum_bitcast_fusion.1
  67.6 0.4 convolution_bitcast_fusion
  67.9 0.6 slice_add_fusion
  (15 shorter events, 0.2 us)
Async XLA Ops:
  2.1 2.6 %copy-start = (bf16[1,16,3,64]{3,1,2,0:T(8,128)(2,1)S(1)}, bf16[1,16,3,64]{3,1,2,0:T(8,128)(2,1)}, u32[]{:S(2)}) copy-start(bf16[1,16,3,64]{3,1,2,0:T(8,128)(2,1)} %param.9) | copy-start | bytes 18436
  5.6 20.3 %all-to-all-start = ((f32[16,48,128]{2,1,0:T(8,128)}), f32[16,48,128]{2,1,0:T(8,128)S(1)}, u32[]{:S(2)}, u32[]{:S(2)}) async-start(f32[16,48,128]{2,1,0:T(8,128)} %broadcast_in_dim.7), calls=%async_computation | async-start | bytes 786432 | tf_op jit(solution)/shard_map/all_to_all | solution.py:24
  15.0 10.9 %collective-permute-start = (bf16[24,128]{1,0:T(8,128)(2,1)S(1)}, bf16[24,128]{1,0:T(8,128)(2,1)S(1)}, u32[]{:S(2)}, u32[]{:S(2)}) collective-permute-start(bf16[24,128]{1,0:T(8,128)(2,1)S(1)} %reshape.293), channel_id=1, source_target_pairs={{0,0},{1,32},{2,64},{3,96},{4,128},{5,160},{6,192},{7,224},{8,256}... | collective-permute-start | bytes 18440 | tf_op jit(solution)/shard_map/ppermute | solution.py:85
  26.6 38.3 %all-to-all-start.1 = ((bf16[32,24,128]{2,1,0:T(8,128)(2,1)}), bf16[32,24,128]{2,1,0:T(8,128)(2,1)}, u32[]{:S(2)}, u32[]{:S(2)}) async-start(bf16[32,24,128]{2,1,0:T(8,128)(2,1)} %broadcast_in_dim.8), calls=%async_computation.1 | async-start | bytes 393216 | tf_op jit(solution)/shard_map/all_to_all | solution.py:24

commit v7 on v6

--- a/solution.py
+++ b/solution.py
@@ -66,27 +66,29 @@
     gram = jnp.einsum("eip,ejp->eij", design, design, preferred_element_type=jnp.float32)
     proj = jnp.einsum("eip,ep->ei", design, weighted, preferred_element_type=jnp.float32)
 
-    payload = jnp.concatenate([node_panel.reshape(-1).astype(jnp.float32), gram.reshape(-1), proj.reshape(-1)])
-    own = exchange_gather(as_lanes(payload, jnp.float32), ("row", "col"))
-    own = own.reshape(tiles, -1)
     n_nodes = node_rows * node_cols * comps * width
     n_gram = elements * 144
-    own_nodes = own[:, :n_nodes].reshape(n_row, n_col, node_rows, node_cols, comps, width)
-    own_nodes = own_nodes.transpose(0, 2, 1, 3, 4, 5).reshape(n_row * node_rows, n_col * node_cols, comps, width)
-    grams = own[:, n_nodes : n_nodes + n_gram].reshape(n_row, n_col, elem_rows, elem_cols, 12, 12)
-    grams = grams.transpose(0, 2, 1, 3, 4, 5).reshape(-1, 12, 12)
-    projs = own[:, n_nodes + n_gram : n_nodes + n_gram + elements * 12]
-    projs = projs.reshape(n_row, n_col, elem_rows, elem_cols, 12).transpose(0, 2, 1, 3, 4).reshape(-1, 12)
-
-    route = []
-    for b in range(n_param):
-        for t in range(tiles):
-            route.append((b * tiles + t, (per_block * t + b % per_block) * tiles + b // per_block))
-    moved = lax.ppermute(as_lanes(node_panel.reshape(-1), jnp.bfloat16), ("param", "row", "col"), route)
-    cross = exchange_gather(moved, "param").reshape(n_param, -1)[:, : node_rows * node_cols * comps * width]
+    panel = exchange_gather(as_lanes(node_panel.reshape(-1), jnp.bfloat16), "param")
+    panel = panel.reshape(n_param, -1)[:, :n_nodes]
+    own_block = lax.dynamic_index_in_dim(panel, lax.axis_index("param"), axis=0, keepdims=False)
+    common = jnp.concatenate([own_block.astype(jnp.float32), gram.reshape(-1), proj.reshape(-1)])
+    per_tile = panel.reshape(tiles, per_block * n_nodes).astype(jnp.float32)
+    chunks = jnp.concatenate([per_tile, jnp.broadcast_to(common[None], (tiles,) + common.shape)], axis=1)
+    rows_used = -(-chunks.shape[1] // (8 * LANES)) * 8
+    chunks = jnp.pad(chunks, ((0, 0), (0, rows_used * LANES - chunks.shape[1])))
+    got = lax.all_to_all(chunks.reshape(tiles, rows_used, LANES), ("row", "col"), 0, 0, tiled=False)
+    got = got.reshape(tiles, -1)
+    cross = got[:, : per_block * n_nodes].astype(jnp.bfloat16)
     cross = cross.reshape(n_row, n_col, per_block, node_rows, node_cols, comps, width)
     cross = cross.transpose(0, 3, 1, 4, 5, 2, 6)
     cross = cross.reshape(n_row * node_rows, n_col * node_cols, comps, per_block * width)
+    base = per_block * n_nodes
+    own_nodes = got[:, base : base + n_nodes].reshape(n_row, n_col, node_rows, node_cols, comps, width)
+    own_nodes = own_nodes.transpose(0, 2, 1, 3, 4, 5).reshape(n_row * node_rows, n_col * node_cols, comps, width)
+    grams = got[:, base + n_nodes : base + n_nodes + n_gram].reshape(n_row, n_col, elem_rows, elem_cols, 12, 12)
+    grams = grams.transpose(0, 2, 1, 3, 4, 5).reshape(-1, 12, 12)
+    projs = got[:, base + n_nodes + n_gram : base + n_nodes + n_gram + elements * 12]
+    projs = projs.reshape(n_row, n_col, elem_rows, elem_cols, 12).transpose(0, 2, 1, 3, 4).reshape(-1, 12)
 
     rows_of = element_corners(own_nodes.astype(jnp.bfloat16))
     cols_of = element_corners(cross)

time: 69 us -> 73.1 us (1.059)
  the two profiles are of different devices: /device:TPU:19 before, /device:TPU:1 now
where the time goes in v7:
time: 73.1 us; the launch traced here: 72.7 us
  waiting for transfers between devices  27.4 us (37%)
  starting transfers between devices  27 us (37%)
  local copies, waits for them, and re-layouts  11.7 us (16%)
  other arithmetic  4.51 us (6%)
  matrix products  1.06 us (1%)
  between operations  0.96 us (1%)
    all_to_all x1, starting transfers between devices, exchange_gather(): return lax.all_to_all(copies, axes, 0, 0, tiled=False)  17 us
    all_to_all x1, waiting for transfers between devices, exchange_gather(): return lax.all_to_all(copies, axes, 0, 0, tiled=False)  13.8 us
    all_to_all x1, waiting for transfers between devices, on_device(): lax.all_to_all(chunks.reshape(tiles, rows_used, LANES), ('row', 'col'), 0...  13.6 us
    all_to_all x1, starting transfers between devices, on_device(): lax.all_to_all(chunks.reshape(tiles, rows_used, LANES), ('row', 'col'), 0...  10 us
    unnamed x9, local copies, waits for them, and re-layouts  2.55 us
    transpose x2, local copies, waits for them, and re-layouts, element_corners(): corners = corners.transpose(0, 3, 1, 2, 4)  1.87 us
  transfers between devices with their start and end apart: 2, of which 2 were waited for; matrix products, arithmetic and copies ran while one was open for 4% of the time, Pallas kernels for 0%

profile of v7, /device:TPU:1, one launch (start us, length us, event | category | flops | bytes accessed | tf_op | source)
XLA Modules:
  0.0 72.7 jit_solution(15139056371332535053)
XLA Ops:
  0.6 0.7 copy.31
  1.4 0.1 broadcast_in_dim.6
  1.5 0.7 broadcast_in_dim.7
  2.2 17.0 %all-to-all-start = ((bf16[32,24,128]{2,1,0:T(8,128)(2,1)}), bf16[32,24,128]{2,1,0:T(8,128)(2,1)S(1)}, u32[]{:S(2)}, u32[]{:S(2)}) async-start(bf16[32,24,128]{2,1,0:T(8,128)(2,1)} %broadcast_in_dim.7), calls=%async_computation | async-start | bytes 393216 | tf_op jit(solution)/shard_map/all_to_all | solution.py:24
  19.2 0.7 convert_bitcast_fusion
  19.9 0.8 %multiply_convert_fusion.1 = (bf16[2,8,128]{2,1,0:T(8,128)(2,1)S(1)}, f32[2,8,128]{2,1,0:T(8,128)S(1)}) fusion(f32[2,8,128]{2,1,0:T(8,128)} %param.7, f32[2,8,128]{2,1,0:T(8,128)} %param.6, f32[8]{0:T(128)S(1)} %convert_bitcast_fusion), kind=kLoop, calls=%fused_computation.37 | loop fusion | flops 6144 | bytes 28704 | tf_op jit(solution)/shard_map/convert_element_type | solution.py:63
  20.7 0.1 mul.159
  20.8 0.1 copy.32
  20.9 0.1 broadcast_multiply_fusion.3
  21.0 0.1 reshape.296
  21.1 0.1 copy.36
  21.3 0.2 reshape.307
  21.6 0.1 copy.33
  21.7 0.1 multiply_convert_fusion
  21.8 0.2 copy.34
  22.0 0.1 fusion.18
  22.2 0.1 reshape.298
  22.3 0.2 fusion.17
  22.4 0.1 reshape.295
  22.5 13.8 %all-to-all-done = bf16[32,24,128]{2,1,0:T(8,128)(2,1)S(1)} async-done(((bf16[32,24,128]{2,1,0:T(8,128)(2,1)}), bf16[32,24,128]{2,1,0:T(8,128)(2,1)S(1)}, u32[]{:S(2)}, u32[]{:S(2)}) %all-to-all-start) | async-done | bytes 196640 | tf_op jit(solution)/shard_map/all_to_all | solution.py:24
  36.5 0.1 reshape.305
  36.7 1.0 %copy.46 = f32[2,8,96,128]{3,2,1,0:T(8,128)} copy(f32[2,8,96,128]{3,1,2,0:T(8,128)S(1)} %pad_bitcast_fusion) | data formatting | bytes 1572864
  37.7 10.0 %all-to-all-start.1 = ((f32[16,96,128]{2,1,0:T(8,128)}), f32[16,96,128]{2,1,0:T(8,128)S(1)}, u32[]{:S(2)}, u32[]{:S(2)}) async-start(f32[16,96,128]{2,1,0:T(8,128)} %bitcast.31), calls=%async_computation.1 | async-start | bytes 1572864 | tf_op jit(solution)/shard_map/all_to_all | solution.py:79
  47.7 13.6 %all-to-all-done.1 = f32[16,96,128]{2,1,0:T(8,128)S(1)} async-done(((f32[16,96,128]{2,1,0:T(8,128)}), f32[16,96,128]{2,1,0:T(8,128)S(1)}, u32[]{:S(2)}, u32[]{:S(2)}) %all-to-all-start.1) | async-done | bytes 786464 | tf_op jit(solution)/shard_map/all_to_all | solution.py:79
  61.3 0.5 copy.50
  61.8 0.2 convert_element_type.114
  62.1 0.2 convert_element_type.113
  62.3 0.4 reshape.302
  62.7 0.5 copy.39
  63.2 0.2 reshape.303
  63.4 0.2 stack.40
  63.6 0.1 reshape_transpose_reshape.8
  63.8 0.1 fusion.4
  63.9 0.1 maximum_bitcast_fusion.1
  64.0 0.9 %copy.41 = bf16[4,3,4,64,128]{4,3,2,1,0:T(8,128)(2,1)} copy(bf16[4,3,4,64,128]{4,3,1,2,0:T(8,128)(2,1)S(1)} %maximum_bitcast_fusion.1) | data formatting | bytes 1572864 | tf_op jit(solution)/shard_map/transpose | solution.py:38
  65.0 0.2 slice_bitcast_fusion.2
  65.2 1.1 %maximum_bitcast_fusion = bf16[4,3,4,64,64]{4,1,3,2,0:T(4,128)(2,1)S(1)} fusion(bf16[1,4,64,3,64]{4,3,2,1,0:T(4,128)(2,1)S(1)} %get-tuple-element.8, bf16[1,4,64,3,64]{4,3,2,1,0:T(4,128)(2,1)S(1)} %get-tuple-element.7, bf16[1,4,64,3,64]{4,3,2,1,0:T(4,128)(2,1)S(1)} %get-tuple-element.6, bf16[1,4,64,3,64]{4,3,2,1,0:T(4,128)(2,1)S(1)} %convert_element_type.113), kind=kLoop, calls=%fused_computation.5 | loop fusion | flops 589824 | bytes 786432 | tf_op jit(solution)/shard_map/transpose | solution.py:38
  66.3 0.9 %copy.38 = bf16[4,3,4,64,64]{3,2,4,1,0:T(4,128)(2,1)S(1)} copy(bf16[4,3,4,64,64]{4,1,3,2,0:T(4,128)(2,1)S(1)} %maximum_bitcast_fusion) | data formatting | bytes 786432 | tf_op jit(solution)/shard_map/transpose | solution.py:38
  67.2 0.5 reshape.301
  67.8 0.4 convolution_bitcast_fusion.1
  68.2 1.0 %reshape_transpose_reshape.7 = f32[256,12,12]{2,1,0:T(8,128)S(1)} reshape(f32[16,2304]{1,0:T(8,128)S(1)} %slice.51) | data formatting | bytes 294912 | tf_op jit(solution)/shard_map/reshape;transpose;reshape | solution.py:89
  69.1 0.8 %copy.37 = f32[12,12,256]{2,1,0:T(8,128)S(1)} copy(f32[12,12,256]{1,0,2:T(8,128)S(1)} %bitcast.64) | data formatting | bytes 294912 | tf_op jit(solution)/shard_map/transpose | solution.py:95
  70.0 0.7 multiply_reduce_fusion
  70.7 0.2 reduce-precision_convert_fusion
  70.8 0.3 copy-done
  71.1 0.4 convolution_bitcast_fusion
  71.5 0.6 slice_add_fusion
  72.1 0.6 dynamic_slice.8
  (19 shorter events, 0.5 us)
Async XLA Ops:
  0.6 20.7 %copy-start.1 = (bf16[3,2,8,128]{3,2,1,0:T(8,128)(2,1)S(1)}, bf16[3,2,8,128]{3,2,1,0:T(8,128)(2,1)}, u32[]{:S(2)}) copy-start(bf16[3,2,8,128]{3,2,1,0:T(8,128)(2,1)} %param.5) | copy-start | bytes 36868
  2.2 34.2 %all-to-all-start = ((bf16[32,24,128]{2,1,0:T(8,128)(2,1)}), bf16[32,24,128]{2,1,0:T(8,128)(2,1)S(1)}, u32[]{:S(2)}, u32[]{:S(2)}) async-start(bf16[32,24,128]{2,1,0:T(8,128)(2,1)} %broadcast_in_dim.7), calls=%async_computation | async-start | bytes 393216 | tf_op jit(solution)/shard_map/all_to_all | solution.py:24
  37.7 23.6 %all-to-all-start.1 = ((f32[16,96,128]{2,1,0:T(8,128)}), f32[16,96,128]{2,1,0:T(8,128)S(1)}, u32[]{:S(2)}, u32[]{:S(2)}) async-start(f32[16,96,128]{2,1,0:T(8,128)} %bitcast.31), calls=%async_computation.1 | async-start | bytes 1572864 | tf_op jit(solution)/shard_map/all_to_all | solution.py:79
  70.0 1.1 %copy-start = (bf16[4,3,4,64,128]{4,3,2,1,0:T(8,128)(2,1)S(1)}, bf16[4,3,4,64,128]{4,3,2,1,0:T(8,128)(2,1)}, u32[]{:S(2)}) copy-start(bf16[4,3,4,64,128]{4,3,2,1,0:T(8,128)(2,1)} %copy.41) | copy-start | bytes 2359300

commit v8 on v6

--- a/solution.py
+++ b/solution.py
@@ -78,12 +78,22 @@
     projs = own[:, n_nodes + n_gram : n_nodes + n_gram + elements * 12]
     projs = projs.reshape(n_row, n_col, elem_rows, elem_cols, 12).transpose(0, 2, 1, 3, 4).reshape(-1, 12)
 
-    route = []
-    for b in range(n_param):
-        for t in range(tiles):
-            route.append((b * tiles + t, (per_block * t + b % per_block) * tiles + b // per_block))
-    moved = lax.ppermute(as_lanes(node_panel.reshape(-1), jnp.bfloat16), ("param", "row", "col"), route)
-    cross = exchange_gather(moved, "param").reshape(n_param, -1)[:, : node_rows * node_cols * comps * width]
+    half = n_param // 2
+    pieces = []
+    for flip in (0, half):
+        route = []
+        for b in range(n_param):
+            for t in range(tiles):
+                target = (per_block * t + b % per_block) ^ flip
+                route.append((b * tiles + t, target * tiles + b // per_block))
+        pieces.append(lax.ppermute(as_lanes(node_panel.reshape(-1), jnp.bfloat16), ("param", "row", "col"), route))
+    pair = jnp.stack(pieces)
+    groups = [list(range(half)), list(range(half, n_param))]
+    copies = jnp.broadcast_to(pair[None], (half,) + pair.shape)
+    got = lax.all_to_all(copies, "param", 0, 0, axis_index_groups=groups, tiled=False)
+    upper = lax.axis_index("param") // half
+    got = jnp.where(upper == 0, got, got[:, ::-1])
+    cross = got.transpose(1, 0, 2, 3).reshape(n_param, -1)[:, : node_rows * node_cols * comps * width]
     cross = cross.reshape(n_row, n_col, per_block, node_rows, node_cols, comps, width)
     cross = cross.transpose(0, 3, 1, 4, 5, 2, 6)
     cross = cross.reshape(n_row * node_rows, n_col * node_cols, comps, per_block * width)

time: 69 us -> 71 us (1.029)
  the two profiles are of different devices: /device:TPU:19 before, /device:TPU:26 now
where the time goes in v8:
time: 71 us; the launch traced here: 70.5 us
  starting transfers between devices  33.9 us (48%)
  waiting for transfers between devices  19.3 us (27%)
  local copies, waits for them, and re-layouts  9.71 us (14%)
  other arithmetic  5.5 us (8%)
  matrix products  1.07 us (2%)
  between operations  0.98 us (1%)
    ppermute x2, starting transfers between devices, on_device(): lax.ppermute(as_lanes(node_panel.reshape(-1), jnp.bfloat16), ('param', 'r...  15.5 us
    all_to_all x1, starting transfers between devices, on_device(): lax.all_to_all(copies, 'param', 0, 0, axis_index_groups=groups, tiled=False)  11.1 us
    ppermute x2, waiting for transfers between devices, on_device(): lax.ppermute(as_lanes(node_panel.reshape(-1), jnp.bfloat16), ('param', 'r...  10.4 us
    all_to_all x1, waiting for transfers between devices, on_device(): lax.all_to_all(copies, 'param', 0, 0, axis_index_groups=groups, tiled=False)  8.93 us
    all_to_all x1, starting transfers between devices, exchange_gather(): return lax.all_to_all(copies, axes, 0, 0, tiled=False)  7.25 us
  transfers between devices with their start and end apart: 4, of which 2 were waited for; matrix products, arithmetic and copies ran while one was open for 10% of the time, Pallas kernels for 0%

profile of v8, /device:TPU:26, one launch (start us, length us, event | category | flops | bytes accessed | tf_op | source)
XLA Modules:
  0.0 70.5 jit_solution(8487773629588819706)
XLA Ops:
  0.7 0.7 convert_bitcast_fusion
  1.3 0.8 %multiply_convert_fusion.1 = (bf16[2,8,128]{2,1,0:T(8,128)(2,1)S(1)}, f32[2,8,128]{2,1,0:T(8,128)S(1)}) fusion(f32[2,8,128]{2,1,0:T(8,128)} %param.7, f32[2,8,128]{2,1,0:T(8,128)} %param.6, f32[8]{0:T(128)S(1)} %convert_bitcast_fusion), kind=kLoop, calls=%fused_computation.37 | loop fusion | flops 6144 | bytes 28704 | tf_op jit(solution)/shard_map/convert_element_type | solution.py:63
  2.1 0.1 mul.159
  2.2 0.1 copy.48
  2.3 0.9 %reshape.299 = f32[3,2,8,16,8]{4,3,2,1,0:T(8,128)S(1)} reshape(bf16[3,2,8,128]{3,2,1,0:T(8,128)(2,1)} %param.5) | data formatting | bytes 36864 | tf_op jit(solution)/shard_map/mul | solution.py:59
  3.2 0.1 copy.49
  3.4 0.1 broadcast_multiply_fusion.3
  3.6 0.1 multiply_convert_fusion
  3.6 0.2 copy.50
  3.9 0.1 reshape.290
  4.0 0.1 copy.52
  4.1 0.2 fusion.19
  4.3 0.1 fusion.20
  4.5 0.1 reshape.292
  4.6 0.1 reshape.289
  4.7 0.1 reshape.298
  4.8 0.8 %broadcast_in_dim.7 = f32[16,48,128]{2,1,0:T(8,128)} broadcast(f32[48,128]{1,0:T(8,128)S(1)} %fusion.8), dimensions={1,2} | broadcast | bytes 417792 | tf_op jit(solution)/shard_map/broadcast_in_dim | solution.py:23
  5.6 7.3 %all-to-all-start = ((f32[16,48,128]{2,1,0:T(8,128)}), f32[16,48,128]{2,1,0:T(8,128)S(1)}, u32[]{:S(2)}, u32[]{:S(2)}) async-start(f32[16,48,128]{2,1,0:T(8,128)} %broadcast_in_dim.7), calls=%async_computation | async-start | bytes 786432 | tf_op jit(solution)/shard_map/all_to_all | solution.py:24
  12.8 0.1 reshape.295
  12.9 13.5 %collective-permute-start = (bf16[24,128]{1,0:T(8,128)(2,1)S(1)}, bf16[24,128]{1,0:T(8,128)(2,1)S(1)}, u32[]{:S(2)}, u32[]{:S(2)}) collective-permute-start(bf16[24,128]{1,0:T(8,128)(2,1)S(1)} %reshape.295), channel_id=1, source_target_pairs={{0,0},{1,32},{2,64},{3,96},{4,128},{5,160},{6,192},{7,224},{8,256}... | collective-permute-start | bytes 18440 | tf_op jit(solution)/shard_map/ppermute | solution.py:89
  26.4 2.0 %collective-permute-start.1 = (bf16[24,128]{1,0:T(8,128)(2,1)S(1)}, bf16[24,128]{1,0:T(8,128)(2,1)S(1)}, u32[]{:S(2)}, u32[]{:S(2)}) collective-permute-start(bf16[24,128]{1,0:T(8,128)(2,1)S(1)} %reshape.295), channel_id=1, source_target_pairs={{0,256},{1,288},{2,320},{3,352},{4,384},{5,416},{6,448},{7,480},{8... | collective-permute-start | bytes 18440 | tf_op jit(solution)/shard_map/ppermute | solution.py:89
  28.5 10.4 %collective-permute-done.1 = bf16[24,128]{1,0:T(8,128)(2,1)S(1)} collective-permute-done((bf16[24,128]{1,0:T(8,128)(2,1)S(1)}, bf16[24,128]{1,0:T(8,128)(2,1)S(1)}, u32[]{:S(2)}, u32[]{:S(2)}) %collective-permute-start.1) | collective-permute-done | bytes 6176 | tf_op jit(solution)/shard_map/ppermute | solution.py:89
  38.9 0.7 broadcast_in_dim.8
  39.6 11.1 %all-to-all-start.1 = ((bf16[16,2,24,128]{3,2,1,0:T(8,128)(2,1)}), bf16[16,2,24,128]{3,2,1,0:T(8,128)(2,1)}, u32[]{:S(2)}, u32[]{:S(2)}) async-start(bf16[16,2,24,128]{3,2,1,0:T(8,128)(2,1)} %broadcast_in_dim.8), calls=%async_computation.1 | async-start | bytes 393216 | tf_op jit(solution)/shard_map/all_to_all | solution.py:93
  50.7 0.1 copy.65
  50.9 0.2 convert_element_type.105
  51.1 0.2 convert_element_type.104
  51.3 0.2 slice_bitcast_fusion.2
  51.6 1.1 %maximum_bitcast_fusion = bf16[4,3,4,64,64]{4,1,3,2,0:T(4,128)(2,1)S(1)} fusion(bf16[1,4,64,3,64]{4,3,2,1,0:T(4,128)(2,1)S(1)} %get-tuple-element.8, bf16[1,4,64,3,64]{4,3,2,1,0:T(4,128)(2,1)S(1)} %get-tuple-element.7, bf16[1,4,64,3,64]{4,3,2,1,0:T(4,128)(2,1)S(1)} %get-tuple-element.6, bf16[1,4,64,3,64]{4,3,2,1,0:T(4,128)(2,1)S(1)} %convert_element_type.104), kind=kLoop, calls=%fused_computation.5 | loop fusion | flops 589824 | bytes 786432 | tf_op jit(solution)/shard_map/transpose | solution.py:38
  52.7 0.9 %copy.54 = bf16[4,3,4,64,64]{3,2,4,1,0:T(4,128)(2,1)S(1)} copy(bf16[4,3,4,64,64]{4,1,3,2,0:T(4,128)(2,1)S(1)} %maximum_bitcast_fusion) | data formatting | bytes 786432 | tf_op jit(solution)/shard_map/transpose | solution.py:38
  53.6 0.5 reshape.294
  54.1 0.1 reshape_transpose_reshape.8
  54.4 0.9 %reshape_transpose_reshape.7 = f32[256,12,12]{2,1,0:T(8,128)S(1)} reshape(f32[16,2304]{1,0:T(8,128)S(1)} %slice.46) | data formatting | bytes 294912 | tf_op jit(solution)/shard_map/reshape;transpose;reshape | solution.py:77
  55.3 0.8 %copy.53 = f32[12,12,256]{2,1,0:T(8,128)S(1)} copy(f32[12,12,256]{1,0,2:T(8,128)S(1)} %bitcast.64) | data formatting | bytes 294912 | tf_op jit(solution)/shard_map/transpose | solution.py:103
  56.1 0.4 convolution_bitcast_fusion.1
  56.5 0.6 dynamic_slice.3
  57.1 0.7 %multiply_reduce_fusion = f32[12,256,64]{1,2,0:T(8,128)S(1)} fusion(f32[12,256,64]{1,2,0:T(8,128)S(1)} %convert_element_type.106, f32[12,12,256]{2,1,0:T(8,128)S(1)} %copy.53), kind=kLoop, calls=%fused_computation | loop fusion | flops 4521984 | bytes 1720320 | tf_op jit(solution)/shard_map/reduce_sum | solution.py:103
  57.9 0.2 reduce-precision_convert_fusion
  58.0 8.9 %all-to-all-done.1 = bf16[16,2,24,128]{3,2,1,0:T(8,128)(2,1)} async-done(((bf16[16,2,24,128]{3,2,1,0:T(8,128)(2,1)}), bf16[16,2,24,128]{3,2,1,0:T(8,128)(2,1)}, u32[]{:S(2)}, u32[]{:S(2)}) %all-to-all-start.1) | async-done | bytes 196640 | tf_op jit(solution)/shard_map/all_to_all | solution.py:93
  67.0 1.1 %fusion.7 = bf16[2,16,24,128]{3,2,0,1:T(8,128)(2,1)S(1)} fusion(bf16[16,2,24,128]{3,2,1,0:T(8,128)(2,1)} %all-to-all-done.1, pred[]{:T(512)S(6)} %eq.7), kind=kLoop, calls=%fused_computation.23 | loop fusion | flops 98304 | bytes 393217 | tf_op jit(solution)/shard_map/transpose | solution.py:96
  68.1 0.3 reshape_reshape.3
  68.3 0.5 copy.57
  68.8 0.2 reshape.296
  69.0 0.2 stack.52
  69.2 0.1 fusion.4
  69.3 0.1 maximum_bitcast_fusion.1
  69.5 0.4 convolution_bitcast_fusion
  69.9 0.6 slice_add_fusion
  (20 shorter events, 0.4 us)
Async XLA Ops:
  2.1 2.6 %copy-start = (bf16[1,16,3,64]{3,1,2,0:T(8,128)(2,1)S(1)}, bf16[1,16,3,64]{3,1,2,0:T(8,128)(2,1)}, u32[]{:S(2)}) copy-start(bf16[1,16,3,64]{3,1,2,0:T(8,128)(2,1)} %param.9) | copy-start | bytes 18436
  5.6 33.3 %all-to-all-start = ((f32[16,48,128]{2,1,0:T(8,128)}), f32[16,48,128]{2,1,0:T(8,128)S(1)}, u32[]{:S(2)}, u32[]{:S(2)}) async-start(f32[16,48,128]{2,1,0:T(8,128)} %broadcast_in_dim.7), calls=%async_computation | async-start | bytes 786432 | tf_op jit(solution)/shard_map/all_to_all | solution.py:24
  12.9 15.6 %collective-permute-start = (bf16[24,128]{1,0:T(8,128)(2,1)S(1)}, bf16[24,128]{1,0:T(8,128)(2,1)S(1)}, u32[]{:S(2)}, u32[]{:S(2)}) collective-permute-start(bf16[24,128]{1,0:T(8,128)(2,1)S(1)} %reshape.295), channel_id=1, source_target_pairs={{0,0},{1,32},{2,64},{3,96},{4,128},{5,160},{6,192},{7,224},{8,256}... | collective-permute-start | bytes 18440 | tf_op jit(solution)/shard_map/ppermute | solution.py:89
  26.4 12.4 %collective-permute-start.1 = (bf16[24,128]{1,0:T(8,128)(2,1)S(1)}, bf16[24,128]{1,0:T(8,128)(2,1)S(1)}, u32[]{:S(2)}, u32[]{:S(2)}) collective-permute-start(bf16[24,128]{1,0:T(8,128)(2,1)S(1)} %reshape.295), channel_id=1, source_target_pairs={{0,256},{1,288},{2,320},{3,352},{4,384},{5,416},{6,448},{7,480},{8... | collective-permute-start | bytes 18440 | tf_op jit(solution)/shard_map/ppermute | solution.py:89
  39.6 27.4 %all-to-all-start.1 = ((bf16[16,2,24,128]{3,2,1,0:T(8,128)(2,1)}), bf16[16,2,24,128]{3,2,1,0:T(8,128)(2,1)}, u32[]{:S(2)}, u32[]{:S(2)}) async-start(bf16[16,2,24,128]{3,2,1,0:T(8,128)(2,1)} %broadcast_in_dim.8), calls=%async_computation.1 | async-start | bytes 393216 | tf_op jit(solution)/shard_map/all_to_all | solution.py:93

commit v9 on v6

--- a/solution.py
+++ b/solution.py
@@ -1,5 +1,6 @@
 import jax
 import jax.numpy as jnp
+import numpy as np
 from jax import lax
 from jax.sharding import PartitionSpec as P
 
@@ -66,17 +67,29 @@
     gram = jnp.einsum("eip,ejp->eij", design, design, preferred_element_type=jnp.float32)
     proj = jnp.einsum("eip,ep->ei", design, weighted, preferred_element_type=jnp.float32)
 
-    payload = jnp.concatenate([node_panel.reshape(-1).astype(jnp.float32), gram.reshape(-1), proj.reshape(-1)])
-    own = exchange_gather(as_lanes(payload, jnp.float32), ("row", "col"))
+    upper_i, upper_j = np.triu_indices(12)
+    full_index = np.zeros((12, 12), np.int32)
+    full_index[upper_i, upper_j] = np.arange(upper_i.size)
+    full_index[upper_j, upper_i] = np.arange(upper_i.size)
+    floats = jnp.concatenate([gram[:, upper_i, upper_j].reshape(-1), proj.reshape(-1)])
+    high = lax.reduce_precision(floats, exponent_bits=8, mantissa_bits=7)
+    low = floats - high
+    payload = jnp.concatenate(
+        [node_panel.reshape(-1), high.astype(jnp.bfloat16), low.astype(jnp.bfloat16)]
+    )
+    own = exchange_gather(as_lanes(payload, jnp.bfloat16), ("row", "col"))
     own = own.reshape(tiles, -1)
     n_nodes = node_rows * node_cols * comps * width
-    n_gram = elements * 144
+    n_floats = elements * upper_i.size + elements * 12
     own_nodes = own[:, :n_nodes].reshape(n_row, n_col, node_rows, node_cols, comps, width)
     own_nodes = own_nodes.transpose(0, 2, 1, 3, 4, 5).reshape(n_row * node_rows, n_col * node_cols, comps, width)
-    grams = own[:, n_nodes : n_nodes + n_gram].reshape(n_row, n_col, elem_rows, elem_cols, 12, 12)
-    grams = grams.transpose(0, 2, 1, 3, 4, 5).reshape(-1, 12, 12)
-    projs = own[:, n_nodes + n_gram : n_nodes + n_gram + elements * 12]
-    projs = projs.reshape(n_row, n_col, elem_rows, elem_cols, 12).transpose(0, 2, 1, 3, 4).reshape(-1, 12)
+    floats = own[:, n_nodes : n_nodes + n_floats].astype(jnp.float32)
+    floats = floats + own[:, n_nodes + n_floats : n_nodes + 2 * n_floats].astype(jnp.float32)
+    n_upper = elements * upper_i.size
+    grams = floats[:, :n_upper].reshape(n_row, n_col, elem_rows, elem_cols, upper_i.size)
+    grams = grams.transpose(0, 2, 1, 3, 4).reshape(-1, upper_i.size)[:, full_index]
+    projs = floats[:, n_upper:].reshape(n_row, n_col, elem_rows, elem_cols, 12)
+    projs = projs.transpose(0, 2, 1, 3, 4).reshape(-1, 12)
 
     route = []
     for b in range(n_param):

time: 69 us -> 69.4 us (level)
    gather x0 -> x4, local copies, waits for them, and re-layouts: none -> 2.13 us  [the longest x2 1.31 us: on_device(): gram[:, upper_i, upper_j].reshape(-1)]
    another operation x1, local copies, waits for them, and re-layouts: 1.46 us -> 0.27 us  [on_device(): cross.reshape(n_row, n_col, per_block, node_rows, node_cols, comps, width)]
    transpose x1 -> x0, local copies, waits for them, and re-layouts: 0.85 us -> none  [on_device(): grams.transpose(1, 2, 0)[:, :, :, None]]
    broadcast_in_dim x2 -> x3, local copies, waits for them, and re-layouts: 1.48 us -> 1.42 us  [exchange_gather(): copies = jnp.broadcast_to(piece[None], (size,) + piece.shape)]
  transfers between devices with their start and end apart: 3 -> 3, of which waited for: 2 -> 2; matrix products, arithmetic and copies ran while one was open for 11% -> 10% of each run, Pallas kernels for 0% -> 0%
where the time goes in v9:
time: 69.4 us; the launch traced here: 68.9 us
  starting transfers between devices  37.3 us (54%)
  waiting for transfers between devices  14.3 us (21%)
  local copies, waits for them, and re-layouts  10.6 us (15%)
  other arithmetic  4.58 us (7%)
  matrix products  1.07 us (2%)
  between operations  1 us (1%)
    all_to_all x2, starting transfers between devices, exchange_gather(): return lax.all_to_all(copies, axes, 0, 0, tiled=False)  27.7 us
    all_to_all x2, waiting for transfers between devices, exchange_gather(): return lax.all_to_all(copies, axes, 0, 0, tiled=False)  13 us
    ppermute x1, starting transfers between devices, on_device(): lax.ppermute(as_lanes(node_panel.reshape(-1), jnp.bfloat16), ('param', 'r...  9.62 us
    broadcast_in_dim x3, local copies, waits for them, and re-layouts, exchange_gather(): copies = jnp.broadcast_to(piece[None], (size,) + piece.shape)  1.42 us
  transfers between devices with their start and end apart: 3, of which 2 were waited for; matrix products, arithmetic and copies ran while one was open for 10% of the time, Pallas kernels for 0%

profile of v9, /device:TPU:19, one launch (start us, length us, event | category | flops | bytes accessed | tf_op | source)
XLA Modules:
  0.0 68.9 jit_solution(4090127014808761512)
XLA Ops:
  0.7 0.7 convert_bitcast_fusion
  1.3 0.8 %multiply_convert_fusion.1 = (bf16[2,8,128]{2,1,0:T(8,128)(2,1)S(1)}, f32[2,8,128]{2,1,0:T(8,128)S(1)}) fusion(f32[2,8,128]{2,1,0:T(8,128)} %param.13, f32[2,8,128]{2,1,0:T(8,128)} %param.12, f32[8]{0:T(128)S(1)} %convert_bitcast_fusion), kind=kLoop, calls=%fused_computation.37 | loop fusion | flops 6144 | bytes 28704 | tf_op jit(solution)/shard_map/convert_element_type | solution.py:64
  2.1 0.1 mul.159
  2.3 0.9 %reshape.286 = f32[3,2,8,16,8]{4,3,2,1,0:T(8,128)S(1)} reshape(bf16[3,2,8,128]{3,2,1,0:T(8,128)(2,1)} %param.11) | data formatting | bytes 36864 | tf_op jit(solution)/shard_map/mul | solution.py:60
  3.2 0.1 copy.45
  3.4 0.1 broadcast_multiply_fusion.3
  3.7 0.2 copy.46
  3.9 0.1 reshape.278
  4.0 0.1 copy.50
  4.2 0.2 fusion.18
  4.4 0.1 fusion.19
  4.5 0.1 reshape.280
  4.6 0.2 copy.48
  4.8 1.2 %gather_fusion = f32[78,16]{1,0:T(8,128)S(1)} fusion(f32[16,12,12]{0,2,1:T(8,128)S(1)} %copy.48, s32[78]{0:T(128)S(1)} %copy-done), kind=kCustom, calls=%fused_computation | custom fusion | bytes 10608 | tf_op jit(solution)/shard_map/gather | solution.py:74
  6.1 0.1 reshape.277
  6.2 0.1 reshape.275
  6.4 0.1 concatenate.15
  6.5 0.7 %broadcast_in_dim.15 = bf16[16,48,128]{2,1,0:T(8,128)(2,1)} broadcast(bf16[48,128]{1,0:T(8,128)(2,1)S(1)} %pad_bitcast_fusion), dimensions={1,2} | broadcast | bytes 208896 | tf_op jit(solution)/shard_map/broadcast_in_dim | solution.py:24
  7.2 9.3 %all-to-all-start = ((bf16[16,48,128]{2,1,0:T(8,128)(2,1)}), bf16[16,48,128]{2,1,0:T(8,128)(2,1)S(1)}, u32[]{:S(2)}, u32[]{:S(2)}) async-start(bf16[16,48,128]{2,1,0:T(8,128)(2,1)} %broadcast_in_dim.15), calls=%async_computation | async-start | bytes 393216 | tf_op jit(solution)/shard_map/all_to_all | solution.py:25
  16.5 0.1 reshape.283
  16.6 9.6 %collective-permute-start = (bf16[24,128]{1,0:T(8,128)(2,1)S(1)}, bf16[24,128]{1,0:T(8,128)(2,1)S(1)}, u32[]{:S(2)}, u32[]{:S(2)}) collective-permute-start(bf16[24,128]{1,0:T(8,128)(2,1)S(1)} %reshape.283), channel_id=1, source_target_pairs={{0,0},{1,32},{2,64},{3,96},{4,128},{5,160},{6,192},{7,224},{8,256}... | collective-permute-start | bytes 18440 | tf_op jit(solution)/shard_map/ppermute | solution.py:98
  26.2 1.3 %collective-permute-done = bf16[24,128]{1,0:T(8,128)(2,1)S(1)} collective-permute-done((bf16[24,128]{1,0:T(8,128)(2,1)S(1)}, bf16[24,128]{1,0:T(8,128)(2,1)S(1)}, u32[]{:S(2)}, u32[]{:S(2)}) %collective-permute-start) | collective-permute-done | bytes 6176 | tf_op jit(solution)/shard_map/ppermute | solution.py:98
  27.5 0.7 %broadcast_in_dim.17 = bf16[32,24,128]{2,1,0:T(8,128)(2,1)} broadcast(bf16[24,128]{1,0:T(8,128)(2,1)S(1)} %collective-permute-done), dimensions={1,2} | broadcast | bytes 202752 | tf_op jit(solution)/shard_map/broadcast_in_dim | solution.py:24
  28.2 18.4 %all-to-all-start.1 = ((bf16[32,24,128]{2,1,0:T(8,128)(2,1)}), bf16[32,24,128]{2,1,0:T(8,128)(2,1)S(1)}, u32[]{:S(2)}, u32[]{:S(2)}) async-start(bf16[32,24,128]{2,1,0:T(8,128)(2,1)} %broadcast_in_dim.17), calls=%async_computation.1 | async-start | bytes 393216 | tf_op jit(solution)/shard_map/all_to_all | solution.py:25
  46.7 0.2 reshape_transpose_reshape.10
  46.9 0.2 stack.38
  47.3 0.2 slice_bitcast_fusion.2
  47.5 1.1 %maximum_bitcast_fusion = bf16[4,3,4,64,64]{4,1,3,2,0:T(4,128)(2,1)S(1)} fusion(bf16[1,4,64,3,64]{4,3,2,1,0:T(4,128)(2,1)S(1)} %get-tuple-element.8, bf16[1,4,64,3,64]{4,3,2,1,0:T(4,128)(2,1)S(1)} %get-tuple-element.7, bf16[1,4,64,3,64]{4,3,2,1,0:T(4,128)(2,1)S(1)} %get-tuple-element.6, bf16[1,4,64,3,64]{4,3,2,1,0:T(4,128)(2,1)S(1)} %stack.38), kind=kLoop, calls=%fused_computation.7 | loop fusion | flops 589824 | bytes 786432 | tf_op jit(solution)/shard_map/transpose | solution.py:39
  48.6 0.9 %copy.52 = bf16[4,3,4,64,64]{3,2,4,1,0:T(4,128)(2,1)S(1)} copy(bf16[4,3,4,64,64]{4,1,3,2,0:T(4,128)(2,1)S(1)} %maximum_bitcast_fusion) | data formatting | bytes 786432 | tf_op jit(solution)/shard_map/transpose | solution.py:39
  49.6 0.5 reshape.282
  50.0 0.1 reshape_transpose_reshape.11
  50.3 0.1 slice-done
  50.4 0.1 reshape_transpose_reshape.9
  50.6 0.1 copy.51
  50.7 0.8 %gather_fusion.1 = f32[144,256]{1,0:T(8,128)S(1)} fusion(f32[256,78]{0,1:T(8,128)S(1)} %copy.51, s32[1024]{0:T(1024)S(1)} %pad_clamp_fusion), kind=kCustom, calls=%fused_computation.1 | custom fusion | bytes 295488 | tf_op jit(solution)/shard_map/gather | solution.py:90
  51.5 0.4 convolution_bitcast_fusion.1
  51.9 0.6 dynamic_slice.3
  52.5 0.7 %multiply_reduce_fusion = f32[12,256,64]{1,2,0:T(8,128)S(1)} fusion(f32[12,256,64]{1,2,0:T(8,128)S(1)} %convert_element_type.95, f32[12,12,256]{2,1,0:T(8,128)S(1)} %reshape.298), kind=kLoop, calls=%fused_computation.2 | loop fusion | flops 4521984 | bytes 1720320 | tf_op jit(solution)/shard_map/reduce_sum | solution.py:106
  53.2 0.2 reduce-precision_convert_fusion
  53.4 13.0 %all-to-all-done.1 = bf16[32,24,128]{2,1,0:T(8,128)(2,1)S(1)} async-done(((bf16[32,24,128]{2,1,0:T(8,128)(2,1)}), bf16[32,24,128]{2,1,0:T(8,128)(2,1)S(1)}, u32[]{:S(2)}, u32[]{:S(2)}) %all-to-all-start.1) | async-done | bytes 196640 | tf_op jit(solution)/shard_map/all_to_all | solution.py:25
  66.4 0.3 reshape_reshape.3
  66.7 0.5 copy.54
  67.2 0.2 reshape.284
  67.4 0.2 stack.43
  67.6 0.1 fusion.4
  67.7 0.1 maximum_bitcast_fusion.1
  67.9 0.4 convolution_bitcast_fusion
  68.2 0.6 slice_add_fusion
  (30 shorter events, 0.9 us)
Async XLA Ops:
  3.5 1.2 %copy-start = (s32[78]{0:T(128)S(1)}, s32[78]{0:T(128)}, u32[]{:S(2)}) copy-start(s32[78]{0:T(128)} %constant.104) | copy-start | bytes 940
  3.6 2.6 %copy-start.2 = (bf16[1,16,3,64]{3,1,2,0:T(8,128)(2,1)S(1)}, bf16[1,16,3,64]{3,1,2,0:T(8,128)(2,1)}, u32[]{:S(2)}) copy-start(bf16[1,16,3,64]{3,1,2,0:T(8,128)(2,1)} %param.15) | copy-start | bytes 18436
  3.7 22.5 %copy-start.3 = (s32[144]{0:T(256)S(1)}, s32[144]{0:T(256)}, u32[]{:S(2)}) copy-start(s32[144]{0:T(256)} %constant.105) | copy-start | bytes 1732
  7.2 20.3 %all-to-all-start = ((bf16[16,48,128]{2,1,0:T(8,128)(2,1)}), bf16[16,48,128]{2,1,0:T(8,128)(2,1)S(1)}, u32[]{:S(2)}, u32[]{:S(2)}) async-start(bf16[16,48,128]{2,1,0:T(8,128)(2,1)} %broadcast_in_dim.15), calls=%async_computation | async-start | bytes 393216 | tf_op jit(solution)/shard_map/all_to_all | solution.py:25
  16.6 10.9 %collective-permute-start = (bf16[24,128]{1,0:T(8,128)(2,1)S(1)}, bf16[24,128]{1,0:T(8,128)(2,1)S(1)}, u32[]{:S(2)}, u32[]{:S(2)}) collective-permute-start(bf16[24,128]{1,0:T(8,128)(2,1)S(1)} %reshape.283), channel_id=1, source_target_pairs={{0,0},{1,32},{2,64},{3,96},{4,128},{5,160},{6,192},{7,224},{8,256}... | collective-permute-start | bytes 18440 | tf_op jit(solution)/shard_map/ppermute | solution.py:98
  28.2 38.2 %all-to-all-start.1 = ((bf16[32,24,128]{2,1,0:T(8,128)(2,1)}), bf16[32,24,128]{2,1,0:T(8,128)(2,1)S(1)}, u32[]{:S(2)}, u32[]{:S(2)}) async-start(bf16[32,24,128]{2,1,0:T(8,128)(2,1)} %broadcast_in_dim.17), calls=%async_computation.1 | async-start | bytes 393216 | tf_op jit(solution)/shard_map/all_to_all | solution.py:25
  47.2 1.4 %copy-start.1 = (f32[16,1440]{1,0:T(8,128)}, f32[16,1440]{1,0:T(8,128)S(1)}, u32[]{:S(2)}) copy-start(f32[16,1440]{1,0:T(8,128)S(1)} %convert_add_fusion) | copy-start | bytes 276484
  49.5 0.9 %slice-start = ((f32[16,1440]{1,0:T(8,128)}), f32[16,1248]{1,0:T(8,128)S(1)}, s32[]{:S(2)}) async-start(f32[16,1440]{1,0:T(8,128)} %copy-done.1), calls=%async_computation.2 | async-start | bytes 163840 | tf_op jit(solution)/shard_map/slice | solution.py:89

commit v10 on v6

--- a/solution.py
+++ b/solution.py
@@ -1,5 +1,6 @@
 import jax
 import jax.numpy as jnp
+import numpy as np
 from jax import lax
 from jax.sharding import PartitionSpec as P
 
@@ -22,6 +23,36 @@
     size = lax.axis_size(axes)
     copies = jnp.broadcast_to(piece[None], (size,) + piece.shape)
     return lax.all_to_all(copies, axes, 0, 0, tiled=False)
+
+
+def ring_distance(a, b, n):
+    d = abs(a - b) % n
+    return min(d, n - d)
+
+
+def landing_places(n_param, n_row, n_col, per_block):
+    z_size = n_param // 2
+    tiles = n_row * n_col
+
+    def hops(t, j, T, a):
+        b = per_block * T + j
+        dz = ring_distance(a % z_size, b % z_size, z_size)
+        dx = ring_distance(t // n_col, T // n_col, n_row)
+        y_from = 2 * ((t % n_col) // 2) + b // z_size
+        y_to = 2 * ((T % n_col) // 2) + a // z_size
+        return dz + dx + ring_distance(y_from, y_to, 4)
+
+    table = np.zeros((tiles, tiles * per_block), np.int32)
+    for T in range(tiles):
+        sources = [(t, j) for t in range(tiles) for j in range(per_block)]
+        sources.sort(key=lambda s: -(ring_distance(s[0] // n_col, T // n_col, n_row)
+                                     + 2 * ring_distance((s[0] % n_col) // 2, (T % n_col) // 2, 2)))
+        free = list(range(n_param))
+        for t, j in sources:
+            place = min(free, key=lambda a: (hops(t, j, T, a), a))
+            free.remove(place)
+            table[T, t * per_block + j] = place
+    return table
 
 
 def as_lanes(flat, dtype):
@@ -78,12 +109,16 @@
     projs = own[:, n_nodes + n_gram : n_nodes + n_gram + elements * 12]
     projs = projs.reshape(n_row, n_col, elem_rows, elem_cols, 12).transpose(0, 2, 1, 3, 4).reshape(-1, 12)
 
+    places = landing_places(n_param, n_row, n_col, per_block)
     route = []
     for b in range(n_param):
         for t in range(tiles):
-            route.append((b * tiles + t, (per_block * t + b % per_block) * tiles + b // per_block))
+            T = b // per_block
+            route.append((b * tiles + t, int(places[T, t * per_block + b % per_block]) * tiles + T))
     moved = lax.ppermute(as_lanes(node_panel.reshape(-1), jnp.bfloat16), ("param", "row", "col"), route)
-    cross = exchange_gather(moved, "param").reshape(n_param, -1)[:, : node_rows * node_cols * comps * width]
+    cross = exchange_gather(moved, "param")
+    cross = jnp.take(cross, jnp.asarray(places)[lax.axis_index(("row", "col"))], axis=0)
+    cross = cross.reshape(n_param, -1)[:, : node_rows * node_cols * comps * width]
     cross = cross.reshape(n_row, n_col, per_block, node_rows, node_cols, comps, width)
     cross = cross.transpose(0, 3, 1, 4, 5, 2, 6)
     cross = cross.reshape(n_row * node_rows, n_col * node_cols, comps, per_block * width)

time: 69 us -> 67 us (0.971)
  the two profiles are of different devices: /device:TPU:19 before, /device:TPU:8 now
where the time goes in v10:
time: 67 us; the launch traced here: 66.5 us
  starting transfers between devices  36.1 us (54%)
  local copies, waits for them, and re-layouts  12 us (18%)
  waiting for transfers between devices  10.9 us (16%)
  other arithmetic  5.45 us (8%)
  matrix products  1.07 us (2%)
  between operations  0.99 us (1%)
    all_to_all x2, starting transfers between devices, exchange_gather(): return lax.all_to_all(copies, axes, 0, 0, tiled=False)  21.4 us
    ppermute x1, starting transfers between devices, on_device(): lax.ppermute(as_lanes(node_panel.reshape(-1), jnp.bfloat16), ('param', 'r...  14.7 us
    all_to_all x2, waiting for transfers between devices, exchange_gather(): return lax.all_to_all(copies, axes, 0, 0, tiled=False)  10.9 us
    gather x2, local copies, waits for them, and re-layouts, on_device(): jnp.take(cross, jnp.asarray(places)[lax.axis_index(('row', 'col'))], axis=0)  1.79 us
    broadcast_in_dim x2, local copies, waits for them, and re-layouts, exchange_gather(): copies = jnp.broadcast_to(piece[None], (size,) + piece.shape)  1.47 us
  transfers between devices with their start and end apart: 3, of which 1 were waited for; matrix products, arithmetic and copies ran while one was open for 13% of the time, Pallas kernels for 0%

profile of v10, /device:TPU:8, one launch (start us, length us, event | category | flops | bytes accessed | tf_op | source)
XLA Modules:
  0.0 66.5 jit_solution(4571931666774012430)
XLA Ops:
  0.7 0.7 convert_bitcast_fusion
  1.3 0.8 %multiply_convert_fusion.1 = (bf16[2,8,128]{2,1,0:T(8,128)(2,1)S(1)}, f32[2,8,128]{2,1,0:T(8,128)S(1)}) fusion(f32[2,8,128]{2,1,0:T(8,128)} %param.8, f32[2,8,128]{2,1,0:T(8,128)} %param.7, f32[8]{0:T(128)S(1)} %convert_bitcast_fusion), kind=kLoop, calls=%fused_computation.37 | loop fusion | flops 6144 | bytes 28704 | tf_op jit(solution)/shard_map/convert_element_type | solution.py:94
  2.1 0.1 mul.160
  2.3 0.9 %reshape.343 = f32[3,2,8,16,8]{4,3,2,1,0:T(8,128)S(1)} reshape(bf16[3,2,8,128]{3,2,1,0:T(8,128)(2,1)} %param.6) | data formatting | bytes 36864 | tf_op jit(solution)/shard_map/mul | solution.py:90
  3.2 0.1 copy.36
  3.4 0.1 broadcast_multiply_fusion.3
  3.6 0.1 multiply_convert_fusion
  3.6 0.2 copy.37
  3.9 0.1 reshape.334
  4.0 0.1 copy.39
  4.1 0.2 fusion.19
  4.3 0.1 fusion.20
  4.5 0.1 reshape.336
  4.6 0.1 reshape.333
  4.8 0.8 %broadcast_in_dim.14 = f32[16,48,128]{2,1,0:T(8,128)} broadcast(f32[48,128]{1,0:T(8,128)S(1)} %fusion.7), dimensions={1,2} | broadcast | bytes 417792 | tf_op jit(solution)/shard_map/broadcast_in_dim | solution.py:24
  5.6 6.1 %all-to-all-start = ((f32[16,48,128]{2,1,0:T(8,128)}), f32[16,48,128]{2,1,0:T(8,128)S(1)}, u32[]{:S(2)}, u32[]{:S(2)}) async-start(f32[16,48,128]{2,1,0:T(8,128)} %broadcast_in_dim.14), calls=%async_computation | async-start | bytes 786432 | tf_op jit(solution)/shard_map/all_to_all | solution.py:25
  11.7 0.1 reshape.339
  11.8 14.7 %collective-permute-start = (bf16[24,128]{1,0:T(8,128)(2,1)S(1)}, bf16[24,128]{1,0:T(8,128)(2,1)S(1)}, u32[]{:S(2)}, u32[]{:S(2)}) collective-permute-start(bf16[24,128]{1,0:T(8,128)(2,1)S(1)} %reshape.339), channel_id=1, source_target_pairs={{0,416},{1,400},{2,464},{3,208},{4,448},{5,160},{6,496},{7,240},{8... | collective-permute-start | bytes 18440 | tf_op jit(solution)/shard_map/ppermute | solution.py:118
  26.5 0.7 %fusion.17 = s32[32]{0:T(128)S(1)} fusion(s32[16,32]{1,0:T(8,128)} %constant.74.clone, s32[]{:T(128)S(6)} %select_n.77), kind=kLoop, calls=%fused_computation.55 | loop fusion | flops 96 | bytes 260 | tf_op jit(solution)/shard_map/jit(_take)/jit(_where)/select_n | solution.py:120
  27.2 0.7 %dynamic-slice_reduce_fusion = s32[32]{0:T(128)S(1)} fusion(s32[16,32]{1,0:T(8,128)} %constant.74.clone, s32[]{:T(128)S(6)} %select_n.77), kind=kLoop, calls=%fused_computation.57 | loop fusion | bytes 260 | tf_op jit(solution)/shard_map/dynamic_slice | solution.py:120
  27.9 0.1 squeeze.5
  28.1 0.7 %broadcast_in_dim.19 = bf16[32,24,128]{2,1,0:T(8,128)(2,1)} broadcast(bf16[24,128]{1,0:T(8,128)(2,1)S(1)} %collective-permute-done), dimensions={1,2} | broadcast | bytes 202752 | tf_op jit(solution)/shard_map/broadcast_in_dim | solution.py:24
  28.8 15.2 %all-to-all-start.1 = ((bf16[32,24,128]{2,1,0:T(8,128)(2,1)}), bf16[32,24,128]{2,1,0:T(8,128)(2,1)}, u32[]{:S(2)}, u32[]{:S(2)}) async-start(bf16[32,24,128]{2,1,0:T(8,128)(2,1)} %broadcast_in_dim.19), calls=%async_computation.1 | async-start | bytes 393216 | tf_op jit(solution)/shard_map/all_to_all | solution.py:25
  44.0 0.1 copy.51
  44.2 0.2 convert_element_type.105
  44.4 0.2 convert_element_type.104
  44.7 0.2 slice_bitcast_fusion.2
  44.9 1.1 %maximum_bitcast_fusion = bf16[4,3,4,64,64]{4,1,3,2,0:T(4,128)(2,1)S(1)} fusion(bf16[1,4,64,3,64]{4,3,2,1,0:T(4,128)(2,1)S(1)} %get-tuple-element.8, bf16[1,4,64,3,64]{4,3,2,1,0:T(4,128)(2,1)S(1)} %get-tuple-element.7, bf16[1,4,64,3,64]{4,3,2,1,0:T(4,128)(2,1)S(1)} %get-tuple-element.6, bf16[1,4,64,3,64]{4,3,2,1,0:T(4,128)(2,1)S(1)} %convert_element_type.104), kind=kLoop, calls=%fused_computation.6 | loop fusion | flops 589824 | bytes 786432 | tf_op jit(solution)/shard_map/transpose | solution.py:69
  46.0 0.9 %copy.41 = bf16[4,3,4,64,64]{3,2,4,1,0:T(4,128)(2,1)S(1)} copy(bf16[4,3,4,64,64]{4,1,3,2,0:T(4,128)(2,1)S(1)} %maximum_bitcast_fusion) | data formatting | bytes 786432 | tf_op jit(solution)/shard_map/transpose | solution.py:69
  46.9 0.5 reshape.338
  47.4 0.1 reshape_transpose_reshape.8
  47.7 0.9 %reshape_transpose_reshape.7 = f32[256,12,12]{2,1,0:T(8,128)S(1)} reshape(f32[16,2304]{1,0:T(8,128)S(1)} %slice.48) | data formatting | bytes 294912 | tf_op jit(solution)/shard_map/reshape;transpose;reshape | solution.py:108
  48.6 0.8 %copy.40 = f32[12,12,256]{2,1,0:T(8,128)S(1)} copy(f32[12,12,256]{1,0,2:T(8,128)S(1)} %bitcast.63) | data formatting | bytes 294912 | tf_op jit(solution)/shard_map/transpose | solution.py:128
  49.4 0.4 convolution_bitcast_fusion.1
  49.8 0.6 dynamic_slice.7
  50.5 0.7 %multiply_reduce_fusion = f32[12,256,64]{1,2,0:T(8,128)S(1)} fusion(f32[12,256,64]{1,2,0:T(8,128)S(1)} %convert_element_type.106, f32[12,12,256]{2,1,0:T(8,128)S(1)} %copy.40), kind=kLoop, calls=%fused_computation.1 | loop fusion | flops 4521984 | bytes 1720320 | tf_op jit(solution)/shard_map/reduce_sum | solution.py:128
  51.2 0.2 reduce-precision_convert_fusion
  51.3 10.9 %all-to-all-done.1 = bf16[32,24,128]{2,1,0:T(8,128)(2,1)} async-done(((bf16[32,24,128]{2,1,0:T(8,128)(2,1)}), bf16[32,24,128]{2,1,0:T(8,128)(2,1)}, u32[]{:S(2)}, u32[]{:S(2)}) %all-to-all-start.1) | async-done | bytes 196640 | tf_op jit(solution)/shard_map/all_to_all | solution.py:25
  62.2 1.5 %gather_fusion = bf16[32,24,128]{2,1,0:T(8,128)(2,1)S(1)} fusion(bf16[32,24,128]{2,1,0:T(8,128)(2,1)} %all-to-all-done.1, s32[1024]{0:T(1024)S(1)} %pad_clamp_fusion), kind=kCustom, calls=%fused_computation | custom fusion | bytes 393344 | tf_op jit(solution)/shard_map/jit(_take)/gather | solution.py:120
  63.7 0.3 gather.7
  64.0 0.3 select_bitcast_fusion
  64.3 0.5 copy.43
  64.8 0.2 reshape.340
  65.0 0.2 stack.40
  65.2 0.1 fusion.4
  65.3 0.1 maximum_bitcast_fusion.1
  65.5 0.4 convolution_bitcast_fusion
  65.9 0.6 slice_add_fusion
  (22 shorter events, 0.6 us)
Async XLA Ops:
  2.1 2.6 %copy-start = (bf16[1,16,3,64]{3,1,2,0:T(8,128)(2,1)S(1)}, bf16[1,16,3,64]{3,1,2,0:T(8,128)(2,1)}, u32[]{:S(2)}) copy-start(bf16[1,16,3,64]{3,1,2,0:T(8,128)(2,1)} %param.10) | copy-start | bytes 18436
  5.6 22.5 %all-to-all-start = ((f32[16,48,128]{2,1,0:T(8,128)}), f32[16,48,128]{2,1,0:T(8,128)S(1)}, u32[]{:S(2)}, u32[]{:S(2)}) async-start(f32[16,48,128]{2,1,0:T(8,128)} %broadcast_in_dim.14), calls=%async_computation | async-start | bytes 786432 | tf_op jit(solution)/shard_map/all_to_all | solution.py:25
  11.8 16.3 %collective-permute-start = (bf16[24,128]{1,0:T(8,128)(2,1)S(1)}, bf16[24,128]{1,0:T(8,128)(2,1)S(1)}, u32[]{:S(2)}, u32[]{:S(2)}) collective-permute-start(bf16[24,128]{1,0:T(8,128)(2,1)S(1)} %reshape.339), channel_id=1, source_target_pairs={{0,416},{1,400},{2,464},{3,208},{4,448},{5,160},{6,496},{7,240},{8... | collective-permute-start | bytes 18440 | tf_op jit(solution)/shard_map/ppermute | solution.py:118
  28.8 33.4 %all-to-all-start.1 = ((bf16[32,24,128]{2,1,0:T(8,128)(2,1)}), bf16[32,24,128]{2,1,0:T(8,128)(2,1)}, u32[]{:S(2)}, u32[]{:S(2)}) async-start(bf16[32,24,128]{2,1,0:T(8,128)(2,1)} %broadcast_in_dim.19), calls=%async_computation.1 | async-start | bytes 393216 | tf_op jit(solution)/shard_map/all_to_all | solution.py:25

commit v11 on v10

--- a/solution.py
+++ b/solution.py
@@ -97,8 +97,16 @@
     gram = jnp.einsum("eip,ejp->eij", design, design, preferred_element_type=jnp.float32)
     proj = jnp.einsum("eip,ep->ei", design, weighted, preferred_element_type=jnp.float32)
 
+    places = landing_places(n_param, n_row, n_col, per_block)
+    route = []
+    for b in range(n_param):
+        for t in range(tiles):
+            T = b // per_block
+            route.append((b * tiles + t, int(places[T, t * per_block + b % per_block]) * tiles + T))
+    moved = lax.ppermute(as_lanes(node_panel.reshape(-1), jnp.bfloat16), ("param", "row", "col"), route)
     payload = jnp.concatenate([node_panel.reshape(-1).astype(jnp.float32), gram.reshape(-1), proj.reshape(-1)])
-    own = exchange_gather(as_lanes(payload, jnp.float32), ("row", "col"))
+    lanes, moved = lax.optimization_barrier((as_lanes(payload, jnp.float32), moved))
+    own = exchange_gather(lanes, ("row", "col"))
     own = own.reshape(tiles, -1)
     n_nodes = node_rows * node_cols * comps * width
     n_gram = elements * 144
@@ -109,13 +117,6 @@
     projs = own[:, n_nodes + n_gram : n_nodes + n_gram + elements * 12]
     projs = projs.reshape(n_row, n_col, elem_rows, elem_cols, 12).transpose(0, 2, 1, 3, 4).reshape(-1, 12)
 
-    places = landing_places(n_param, n_row, n_col, per_block)
-    route = []
-    for b in range(n_param):
-        for t in range(tiles):
-            T = b // per_block
-            route.append((b * tiles + t, int(places[T, t * per_block + b % per_block]) * tiles + T))
-    moved = lax.ppermute(as_lanes(node_panel.reshape(-1), jnp.bfloat16), ("param", "row", "col"), route)
     cross = exchange_gather(moved, "param")
     cross = jnp.take(cross, jnp.asarray(places)[lax.axis_index(("row", "col"))], axis=0)
     cross = cross.reshape(n_param, -1)[:, : node_rows * node_cols * comps * width]

time: 67 us -> 71.5 us (1.067)
  the two profiles are of different devices: /device:TPU:8 before, /device:TPU:1 now
where the time goes in v11:
time: 71.5 us; the launch traced here: 70.4 us
  starting transfers between devices  30.6 us (43%)
  waiting for transfers between devices  18.9 us (26%)
  local copies, waits for them, and re-layouts  13.5 us (19%)
  other arithmetic  5.42 us (8%)
  matrix products  1.05 us (1%)
  between operations  0.96 us (1%)
    all_to_all x2, waiting for transfers between devices, exchange_gather(): return lax.all_to_all(copies, axes, 0, 0, tiled=False)  18.9 us
    ppermute x1, starting transfers between devices, on_device(): lax.ppermute(as_lanes(node_panel.reshape(-1), jnp.bfloat16), ('param', 'r...  17.4 us
    all_to_all x2, starting transfers between devices, exchange_gather(): return lax.all_to_all(copies, axes, 0, 0, tiled=False)  13.2 us
    gather x2, local copies, waits for them, and re-layouts, on_device(): jnp.take(cross, jnp.asarray(places)[lax.axis_index(('row', 'col'))], axis=0)  1.79 us
    broadcast_in_dim x2, local copies, waits for them, and re-layouts, exchange_gather(): copies = jnp.broadcast_to(piece[None], (size,) + piece.shape)  1.5 us
  transfers between devices with their start and end apart: 3, of which 2 were waited for; matrix products, arithmetic and copies ran while one was open for 19% of the time, Pallas kernels for 0%

profile of v11, /device:TPU:1, one launch (start us, length us, event | category | flops | bytes accessed | tf_op | source)
XLA Modules:
  0.0 70.4 jit_solution(7610971193960639813)
XLA Ops:
  0.6 0.7 %copy.40 = bf16[1,16,3,64]{3,2,1,0:T(4,128)(2,1)S(1)} copy(bf16[1,16,3,64]{3,1,2,0:T(8,128)(2,1)} %param.10) | data formatting | bytes 12288 | tf_op args[4]
  1.4 17.4 %collective-permute-start = (bf16[24,128]{1,0:T(8,128)(2,1)S(1)}, bf16[24,128]{1,0:T(8,128)(2,1)S(1)}, u32[]{:S(2)}, u32[]{:S(2)}) collective-permute-start(bf16[24,128]{1,0:T(8,128)(2,1)S(1)} %reshape.341), channel_id=1, source_target_pairs={{0,416},{1,400},{2,464},{3,208},{4,448},{5,160},{6,496},{7,240},{8... | collective-permute-start | bytes 18440 | tf_op jit(solution)/shard_map/ppermute | solution.py:106
  18.9 0.7 %copy.34 = f32[1,16,3,64]{3,2,1,0:T(4,128)S(1)} copy(bf16[1,16,3,64]{3,1,2,0:T(8,128)(2,1)} %param.10) | data formatting | bytes 18432 | tf_op jit(solution)/shard_map/convert_element_type | solution.py:107
  19.6 0.7 convert_bitcast_fusion
  20.3 0.8 %multiply_convert_fusion.1 = (bf16[2,8,128]{2,1,0:T(8,128)(2,1)S(1)}, f32[2,8,128]{2,1,0:T(8,128)S(1)}) fusion(f32[2,8,128]{2,1,0:T(8,128)} %param.8, f32[2,8,128]{2,1,0:T(8,128)} %param.7, f32[8]{0:T(128)S(1)} %convert_bitcast_fusion), kind=kLoop, calls=%fused_computation.37 | loop fusion | flops 6144 | bytes 28704 | tf_op jit(solution)/shard_map/convert_element_type | solution.py:94
  21.1 0.1 reshape.337
  21.2 0.1 copy.39
  21.4 0.1 mul.160
  21.6 0.9 %reshape.347 = f32[3,2,8,16,8]{4,3,2,1,0:T(8,128)S(1)} reshape(bf16[3,2,8,128]{3,2,1,0:T(8,128)(2,1)} %param.6) | data formatting | bytes 36864 | tf_op jit(solution)/shard_map/mul | solution.py:90
  22.5 0.1 copy.36
  22.7 0.1 broadcast_multiply_fusion.3
  22.9 0.2 copy.37
  23.2 0.2 fusion.19
  23.3 0.1 fusion.20
  23.5 0.1 reshape.339
  23.6 0.1 reshape.336
  23.7 0.8 %broadcast_in_dim.11 = f32[16,48,128]{2,1,0:T(8,128)} broadcast(f32[48,128]{1,0:T(8,128)S(1)} %fusion.7), dimensions={1,2} | broadcast | bytes 417792 | tf_op jit(solution)/shard_map/broadcast_in_dim | solution.py:24
  24.5 3.5 %all-to-all-start = ((f32[16,48,128]{2,1,0:T(8,128)}), f32[16,48,128]{2,1,0:T(8,128)S(1)}, u32[]{:S(2)}, u32[]{:S(2)}) async-start(f32[16,48,128]{2,1,0:T(8,128)} %broadcast_in_dim.11), calls=%async_computation | async-start | bytes 786432 | tf_op jit(solution)/shard_map/all_to_all | solution.py:25
  28.0 0.7 fusion.17
  28.6 0.7 %dynamic-slice_reduce_fusion = s32[32]{0:T(128)S(1)} fusion(s32[16,32]{1,0:T(8,128)} %constant.74.clone, s32[]{:T(128)S(6)} %select_n.77), kind=kLoop, calls=%fused_computation.57 | loop fusion | bytes 260 | tf_op jit(solution)/shard_map/dynamic_slice | solution.py:121
  29.5 8.6 %all-to-all-done = f32[16,48,128]{2,1,0:T(8,128)S(1)} async-done(((f32[16,48,128]{2,1,0:T(8,128)}), f32[16,48,128]{2,1,0:T(8,128)S(1)}, u32[]{:S(2)}, u32[]{:S(2)}) %all-to-all-start) | async-done | bytes 393248 | tf_op jit(solution)/shard_map/all_to_all | solution.py:25
  38.1 0.7 %broadcast_in_dim.13 = bf16[32,24,128]{2,1,0:T(8,128)(2,1)} broadcast(bf16[24,128]{1,0:T(8,128)(2,1)S(1)} %collective-permute-done), dimensions={1,2} | broadcast | bytes 202752 | tf_op jit(solution)/shard_map/broadcast_in_dim | solution.py:24
  38.8 9.7 %all-to-all-start.1 = ((bf16[32,24,128]{2,1,0:T(8,128)(2,1)}), bf16[32,24,128]{2,1,0:T(8,128)(2,1)}, u32[]{:S(2)}, u32[]{:S(2)}) async-start(bf16[32,24,128]{2,1,0:T(8,128)(2,1)} %broadcast_in_dim.13), calls=%async_computation.1 | async-start | bytes 393216 | tf_op jit(solution)/shard_map/all_to_all | solution.py:25
  48.5 0.1 copy.51
  48.7 0.2 convert_element_type.105
  48.9 0.2 convert_element_type.104
  49.1 0.1 reshape_transpose_reshape.8
  49.3 0.3 slice_bitcast_fusion.2
  49.6 1.1 %maximum_bitcast_fusion = bf16[4,3,4,64,64]{4,1,3,2,0:T(4,128)(2,1)S(1)} fusion(bf16[1,4,64,3,64]{4,3,2,1,0:T(4,128)(2,1)S(1)} %get-tuple-element.12, bf16[1,4,64,3,64]{4,3,2,1,0:T(4,128)(2,1)S(1)} %get-tuple-element.11, bf16[1,4,64,3,64]{4,3,2,1,0:T(4,128)(2,1)S(1)} %get-tuple-element.10, bf16[1,4,64,3,64]{4,3,2,1,0:T(4,128)(2,1)S(1)} %convert_element_type.104), kind=kLoop, calls=%fused_computation.6 | loop fusion | flops 589824 | bytes 786432 | tf_op jit(solution)/shard_map/transpose | solution.py:69
  50.6 0.9 %copy.42 = bf16[4,3,4,64,64]{3,2,4,1,0:T(4,128)(2,1)S(1)} copy(bf16[4,3,4,64,64]{4,1,3,2,0:T(4,128)(2,1)S(1)} %maximum_bitcast_fusion) | data formatting | bytes 786432 | tf_op jit(solution)/shard_map/transpose | solution.py:69
  51.6 0.5 reshape.343
  52.1 0.9 %reshape_transpose_reshape.7 = f32[256,12,12]{2,1,0:T(8,128)S(1)} reshape(f32[16,2304]{1,0:T(8,128)S(1)} %slice.48) | data formatting | bytes 294912 | tf_op jit(solution)/shard_map/reshape;transpose;reshape | solution.py:116
  53.1 0.8 %copy.41 = f32[12,12,256]{2,1,0:T(8,128)S(1)} copy(f32[12,12,256]{1,0,2:T(8,128)S(1)} %bitcast.63) | data formatting | bytes 294912 | tf_op jit(solution)/shard_map/transpose | solution.py:129
  53.9 0.4 convolution_bitcast_fusion.1
  54.3 0.6 dynamic_slice.7
  54.9 0.7 %multiply_reduce_fusion = f32[12,256,64]{1,2,0:T(8,128)S(1)} fusion(f32[12,256,64]{1,2,0:T(8,128)S(1)} %convert_element_type.106, f32[12,12,256]{2,1,0:T(8,128)S(1)} %copy.41), kind=kLoop, calls=%fused_computation.1 | loop fusion | flops 4521984 | bytes 1720320 | tf_op jit(solution)/shard_map/reduce_sum | solution.py:129
  55.6 0.2 reduce-precision_convert_fusion
  55.8 10.3 %all-to-all-done.1 = bf16[32,24,128]{2,1,0:T(8,128)(2,1)} async-done(((bf16[32,24,128]{2,1,0:T(8,128)(2,1)}), bf16[32,24,128]{2,1,0:T(8,128)(2,1)}, u32[]{:S(2)}, u32[]{:S(2)}) %all-to-all-start.1) | async-done | bytes 196640 | tf_op jit(solution)/shard_map/all_to_all | solution.py:25
  66.1 1.5 %gather_fusion = bf16[32,24,128]{2,1,0:T(8,128)(2,1)S(1)} fusion(bf16[32,24,128]{2,1,0:T(8,128)(2,1)} %all-to-all-done.1, s32[1024]{0:T(1024)S(1)} %pad_clamp_fusion), kind=kCustom, calls=%fused_computation | custom fusion | bytes 393344 | tf_op jit(solution)/shard_map/jit(_take)/gather | solution.py:121
  67.6 0.3 gather.7
  67.9 0.3 select_bitcast_fusion
  68.2 0.5 copy.43
  68.7 0.2 reshape.344
  68.9 0.2 stack.40
  69.1 0.1 fusion.4
  69.2 0.1 maximum_bitcast_fusion.1
  69.4 0.4 convolution_bitcast_fusion
  69.8 0.6 slice_add_fusion
  (20 shorter events, 0.8 us)
Async XLA Ops:
  1.4 22.3 %collective-permute-start = (bf16[24,128]{1,0:T(8,128)(2,1)S(1)}, bf16[24,128]{1,0:T(8,128)(2,1)S(1)}, u32[]{:S(2)}, u32[]{:S(2)}) collective-permute-start(bf16[24,128]{1,0:T(8,128)(2,1)S(1)} %reshape.341), channel_id=1, source_target_pairs={{0,416},{1,400},{2,464},{3,208},{4,448},{5,160},{6,496},{7,240},{8... | collective-permute-start | bytes 18440 | tf_op jit(solution)/shard_map/ppermute | solution.py:106
  24.5 13.6 %all-to-all-start = ((f32[16,48,128]{2,1,0:T(8,128)}), f32[16,48,128]{2,1,0:T(8,128)S(1)}, u32[]{:S(2)}, u32[]{:S(2)}) async-start(f32[16,48,128]{2,1,0:T(8,128)} %broadcast_in_dim.11), calls=%async_computation | async-start | bytes 786432 | tf_op jit(solution)/shard_map/all_to_all | solution.py:25
  38.8 27.3 %all-to-all-start.1 = ((bf16[32,24,128]{2,1,0:T(8,128)(2,1)}), bf16[32,24,128]{2,1,0:T(8,128)(2,1)}, u32[]{:S(2)}, u32[]{:S(2)}) async-start(bf16[32,24,128]{2,1,0:T(8,128)(2,1)} %broadcast_in_dim.13), calls=%async_computation.1 | async-start | bytes 393216 | tf_op jit(solution)/shard_map/all_to_all | solution.py:25

commit v12 on v10

--- a/solution.py
+++ b/solution.py
@@ -117,8 +117,10 @@
             route.append((b * tiles + t, int(places[T, t * per_block + b % per_block]) * tiles + T))
     moved = lax.ppermute(as_lanes(node_panel.reshape(-1), jnp.bfloat16), ("param", "row", "col"), route)
     cross = exchange_gather(moved, "param")
-    cross = jnp.take(cross, jnp.asarray(places)[lax.axis_index(("row", "col"))], axis=0)
-    cross = cross.reshape(n_param, -1)[:, : node_rows * node_cols * comps * width]
+    picks = jnp.asarray(places)[lax.axis_index(("row", "col"))]
+    select = (picks[:, None] == jnp.arange(n_param)[None, :]).astype(jnp.bfloat16)
+    cross = jnp.einsum("ka,ar->kr", select, cross.reshape(n_param, -1), preferred_element_type=jnp.float32)
+    cross = cross.astype(jnp.bfloat16)[:, : node_rows * node_cols * comps * width]
     cross = cross.reshape(n_row, n_col, per_block, node_rows, node_cols, comps, width)
     cross = cross.transpose(0, 3, 1, 4, 5, 2, 6)
     cross = cross.reshape(n_row * node_rows, n_col * node_cols, comps, per_block * width)

time: 67 us -> 66.5 us (level)
  local copies, waits for them, and re-layouts: 12 us -> 10.6 us
  matrix products: 1.07 us -> 2.24 us
  other arithmetic: 5.45 us -> 4.42 us
    gather x2 -> x0, local copies, waits for them, and re-layouts: 1.79 us -> none  [on_device(): jnp.take(cross, jnp.asarray(places)[lax.axis_index(('row', 'col'))], axis=0)]
    dot_general x0 -> x1, matrix products: none -> 1.17 us  [on_device(): jnp.einsum('ka,ar->kr', select, cross.reshape(n_param, -1), preferred_ele...]
    dynamic_slice x1 -> x0, local copies, waits for them, and re-layouts: 0.71 us -> none  [on_device(): jnp.asarray(places)[lax.axis_index(('row', 'col'))]]
    select_n x1 -> x0, other arithmetic: 0.7 us -> none  [on_device(): jnp.take(cross, jnp.asarray(places)[lax.axis_index(('row', 'col'))], axis=0)]
    eq x0 -> x1, local copies, waits for them, and re-layouts: none -> 0.7 us  [on_device(): picks[:, None] == jnp.arange(n_param)[None, :]]
  transfers between devices with their start and end apart: 3 -> 3, of which waited for: 1 -> 2; matrix products, arithmetic and copies ran while one was open for 13% -> 12% of each run, Pallas kernels for 0% -> 0%
where the time goes in v12:
time: 66.5 us; the launch traced here: 66 us
  starting transfers between devices  36.3 us (55%)
  waiting for transfers between devices  11.5 us (17%)
  local copies, waits for them, and re-layouts  10.6 us (16%)
  other arithmetic  4.42 us (7%)
  matrix products  2.24 us (3%)
  between operations  0.96 us (1%)
    all_to_all x2, starting transfers between devices, exchange_gather(): return lax.all_to_all(copies, axes, 0, 0, tiled=False)  21.6 us
    ppermute x1, starting transfers between devices, on_device(): lax.ppermute(as_lanes(node_panel.reshape(-1), jnp.bfloat16), ('param', 'r...  14.7 us
    all_to_all x2, waiting for transfers between devices, exchange_gather(): return lax.all_to_all(copies, axes, 0, 0, tiled=False)  10.9 us
    broadcast_in_dim x2, local copies, waits for them, and re-layouts, exchange_gather(): copies = jnp.broadcast_to(piece[None], (size,) + piece.shape)  1.48 us
  transfers between devices with their start and end apart: 3, of which 2 were waited for; matrix products, arithmetic and copies ran while one was open for 12% of the time, Pallas kernels for 0%

profile of v12, /device:TPU:8, one launch (start us, length us, event | category | flops | bytes accessed | tf_op | source)
XLA Modules:
  0.0 66.0 jit_solution(6444440647982053807)
XLA Ops:
  0.7 0.7 %convert_bitcast_fusion = f32[8]{0:T(128)S(1)} fusion(s32[8,1]{0,1:T(1,128)} %param.9), kind=kLoop, calls=%fused_computation.55 | loop fusion | flops 8 | bytes 64 | tf_op jit(solution)/shard_map/convert_element_type | solution.py:87
  1.3 0.8 %multiply_convert_fusion.1 = (bf16[2,8,128]{2,1,0:T(8,128)(2,1)S(1)}, f32[2,8,128]{2,1,0:T(8,128)S(1)}) fusion(f32[2,8,128]{2,1,0:T(8,128)} %param.8, f32[2,8,128]{2,1,0:T(8,128)} %param.7, f32[8]{0:T(128)S(1)} %convert_bitcast_fusion), kind=kLoop, calls=%fused_computation.39 | loop fusion | flops 6144 | bytes 28704 | tf_op jit(solution)/shard_map/convert_element_type | solution.py:94
  2.1 0.1 mul.160
  2.2 0.1 copy.25
  2.3 0.9 %reshape.306 = f32[3,2,8,16,8]{4,3,2,1,0:T(8,128)S(1)} reshape(bf16[3,2,8,128]{3,2,1,0:T(8,128)(2,1)} %param.6) | data formatting | bytes 36864 | tf_op jit(solution)/shard_map/mul | solution.py:90
  3.2 0.1 copy.26
  3.4 0.1 broadcast_multiply_fusion.3
  3.6 0.1 multiply_convert_fusion
  3.6 0.2 copy.27
  3.9 0.1 reshape.295
  4.0 0.1 copy.29
  4.1 0.2 fusion.21
  4.3 0.1 fusion.22
  4.5 0.1 reshape.297
  4.6 0.1 reshape.294
  4.7 0.1 reshape.305
  4.8 0.8 %broadcast_in_dim.7 = f32[16,48,128]{2,1,0:T(8,128)} broadcast(f32[48,128]{1,0:T(8,128)S(1)} %fusion.9), dimensions={1,2} | broadcast | bytes 417792 | tf_op jit(solution)/shard_map/broadcast_in_dim | solution.py:24
  5.6 6.1 %all-to-all-start = ((f32[16,48,128]{2,1,0:T(8,128)}), f32[16,48,128]{2,1,0:T(8,128)S(1)}, u32[]{:S(2)}, u32[]{:S(2)}) async-start(f32[16,48,128]{2,1,0:T(8,128)} %broadcast_in_dim.7), calls=%async_computation | async-start | bytes 786432 | tf_op jit(solution)/shard_map/all_to_all | solution.py:25
  11.7 0.1 reshape.300
  11.8 14.7 %collective-permute-start = (bf16[24,128]{1,0:T(8,128)(2,1)S(1)}, bf16[24,128]{1,0:T(8,128)(2,1)S(1)}, u32[]{:S(2)}, u32[]{:S(2)}) collective-permute-start(bf16[24,128]{1,0:T(8,128)(2,1)S(1)} %reshape.300), channel_id=1, source_target_pairs={{0,416},{1,400},{2,464},{3,208},{4,448},{5,160},{6,496},{7,240},{8... | collective-permute-start | bytes 18440 | tf_op jit(solution)/shard_map/ppermute | solution.py:118
  26.5 0.7 %dynamic-slice_bitcast_fusion = s32[32]{0:T(128)S(1)} fusion(s32[16,32]{1,0:T(8,128)} %constant.59.clone, s32[]{:T(128)S(6)} %select_n.49), kind=kLoop, calls=%fused_computation.54 | loop fusion | bytes 260 | tf_op jit(solution)/shard_map/eq | solution.py:121
  27.2 0.6 collective-permute-done
  27.9 0.7 %broadcast_in_dim.8 = bf16[32,24,128]{2,1,0:T(8,128)(2,1)} broadcast(bf16[24,128]{1,0:T(8,128)(2,1)S(1)} %collective-permute-done), dimensions={1,2} | broadcast | bytes 202752 | tf_op jit(solution)/shard_map/broadcast_in_dim | solution.py:24
  28.6 15.5 %all-to-all-start.1 = ((bf16[32,24,128]{2,1,0:T(8,128)(2,1)}), bf16[32,24,128]{2,1,0:T(8,128)(2,1)}, u32[]{:S(2)}, u32[]{:S(2)}) async-start(bf16[32,24,128]{2,1,0:T(8,128)(2,1)} %broadcast_in_dim.8), calls=%async_computation.1 | async-start | bytes 393216 | tf_op jit(solution)/shard_map/all_to_all | solution.py:25
  44.0 0.1 copy.46
  44.2 0.2 convert_element_type.109
  44.4 0.2 convert_element_type.108
  44.7 0.2 slice_bitcast_fusion.2
  44.9 1.1 %maximum_bitcast_fusion = bf16[4,3,4,64,64]{4,1,3,2,0:T(4,128)(2,1)S(1)} fusion(bf16[1,4,64,3,64]{4,3,2,1,0:T(4,128)(2,1)S(1)} %get-tuple-element.8, bf16[1,4,64,3,64]{4,3,2,1,0:T(4,128)(2,1)S(1)} %get-tuple-element.7, bf16[1,4,64,3,64]{4,3,2,1,0:T(4,128)(2,1)S(1)} %get-tuple-element.6, bf16[1,4,64,3,64]{4,3,2,1,0:T(4,128)(2,1)S(1)} %convert_element_type.108), kind=kLoop, calls=%fused_computation.6 | loop fusion | flops 589824 | bytes 786432 | tf_op jit(solution)/shard_map/transpose | solution.py:69
  46.0 0.9 %copy.31 = bf16[4,3,4,64,64]{3,2,4,1,0:T(4,128)(2,1)S(1)} copy(bf16[4,3,4,64,64]{4,1,3,2,0:T(4,128)(2,1)S(1)} %maximum_bitcast_fusion) | data formatting | bytes 786432 | tf_op jit(solution)/shard_map/transpose | solution.py:69
  46.9 0.5 reshape.299
  47.4 0.1 reshape_transpose_reshape.8
  47.7 0.9 %reshape_transpose_reshape.7 = f32[256,12,12]{2,1,0:T(8,128)S(1)} reshape(f32[16,2304]{1,0:T(8,128)S(1)} %slice.46) | data formatting | bytes 294912 | tf_op jit(solution)/shard_map/reshape;transpose;reshape | solution.py:108
  48.6 0.8 %copy.30 = f32[12,12,256]{2,1,0:T(8,128)S(1)} copy(f32[12,12,256]{1,0,2:T(8,128)S(1)} %bitcast.64) | data formatting | bytes 294912 | tf_op jit(solution)/shard_map/transpose | solution.py:130
  49.4 0.4 convolution_bitcast_fusion.1
  49.8 0.6 dynamic_slice.7
  50.5 0.7 %multiply_reduce_fusion = f32[12,256,64]{1,2,0:T(8,128)S(1)} fusion(f32[12,256,64]{1,2,0:T(8,128)S(1)} %convert_element_type.110, f32[12,12,256]{2,1,0:T(8,128)S(1)} %copy.30), kind=kLoop, calls=%fused_computation | loop fusion | flops 4521984 | bytes 1720320 | tf_op jit(solution)/shard_map/reduce_sum | solution.py:130
  51.2 0.2 reduce-precision_convert_fusion
  51.3 10.9 %all-to-all-done.1 = bf16[32,24,128]{2,1,0:T(8,128)(2,1)} async-done(((bf16[32,24,128]{2,1,0:T(8,128)(2,1)}), bf16[32,24,128]{2,1,0:T(8,128)(2,1)}, u32[]{:S(2)}, u32[]{:S(2)}) %all-to-all-start.1) | async-done | bytes 196640 | tf_op jit(solution)/shard_map/all_to_all | solution.py:25
  62.2 1.2 %convolution_convert_fusion = bf16[32,3072]{1,0:T(8,128)(2,1)S(1)} fusion(bf16[4,8,24,128]{3,2,1,0:T(8,128)(2,1)} %bitcast.32, s32[32]{0:T(128)S(1)} %dynamic-slice_bitcast_fusion), kind=kOutput, calls=%fused_computation.1 | convolution fusion | flops 6390784 | bytes 393344 | tf_op jit(solution)/shard_map/ka,ar->kr/dot_general | solution.py:122
  63.4 0.4 reshape.302
  63.8 0.5 copy.33
  64.3 0.2 reshape.303
  64.5 0.2 stack.40
  64.7 0.1 fusion.4
  64.8 0.1 maximum_bitcast_fusion.1
  65.0 0.4 convolution_bitcast_fusion
  65.4 0.6 slice_add_fusion
  (17 shorter events, 0.4 us)
Async XLA Ops:
  2.1 2.6 %copy-start = (bf16[1,16,3,64]{3,1,2,0:T(8,128)(2,1)S(1)}, bf16[1,16,3,64]{3,1,2,0:T(8,128)(2,1)}, u32[]{:S(2)}) copy-start(bf16[1,16,3,64]{3,1,2,0:T(8,128)(2,1)} %param.10) | copy-start | bytes 18436
  5.6 22.3 %all-to-all-start = ((f32[16,48,128]{2,1,0:T(8,128)}), f32[16,48,128]{2,1,0:T(8,128)S(1)}, u32[]{:S(2)}, u32[]{:S(2)}) async-start(f32[16,48,128]{2,1,0:T(8,128)} %broadcast_in_dim.7), calls=%async_computation | async-start | bytes 786432 | tf_op jit(solution)/shard_map/all_to_all | solution.py:25
  11.8 16.0 %collective-permute-start = (bf16[24,128]{1,0:T(8,128)(2,1)S(1)}, bf16[24,128]{1,0:T(8,128)(2,1)S(1)}, u32[]{:S(2)}, u32[]{:S(2)}) collective-permute-start(bf16[24,128]{1,0:T(8,128)(2,1)S(1)} %reshape.300), channel_id=1, source_target_pairs={{0,416},{1,400},{2,464},{3,208},{4,448},{5,160},{6,496},{7,240},{8... | collective-permute-start | bytes 18440 | tf_op jit(solution)/shard_map/ppermute | solution.py:118
  28.6 33.7 %all-to-all-start.1 = ((bf16[32,24,128]{2,1,0:T(8,128)(2,1)}), bf16[32,24,128]{2,1,0:T(8,128)(2,1)}, u32[]{:S(2)}, u32[]{:S(2)}) async-start(bf16[32,24,128]{2,1,0:T(8,128)(2,1)} %broadcast_in_dim.8), calls=%async_computation.1 | async-start | bytes 393216 | tf_op jit(solution)/shard_map/all_to_all | solution.py:25

commit v13 on v12

--- a/solution.py
+++ b/solution.py
@@ -133,7 +133,9 @@
     stacked = jnp.concatenate([high.astype(jnp.bfloat16), low.astype(jnp.bfloat16)], axis=2)
     product = jnp.einsum("jep,jeq->pq", stacked, cols_of, preferred_element_type=jnp.float32)
     hessian = product[:width] + product[width:]
-    gradient = jnp.einsum("iep,ie->p", rows_of.astype(jnp.float32), projs.T, precision=HIGHEST)
+    proj_high = lax.reduce_precision(projs.T, exponent_bits=8, mantissa_bits=7)
+    proj_pair = jnp.stack([proj_high, projs.T - proj_high], axis=2).astype(jnp.bfloat16)
+    gradient = jnp.einsum("iep,iek->pk", rows_of, proj_pair, preferred_element_type=jnp.float32).sum(axis=1)
     share = width // tiles
     gradient = lax.dynamic_slice(gradient, (lax.axis_index(("row", "col")) * share,), (share,))
     return (hessian, gradient)

time: 66.5 us -> 66.5 us (level)
  no operation moved by 1% of the time
where the time goes in v13:
time: 66.5 us; the launch traced here: 66 us
  starting transfers between devices  36.3 us (55%)
  waiting for transfers between devices  11.7 us (18%)
  local copies, waits for them, and re-layouts  10.6 us (16%)
  other arithmetic  4.41 us (7%)
  matrix products  2.05 us (3%)
  between operations  0.97 us (1%)
    all_to_all x2, starting transfers between devices, exchange_gather(): return lax.all_to_all(copies, axes, 0, 0, tiled=False)  21.6 us
    ppermute x1, starting transfers between devices, on_device(): lax.ppermute(as_lanes(node_panel.reshape(-1), jnp.bfloat16), ('param', 'r...  14.7 us
    all_to_all x2, waiting for transfers between devices, exchange_gather(): return lax.all_to_all(copies, axes, 0, 0, tiled=False)  11 us
    broadcast_in_dim x2, local copies, waits for them, and re-layouts, exchange_gather(): copies = jnp.broadcast_to(piece[None], (size,) + piece.shape)  1.46 us
  transfers between devices with their start and end apart: 3, of which 2 were waited for; matrix products, arithmetic and copies ran while one was open for 12% of the time, Pallas kernels for 0%

profile of v13, /device:TPU:8, one launch (start us, length us, event | category | flops | bytes accessed | tf_op | source)
XLA Modules:
  0.0 66.0 jit_solution(4569501230224879434)
XLA Ops:
  0.7 0.7 %convert_bitcast_fusion = f32[8]{0:T(128)S(1)} fusion(s32[8,1]{0,1:T(1,128)} %param.9), kind=kLoop, calls=%fused_computation.64 | loop fusion | flops 8 | bytes 64 | tf_op jit(solution)/shard_map/convert_element_type | solution.py:87
  1.3 0.8 %multiply_convert_fusion.1 = (bf16[2,8,128]{2,1,0:T(8,128)(2,1)S(1)}, f32[2,8,128]{2,1,0:T(8,128)S(1)}) fusion(f32[2,8,128]{2,1,0:T(8,128)} %param.8, f32[2,8,128]{2,1,0:T(8,128)} %param.7, f32[8]{0:T(128)S(1)} %convert_bitcast_fusion), kind=kLoop, calls=%fused_computation.48 | loop fusion | flops 6144 | bytes 28704 | tf_op jit(solution)/shard_map/convert_element_type | solution.py:94
  2.1 0.1 mul.160
  2.2 0.1 copy.62
  2.3 0.9 %reshape.306 = f32[3,2,8,16,8]{4,3,2,1,0:T(8,128)S(1)} reshape(bf16[3,2,8,128]{3,2,1,0:T(8,128)(2,1)} %param.6) | data formatting | bytes 36864 | tf_op jit(solution)/shard_map/mul | solution.py:90
  3.2 0.1 copy.63
  3.4 0.1 broadcast_multiply_fusion.3
  3.6 0.1 multiply_convert_fusion
  3.6 0.2 copy.64
  3.9 0.1 reshape.295
  4.0 0.1 copy.66
  4.1 0.2 fusion.29
  4.3 0.1 fusion.30
  4.5 0.1 reshape.297
  4.6 0.1 reshape.294
  4.7 0.1 reshape.305
  4.8 0.8 %broadcast_in_dim.7 = f32[16,48,128]{2,1,0:T(8,128)} broadcast(f32[48,128]{1,0:T(8,128)S(1)} %fusion.10), dimensions={1,2} | broadcast | bytes 417792 | tf_op jit(solution)/shard_map/broadcast_in_dim | solution.py:24
  5.6 6.1 %all-to-all-start = ((f32[16,48,128]{2,1,0:T(8,128)}), f32[16,48,128]{2,1,0:T(8,128)S(1)}, u32[]{:S(2)}, u32[]{:S(2)}) async-start(f32[16,48,128]{2,1,0:T(8,128)} %broadcast_in_dim.7), calls=%async_computation | async-start | bytes 786432 | tf_op jit(solution)/shard_map/all_to_all | solution.py:25
  11.7 0.1 reshape.300
  11.8 14.7 %collective-permute-start = (bf16[24,128]{1,0:T(8,128)(2,1)S(1)}, bf16[24,128]{1,0:T(8,128)(2,1)S(1)}, u32[]{:S(2)}, u32[]{:S(2)}) collective-permute-start(bf16[24,128]{1,0:T(8,128)(2,1)S(1)} %reshape.300), channel_id=1, source_target_pairs={{0,416},{1,400},{2,464},{3,208},{4,448},{5,160},{6,496},{7,240},{8... | collective-permute-start | bytes 18440 | tf_op jit(solution)/shard_map/ppermute | solution.py:118
  26.5 0.7 %dynamic-slice_bitcast_fusion = s32[32]{0:T(128)S(1)} fusion(s32[16,32]{1,0:T(8,128)} %constant.59.clone, s32[]{:T(128)S(6)} %select_n.49), kind=kLoop, calls=%fused_computation.63 | loop fusion | bytes 260 | tf_op jit(solution)/shard_map/eq | solution.py:121
  27.2 0.6 collective-permute-done
  27.9 0.7 %broadcast_in_dim.8 = bf16[32,24,128]{2,1,0:T(8,128)(2,1)} broadcast(bf16[24,128]{1,0:T(8,128)(2,1)S(1)} %collective-permute-done), dimensions={1,2} | broadcast | bytes 202752 | tf_op jit(solution)/shard_map/broadcast_in_dim | solution.py:24
  28.5 15.5 %all-to-all-start.1 = ((bf16[32,24,128]{2,1,0:T(8,128)(2,1)}), bf16[32,24,128]{2,1,0:T(8,128)(2,1)}, u32[]{:S(2)}, u32[]{:S(2)}) async-start(bf16[32,24,128]{2,1,0:T(8,128)(2,1)} %broadcast_in_dim.8), calls=%async_computation.1 | async-start | bytes 393216 | tf_op jit(solution)/shard_map/all_to_all | solution.py:25
  44.0 0.1 copy.85
  44.2 0.2 convert_element_type.109
  44.4 0.2 convert_element_type.108
  44.6 0.2 slice_bitcast_fusion.2
  44.9 1.1 %maximum_bitcast_fusion = bf16[4,3,4,64,64]{4,1,3,2,0:T(4,128)(2,1)S(1)} fusion(bf16[1,4,64,3,64]{4,3,2,1,0:T(4,128)(2,1)S(1)} %get-tuple-element.8, bf16[1,4,64,3,64]{4,3,2,1,0:T(4,128)(2,1)S(1)} %get-tuple-element.7, bf16[1,4,64,3,64]{4,3,2,1,0:T(4,128)(2,1)S(1)} %get-tuple-element.6, bf16[1,4,64,3,64]{4,3,2,1,0:T(4,128)(2,1)S(1)} %convert_element_type.108), kind=kLoop, calls=%fused_computation.7 | loop fusion | flops 589824 | bytes 786432 | tf_op jit(solution)/shard_map/transpose | solution.py:69
  46.0 0.9 %copy.68 = bf16[4,3,4,64,64]{3,2,4,1,0:T(4,128)(2,1)S(1)} copy(bf16[4,3,4,64,64]{4,1,3,2,0:T(4,128)(2,1)S(1)} %maximum_bitcast_fusion) | data formatting | bytes 786432 | tf_op jit(solution)/shard_map/transpose | solution.py:69
  46.9 0.5 reshape.299
  47.4 0.1 reshape_transpose_reshape.8
  47.7 0.9 %reshape_transpose_reshape.7 = f32[256,12,12]{2,1,0:T(8,128)S(1)} reshape(f32[16,2304]{1,0:T(8,128)S(1)} %slice.46) | data formatting | bytes 294912 | tf_op jit(solution)/shard_map/reshape;transpose;reshape | solution.py:108
  48.6 0.8 %copy.67 = f32[12,12,256]{2,1,0:T(8,128)S(1)} copy(f32[12,12,256]{1,0,2:T(8,128)S(1)} %bitcast.73) | data formatting | bytes 294912 | tf_op jit(solution)/shard_map/transpose | solution.py:130
  49.5 0.2 fusion
  49.7 0.6 dynamic_slice.7
  50.3 0.7 %multiply_reduce_fusion = f32[12,256,64]{1,2,0:T(8,128)S(1)} fusion(f32[12,256,64]{1,2,0:T(8,128)S(1)} %convert_element_type.110, f32[12,12,256]{2,1,0:T(8,128)S(1)} %copy.67), kind=kLoop, calls=%fused_computation | loop fusion | flops 4521984 | bytes 1720320 | tf_op jit(solution)/shard_map/reduce_sum | solution.py:130
  51.0 0.2 reduce-precision_convert_fusion
  51.2 11.0 %all-to-all-done.1 = bf16[32,24,128]{2,1,0:T(8,128)(2,1)} async-done(((bf16[32,24,128]{2,1,0:T(8,128)(2,1)}), bf16[32,24,128]{2,1,0:T(8,128)(2,1)}, u32[]{:S(2)}, u32[]{:S(2)}) %all-to-all-start.1) | async-done | bytes 196640 | tf_op jit(solution)/shard_map/all_to_all | solution.py:25
  62.2 1.2 %convolution_convert_fusion = bf16[32,3072]{1,0:T(8,128)(2,1)S(1)} fusion(bf16[4,8,24,128]{3,2,1,0:T(8,128)(2,1)} %bitcast.32, s32[32]{0:T(128)S(1)} %dynamic-slice_bitcast_fusion), kind=kOutput, calls=%fused_computation.1 | convolution fusion | flops 6390784 | bytes 393344 | tf_op jit(solution)/shard_map/ka,ar->kr/dot_general | solution.py:122
  63.4 0.4 reshape.302
  63.8 0.5 copy.70
  64.3 0.2 reshape.303
  64.5 0.2 stack.52
  64.7 0.1 fusion.5
  64.8 0.1 maximum_bitcast_fusion.1
  65.0 0.4 convolution_bitcast_fusion
  65.4 0.6 slice_add_fusion
  (20 shorter events, 0.4 us)
Async XLA Ops:
  2.1 2.6 %copy-start = (bf16[1,16,3,64]{3,1,2,0:T(8,128)(2,1)S(1)}, bf16[1,16,3,64]{3,1,2,0:T(8,128)(2,1)}, u32[]{:S(2)}) copy-start(bf16[1,16,3,64]{3,1,2,0:T(8,128)(2,1)} %param.10) | copy-start | bytes 18436
  5.6 22.3 %all-to-all-start = ((f32[16,48,128]{2,1,0:T(8,128)}), f32[16,48,128]{2,1,0:T(8,128)S(1)}, u32[]{:S(2)}, u32[]{:S(2)}) async-start(f32[16,48,128]{2,1,0:T(8,128)} %broadcast_in_dim.7), calls=%async_computation | async-start | bytes 786432 | tf_op jit(solution)/shard_map/all_to_all | solution.py:25
  11.8 16.0 %collective-permute-start = (bf16[24,128]{1,0:T(8,128)(2,1)S(1)}, bf16[24,128]{1,0:T(8,128)(2,1)S(1)}, u32[]{:S(2)}, u32[]{:S(2)}) collective-permute-start(bf16[24,128]{1,0:T(8,128)(2,1)S(1)} %reshape.300), channel_id=1, source_target_pairs={{0,416},{1,400},{2,464},{3,208},{4,448},{5,160},{6,496},{7,240},{8... | collective-permute-start | bytes 18440 | tf_op jit(solution)/shard_map/ppermute | solution.py:118
  28.5 33.7 %all-to-all-start.1 = ((bf16[32,24,128]{2,1,0:T(8,128)(2,1)}), bf16[32,24,128]{2,1,0:T(8,128)(2,1)}, u32[]{:S(2)}, u32[]{:S(2)}) async-start(bf16[32,24,128]{2,1,0:T(8,128)(2,1)} %broadcast_in_dim.8), calls=%async_computation.1 | async-start | bytes 393216 | tf_op jit(solution)/shard_map/all_to_all | solution.py:25

commit v14 on v12

--- a/solution.py
+++ b/solution.py
@@ -130,9 +130,9 @@
     weighted_rows = jnp.sum(grams.transpose(1, 2, 0)[:, :, :, None] * rows_of.astype(jnp.float32)[:, None], axis=0)
     high = lax.reduce_precision(weighted_rows, exponent_bits=8, mantissa_bits=7)
     low = weighted_rows - high
-    stacked = jnp.concatenate([high.astype(jnp.bfloat16), low.astype(jnp.bfloat16)], axis=2)
-    product = jnp.einsum("jep,jeq->pq", stacked, cols_of, preferred_element_type=jnp.float32)
-    hessian = product[:width] + product[width:]
+    stacked = jnp.concatenate([high.astype(jnp.bfloat16), low.astype(jnp.bfloat16)], axis=0)
+    paired = jnp.concatenate([cols_of, cols_of], axis=0)
+    hessian = jnp.einsum("jep,jeq->pq", stacked, paired, preferred_element_type=jnp.float32)
     gradient = jnp.einsum("iep,ie->p", rows_of.astype(jnp.float32), projs.T, precision=HIGHEST)
     share = width // tiles
     gradient = lax.dynamic_slice(gradient, (lax.axis_index(("row", "col")) * share,), (share,))

time: 66.5 us -> 66.6 us (level)
  matrix products: 2.24 us -> 2.96 us
    dot_general x1, matrix products: 0.36 us -> 1.07 us  [on_device(): jnp.einsum('jep,jeq->pq', stacked, paired, preferred_element_type=jnp.flo...]
where the time goes in v14:
time: 66.6 us; the launch traced here: 66.1 us
  starting transfers between devices  36.3 us (55%)
  waiting for transfers between devices  11.5 us (17%)
  local copies, waits for them, and re-layouts  10.5 us (16%)
  other arithmetic  3.8 us (6%)
  matrix products  2.96 us (4%)
  between operations  0.95 us (1%)
    all_to_all x2, starting transfers between devices, exchange_gather(): return lax.all_to_all(copies, axes, 0, 0, tiled=False)  21.6 us
    ppermute x1, starting transfers between devices, on_device(): lax.ppermute(as_lanes(node_panel.reshape(-1), jnp.bfloat16), ('param', 'r...  14.7 us
    all_to_all x2, waiting for transfers between devices, exchange_gather(): return lax.all_to_all(copies, axes, 0, 0, tiled=False)  10.9 us
    broadcast_in_dim x2, local copies, waits for them, and re-layouts, exchange_gather(): copies = jnp.broadcast_to(piece[None], (size,) + piece.shape)  1.48 us
  transfers between devices with their start and end apart: 3, of which 2 were waited for; matrix products, arithmetic and copies ran while one was open for 12% of the time, Pallas kernels for 0%

profile of v14, /device:TPU:8, one launch (start us, length us, event | category | flops | bytes accessed | tf_op | source)
XLA Modules:
  0.0 66.1 jit_solution(3127184328025175457)
XLA Ops:
  0.7 0.7 convert_bitcast_fusion
  1.3 0.8 %multiply_convert_fusion.1 = (bf16[2,8,128]{2,1,0:T(8,128)(2,1)S(1)}, f32[2,8,128]{2,1,0:T(8,128)S(1)}) fusion(f32[2,8,128]{2,1,0:T(8,128)} %param.8, f32[2,8,128]{2,1,0:T(8,128)} %param.7, f32[8]{0:T(128)S(1)} %convert_bitcast_fusion), kind=kLoop, calls=%fused_computation.42 | loop fusion | flops 6144 | bytes 28704 | tf_op jit(solution)/shard_map/convert_element_type | solution.py:94
  2.1 0.1 mul.160
  2.2 0.1 copy.25
  2.3 0.9 %reshape.306 = f32[3,2,8,16,8]{4,3,2,1,0:T(8,128)S(1)} reshape(bf16[3,2,8,128]{3,2,1,0:T(8,128)(2,1)} %param.6) | data formatting | bytes 36864 | tf_op jit(solution)/shard_map/mul | solution.py:90
  3.2 0.1 copy.26
  3.4 0.1 broadcast_multiply_fusion.3
  3.6 0.1 multiply_convert_fusion
  3.6 0.2 copy.27
  3.9 0.1 reshape.295
  4.0 0.1 copy.29
  4.1 0.2 fusion.28
  4.3 0.1 fusion.29
  4.5 0.1 reshape.297
  4.6 0.1 reshape.294
  4.7 0.1 reshape.305
  4.8 0.8 %broadcast_in_dim.7 = f32[16,48,128]{2,1,0:T(8,128)} broadcast(f32[48,128]{1,0:T(8,128)S(1)} %fusion.16), dimensions={1,2} | broadcast | bytes 417792 | tf_op jit(solution)/shard_map/broadcast_in_dim | solution.py:24
  5.6 6.1 %all-to-all-start = ((f32[16,48,128]{2,1,0:T(8,128)}), f32[16,48,128]{2,1,0:T(8,128)S(1)}, u32[]{:S(2)}, u32[]{:S(2)}) async-start(f32[16,48,128]{2,1,0:T(8,128)} %broadcast_in_dim.7), calls=%async_computation | async-start | bytes 786432 | tf_op jit(solution)/shard_map/all_to_all | solution.py:25
  11.7 0.1 reshape.300
  11.8 14.7 %collective-permute-start = (bf16[24,128]{1,0:T(8,128)(2,1)S(1)}, bf16[24,128]{1,0:T(8,128)(2,1)S(1)}, u32[]{:S(2)}, u32[]{:S(2)}) collective-permute-start(bf16[24,128]{1,0:T(8,128)(2,1)S(1)} %reshape.300), channel_id=1, source_target_pairs={{0,416},{1,400},{2,464},{3,208},{4,448},{5,160},{6,496},{7,240},{8... | collective-permute-start | bytes 18440 | tf_op jit(solution)/shard_map/ppermute | solution.py:118
  26.5 0.7 %dynamic-slice_bitcast_fusion = s32[32]{0:T(128)S(1)} fusion(s32[16,32]{1,0:T(8,128)} %constant.59.clone, s32[]{:T(128)S(6)} %select_n.49), kind=kLoop, calls=%fused_computation.57 | loop fusion | bytes 260 | tf_op jit(solution)/shard_map/eq | solution.py:121
  27.2 0.6 collective-permute-done
  27.9 0.7 %broadcast_in_dim.8 = bf16[32,24,128]{2,1,0:T(8,128)(2,1)} broadcast(bf16[24,128]{1,0:T(8,128)(2,1)S(1)} %collective-permute-done), dimensions={1,2} | broadcast | bytes 202752 | tf_op jit(solution)/shard_map/broadcast_in_dim | solution.py:24
  28.6 15.5 %all-to-all-start.1 = ((bf16[32,24,128]{2,1,0:T(8,128)(2,1)}), bf16[32,24,128]{2,1,0:T(8,128)(2,1)}, u32[]{:S(2)}, u32[]{:S(2)}) async-start(bf16[32,24,128]{2,1,0:T(8,128)(2,1)} %broadcast_in_dim.8), calls=%async_computation.1 | async-start | bytes 393216 | tf_op jit(solution)/shard_map/all_to_all | solution.py:25
  44.0 0.1 copy.46
  44.2 0.2 convert_element_type.109
  44.4 0.2 convert_element_type.108
  44.7 0.2 slice_bitcast_fusion.2
  44.9 1.1 %maximum_bitcast_fusion = bf16[4,3,4,64,64]{4,1,3,2,0:T(4,128)(2,1)S(1)} fusion(bf16[1,4,64,3,64]{4,3,2,1,0:T(4,128)(2,1)S(1)} %get-tuple-element.8, bf16[1,4,64,3,64]{4,3,2,1,0:T(4,128)(2,1)S(1)} %get-tuple-element.7, bf16[1,4,64,3,64]{4,3,2,1,0:T(4,128)(2,1)S(1)} %get-tuple-element.6, bf16[1,4,64,3,64]{4,3,2,1,0:T(4,128)(2,1)S(1)} %convert_element_type.108), kind=kLoop, calls=%fused_computation.10 | loop fusion | flops 589824 | bytes 786432 | tf_op jit(solution)/shard_map/transpose | solution.py:69
  46.0 0.9 %copy.31 = bf16[4,3,4,64,64]{3,2,4,1,0:T(4,128)(2,1)S(1)} copy(bf16[4,3,4,64,64]{4,1,3,2,0:T(4,128)(2,1)S(1)} %maximum_bitcast_fusion) | data formatting | bytes 786432 | tf_op jit(solution)/shard_map/transpose | solution.py:69
  46.9 0.5 reshape.299
  47.4 0.1 reshape_transpose_reshape.8
  47.6 0.1 convert_element_type.110
  47.7 0.9 %reshape_transpose_reshape.7 = f32[256,12,12]{2,1,0:T(8,128)S(1)} reshape(f32[16,2304]{1,0:T(8,128)S(1)} %slice.38) | data formatting | bytes 294912 | tf_op jit(solution)/shard_map/reshape;transpose;reshape | solution.py:108
  48.6 0.8 %copy.30 = f32[12,12,256]{2,1,0:T(8,128)S(1)} copy(f32[12,12,256]{1,0,2:T(8,128)S(1)} %bitcast.63) | data formatting | bytes 294912 | tf_op jit(solution)/shard_map/transpose | solution.py:130
  49.4 0.4 convolution_bitcast_fusion
  49.8 0.6 dynamic_slice.7
  50.5 0.7 %multiply_reduce_fusion = f32[12,256,64]{1,2,0:T(8,128)S(1)} fusion(f32[12,256,64]{1,2,0:T(8,128)S(1)} %convert_element_type.110, f32[12,12,256]{2,1,0:T(8,128)S(1)} %copy.30), kind=kLoop, calls=%fused_computation | loop fusion | flops 4521984 | bytes 1720320 | tf_op jit(solution)/shard_map/reduce_sum | solution.py:130
  51.2 0.2 reduce-precision_convert_fusion
  51.3 10.9 %all-to-all-done.1 = bf16[32,24,128]{2,1,0:T(8,128)(2,1)} async-done(((bf16[32,24,128]{2,1,0:T(8,128)(2,1)}), bf16[32,24,128]{2,1,0:T(8,128)(2,1)}, u32[]{:S(2)}, u32[]{:S(2)}) %all-to-all-start.1) | async-done | bytes 196640 | tf_op jit(solution)/shard_map/all_to_all | solution.py:25
  62.2 1.2 %convolution_convert_fusion = bf16[32,3072]{1,0:T(8,128)(2,1)S(1)} fusion(bf16[4,8,24,128]{3,2,1,0:T(8,128)(2,1)} %bitcast.32, s32[32]{0:T(128)S(1)} %dynamic-slice_bitcast_fusion), kind=kOutput, calls=%fused_computation.1 | convolution fusion | flops 6390784 | bytes 393344 | tf_op jit(solution)/shard_map/ka,ar->kr/dot_general | solution.py:122
  63.4 0.4 reshape.302
  63.8 0.5 copy.33
  64.3 0.2 reshape.303
  64.5 0.2 stack.40
  64.7 0.1 fusion.11
  64.8 0.1 maximum_bitcast_fusion.1
  65.0 1.1 %fusion.4 = f32[64,128]{1,0:T(8,128)} fusion(bf16[12,256,128]{2,1,0:T(8,128)(2,1)S(1)} %bitcast.70, bf16[12,256,64]{1,2,0:T(8,128)(2,1)S(1)} %get-tuple-element.5, bf16[12,256,64]{1,2,0:T(8,128)(2,1)S(1)} %get-tuple-element.4), kind=kOutput, calls=%fused_computation.8 | convolution fusion | flops 101842944 | bytes 1605632 | tf_op jit(solution)/shard_map/jep,jeq->pq/dot_general | solution.py:135
  (16 shorter events, 0.3 us)
Async XLA Ops:
  2.1 2.6 %copy-start = (bf16[1,16,3,64]{3,1,2,0:T(8,128)(2,1)S(1)}, bf16[1,16,3,64]{3,1,2,0:T(8,128)(2,1)}, u32[]{:S(2)}) copy-start(bf16[1,16,3,64]{3,1,2,0:T(8,128)(2,1)} %param.10) | copy-start | bytes 18436
  5.6 22.3 %all-to-all-start = ((f32[16,48,128]{2,1,0:T(8,128)}), f32[16,48,128]{2,1,0:T(8,128)S(1)}, u32[]{:S(2)}, u32[]{:S(2)}) async-start(f32[16,48,128]{2,1,0:T(8,128)} %broadcast_in_dim.7), calls=%async_computation | async-start | bytes 786432 | tf_op jit(solution)/shard_map/all_to_all | solution.py:25
  11.8 16.0 %collective-permute-start = (bf16[24,128]{1,0:T(8,128)(2,1)S(1)}, bf16[24,128]{1,0:T(8,128)(2,1)S(1)}, u32[]{:S(2)}, u32[]{:S(2)}) collective-permute-start(bf16[24,128]{1,0:T(8,128)(2,1)S(1)} %reshape.300), channel_id=1, source_target_pairs={{0,416},{1,400},{2,464},{3,208},{4,448},{5,160},{6,496},{7,240},{8... | collective-permute-start | bytes 18440 | tf_op jit(solution)/shard_map/ppermute | solution.py:118
  28.6 33.7 %all-to-all-start.1 = ((bf16[32,24,128]{2,1,0:T(8,128)(2,1)}), bf16[32,24,128]{2,1,0:T(8,128)(2,1)}, u32[]{:S(2)}, u32[]{:S(2)}) async-start(bf16[32,24,128]{2,1,0:T(8,128)(2,1)} %broadcast_in_dim.8), calls=%async_computation.1 | async-start | bytes 393216 | tf_op jit(solution)/shard_map/all_to_all | solution.py:25
